TPU v7x, 256 devices: a whole 4x4x8 slice. The times are simulated.
256 devices in a mesh: req: 8 (over z), cfg: 2 (over core), seq: 16 (over x, y).
Axes of the slice: x: 4, y: 4, z: 8, core: 2. Of those that a mesh axis runs over, the one named last changes fastest.
Arguments:
- projected: bfloat16 [2, 8, 3584, 6144], P('cfg', 'req', 'seq'), parts along dimension 1, may hold values from -8 to 8
- lengths: int32 [8, 16], P('req'), parts along dimension 0, may hold values from 1 to 224, 3226 in all within a row
- text_len: int32 [8], P('req'), parts along dimension 0, may hold values from 113 to 226
- out_weight: bfloat16 [2048, 3072], P('seq', 'cfg'), may hold values from -0.5 to 0.5
- modulation: float32 [8, 2, 3072], P('req'), parts along dimension 0, may hold values from -3 to 3
- proj_weight: bfloat16 [3072, 64], replicated, may hold values from -0.109375 to 0.109375
- latent: float32 [8, 3584, 64], P('req', 'seq', 'cfg'), parts along dimension 0, may hold values from -6 to 6
- timestep: int32 [8], P('req'), parts along dimension 0, may hold values from 20 to 999
Outputs:
- guided: float32 [8, 3584, 64], P('req', 'seq', 'cfg'), parts along dimension 0
- previous: float32 [8, 3584, 64], P('req', 'seq', 'cfg'), parts along dimension 0
There are 8 independent parts, one for each index of `req`. A program takes and returns all parts, laid end to end along the dimension named above; an argument that names none is the same for every part. Nothing has to cross between parts.
Inputs may be any that keep to these rules, and one draw needn't show every extreme that they name: `lengths`: each row sums to 3226, and its largest entry is 224.
All inputs are finite; a program needn't handle non-finite values.
Results may differ from a plain program's by a relative error of at most 0.006.
Values may be sent and summed in bfloat16 or wider, within the bound.
No kernel may reach another device: no remote copies, remote signals or barrier semaphores. Data moves between devices by JAX's collectives and lax.ppermute only.
A program may use at most 64 MiB of HBM per device.

v0:
```python
import math

import jax
import jax.numpy as jnp
from jax import lax
from jax.sharding import PartitionSpec as P

D = 3072
HEAD = 64
OUT_CH = 64
TEXT = 226


guide_scale = 6.0
ln_epsilon = 1e-05
step_gap = 20


def partner_2(array, axis, bit):
    return lax.ppermute(array, axis, [(i, i ^ 1 << bit) for i in range(lax.axis_size(axis))])


def slot_masks(lengths, text_len, slot_ids, capacity):
    piece_ids = slot_ids // capacity
    local_ids = slot_ids % capacity
    seq_ids = jnp.arange(lengths.shape[1], dtype=jnp.int32)
    select = (piece_ids[None, :] == seq_ids[:, None]).astype(jnp.int32)
    offsets = jnp.cumsum(lengths, axis=1) - lengths
    piece_len = jnp.sum(lengths[:, :, None] * select[None], axis=1)
    start_pos = jnp.sum(offsets[:, :, None] * select[None], axis=1)
    position = start_pos + local_ids[None, :]
    live_slots = local_ids[None, :] < piece_len
    key_slots = live_slots & ((position >= TEXT) | (position < text_len[:, None]))
    video_slots = live_slots & (position >= TEXT)
    return (key_slots, video_slots)


def plan(timestep):
    indices = jnp.arange(1000, dtype=jnp.int32)
    counter = jnp.arange(1000, dtype=jnp.float32)
    root_beta = math.sqrt(0.00085) + (math.sqrt(0.012) - math.sqrt(0.00085)) * counter / 999.0
    log_keep = jnp.log1p(-root_beta * root_beta)
    current = timestep[0]
    earlier = jnp.maximum(current - step_gap, 0)
    alpha_now = jnp.exp(jnp.sum(jnp.where(indices <= current, log_keep, 0.0)))
    alpha_prev = jnp.exp(jnp.sum(jnp.where(indices <= earlier, log_keep, 0.0)))
    return (alpha_now, alpha_prev)


def attention(grouped, key_slots, capacity):
    item_count, slot_count, heads_here = (grouped.shape[0], grouped.shape[1], grouped.shape[3])
    stacked = grouped.transpose(0, 3, 2, 1, 4).reshape(item_count * heads_here, 3, slot_count, HEAD)
    head_masks = jnp.repeat(key_slots, heads_here, axis=0)
    block_rows = 4 * capacity
    block_count = slot_count // block_rows

    def one_head(inputs):
        triple, key_mask = inputs
        queries = triple[0].reshape(block_count, block_rows, HEAD)

        def one_block(query):
            scores = jnp.einsum(
                "qd,kd->qk", query, triple[1], preferred_element_type=jnp.float32
            ) / math.sqrt(HEAD)
            scores = jnp.where(key_mask[None, :], scores, -jnp.inf)
            row_top = jnp.max(scores, axis=1, keepdims=True)
            weights = jnp.exp(scores - row_top)
            weights = (weights / jnp.sum(weights, axis=1, keepdims=True)).astype(jnp.bfloat16)
            return jnp.dot(weights, triple[2], preferred_element_type=jnp.float32).astype(
                jnp.bfloat16
            )

        return lax.map(one_block, queries).reshape(slot_count, HEAD)

    result = lax.map(one_head, (stacked, head_masks))
    return (
        result.reshape(item_count, heads_here, slot_count, HEAD)
        .transpose(0, 2, 1, 3)
        .reshape(item_count, slot_count, heads_here * HEAD)
    )


def modulate(hidden, row_mean, spread, shift_part, gain_part):
    return (
        (hidden - row_mean) / jnp.sqrt(spread + ln_epsilon) * (1.0 + gain_part) + shift_part
    ).astype(jnp.bfloat16)


def body(projected, lengths, text_len, out_weight, modulation, proj_weight, latent, timestep):
    seq_count = lax.axis_size("seq")
    item_count, capacity = (projected.shape[1], projected.shape[2])
    attn_width = projected.shape[3] // 3
    group_width = attn_width // seq_count
    slot_count = capacity * seq_count
    outgoing = projected[0].reshape(item_count, capacity, 3, seq_count, group_width)
    arrived = lax.all_to_all(outgoing, "seq", split_axis=3, concat_axis=1, tiled=True)
    grouped = arrived.reshape(item_count, slot_count, 3, group_width // HEAD, HEAD)
    key_slots, unused_video = slot_masks(
        lengths, text_len, jnp.arange(slot_count, dtype=jnp.int32), capacity
    )
    attended = attention(grouped, key_slots, capacity)
    returned = lax.all_to_all(
        attended.reshape(item_count, slot_count, 1, group_width),
        "seq",
        split_axis=1,
        concat_axis=2,
        tiled=True,
    )
    attn_rows = returned.reshape(item_count * capacity, attn_width)
    first = lax.axis_index("cfg") == 0
    columns = lax.all_gather(out_weight, "cfg", axis=1, tiled=True)
    hidden = jnp.dot(
        attn_rows,
        lax.all_gather(columns, "seq", axis=0, tiled=True),
        preferred_element_type=jnp.float32,
    )
    hidden = hidden.reshape(item_count, capacity, D)
    row_mean = jnp.mean(hidden, axis=2, keepdims=True)
    spread = jnp.mean(hidden * hidden, axis=2, keepdims=True) - row_mean * row_mean
    normed = modulate(
        hidden, row_mean, spread, modulation[:, 0][:, None, :], modulation[:, 1][:, None, :]
    )
    velocity = jnp.dot(
        normed.reshape(item_count * capacity, D), proj_weight, preferred_element_type=jnp.float32
    ).reshape(item_count, capacity, OUT_CH)
    partner = partner_2(velocity.astype(jnp.bfloat16), "cfg", 0).astype(velocity.dtype)
    conditional = jnp.where(first, velocity, partner)
    unconditional = jnp.where(first, partner, velocity)
    own_slots = lax.axis_index("seq") * capacity + jnp.arange(capacity, dtype=jnp.int32)
    unused_keys, video_slots = slot_masks(lengths, text_len, own_slots, capacity)
    video_mask = video_slots[:, :, None]
    half_channels = latent.shape[2]
    channel_start = lax.axis_index("cfg") * half_channels
    conditional = lax.dynamic_slice_in_dim(conditional, channel_start, half_channels, 2)
    unconditional = lax.dynamic_slice_in_dim(unconditional, channel_start, half_channels, 2)
    guided = jnp.where(video_mask, unconditional + guide_scale * (conditional - unconditional), 0.0)
    alpha_now, alpha_prev = plan(timestep)
    clean_part = jnp.sqrt(alpha_now) * latent - jnp.sqrt(1.0 - alpha_now) * guided
    noise_part = jnp.sqrt(1.0 - alpha_now) * latent + jnp.sqrt(alpha_now) * guided
    previous = jnp.where(
        video_mask, jnp.sqrt(alpha_prev) * clean_part + jnp.sqrt(1.0 - alpha_prev) * noise_part, 0.0
    )
    return (guided, previous)


def solution(mesh):
    placed = (
        P("cfg", "req", "seq", None),
        P("req", None),
        P("req"),
        P("seq", "cfg"),
        P("req", None, None),
        P(),
        P("req", "seq", "cfg"),
        P("req"),
    )
    return jax.shard_map(
        body,
        mesh=mesh,
        in_specs=placed,
        out_specs=(P("req", "seq", "cfg"), P("req", "seq", "cfg")),
        check_vma=False,
    )
```

profile of v0, /device:TPU:1, one launch (start us, length us, event | category | flops | bytes accessed | tf_op | source)
XLA Modules:
  0.0 241.6 jit_solution(4758087153415635634)
XLA Ops:
  11.8 7.7 %all-to-all-start = ((bf16[1,224,3,16,128]{4,1,2,0,3:T(8,128)(2,1)}), bf16[1,224,3,16,128]{4,1,2,0,3:T(8,128)(2,1)S(1)}, u32[]{:S(2)}, u32[]{:S(2)}) async-start(bf16[1,224,3,16,128]{4,1,2,0,3:T(8,128)(2,1)} %copy.31), calls=%async_computation | async-start | bytes 5505024 | tf_op jit(solution)/shard_map/all_to_all | solution.py:96
  19.6 3.1 %all_gather.6 = bf16[128,3072]{1,0:T(8,128)(2,1)} all-gather(bf16[128,1536]{1,0:T(8,128)(2,1)S(1)} %copy-done.2), channel_id=1, replica_groups=mesh['req'=8,'cfg'=2,'seq'=16] {'cfg'}, dimensions={1}, use_global_device_ids=true | all-gather | bytes 1179648 | tf_op jit(solution)/shard_map/all_gather | solution.py:111
  23.8 37.0 %all-to-all-done = bf16[1,224,3,16,128]{4,1,2,0,3:T(8,128)(2,1)S(1)} async-done(((bf16[1,224,3,16,128]{4,1,2,0,3:T(8,128)(2,1)}), bf16[1,224,3,16,128]{4,1,2,0,3:T(8,128)(2,1)S(1)}, u32[]{:S(2)}, u32[]{:S(2)}) %all-to-all-start) | async-done | bytes 2752544 | tf_op jit(solution)/shard_map/all_to_all | solution.py:96
  62.4 3.8 %copy.32 = bf16[1,16,224,3,1,128]{2,1,5,3,4,0:T(8,128)(2,1)S(1)} copy(bf16[1,16,224,3,1,128]{5,2,3,1,4,0:T(8,128)(2,1)} %bitcast.85) | data formatting | bytes 5505024 | tf_op jit(solution)/shard_map/all_to_all | solution.py:96
  66.2 6.2 %reshape.377 = bf16[1,3584,3,2,64]{1,4,3,2,0:T(8,128)(2,1)} reshape(bf16[1,16,224,3,1,128]{2,1,5,3,4,0:T(8,128)(2,1)S(1)} %copy.32) | data formatting | bytes 5505024 | tf_op jit(solution)/shard_map/reshape | solution.py:97
  72.4 98.2 %while.21 = (s32[]{:T(128)}, bf16[2,3584,64]{1,2,0:T(8,128)(2,1)}, bf16[2,3,3584,64]{2,3,0,1:T(8,128)(2,1)}, pred[2,3584]{1,0:T(4,128)(4,1)S(1)}, s32[]{:T(128)}, /*index=5*/s32[]{:T(128)}, s32[]{:T(128)}) while((s32[]{:T(128)}, bf16[2,3584,64]{1,2,0:T(8,128)(2,1)}, bf16[2,3,3584,64]{2,3,0,1:T(8,128)(2,1)}, pred[2,3584]{1,0:T(4,128)(4,1)S(1)}, ...), condition=%wide.region_10.11_spmd, body=%wide.region_5.10_spmd.sunk | while | flops 860674304 | bytes 49928912 | solution.py:75
  75.0 2.9 %copy.52 = bf16[1,3,3584,64]{3,2,1,0:T(8,128)(2,1)S(1)} copy(bf16[1,3,3584,64]{2,3,0,1:T(8,128)(2,1)} %constant_dynamic-slice_fusion.2) | data formatting | bytes 2752512 | tf_op jit(solution)/shard_map/while/body/jit(dynamic_index_in_dim)/dynamic_slice | solution.py:75
  79.0 40.0 %while.22 = (s32[]{:T(128)}, bf16[4,896,64]{1,2,0:T(8,128)(2,1)}, pred[3584]{0:T(1024)(128)(4,1)S(1)}, bf16[4,896,64]{2,1,0:T(8,128)(2,1)}, bf16[3,3584,64]{2,1,0:T(8,128)(2,1)S(1)}, /*index=5*/s32[]{:T(128)}) while((s32[]{:T(128)}, bf16[4,896,64]{1,2,0:T(8,128)(2,1)}, pred[3584]{0:T(1024)(128)(4,1)S(1)}, bf16[4,896,64]{2,1,0:T(8,128)(2,1)}, ...), condition=%wide.region_9.9_spmd, body=%wide.region_6.8_spmd.sunk | while | flops 860674304 | bytes 40746052 | solution.py:73
  79.0 3.1 %fusion.39 = (f32[896]{0:T(1024)S(1)}, f32[896,3584]{1,0:T(8,128)S(1)}) fusion(pred[3584]{0:T(1024)(128)(4,1)S(1)} %get-tuple-element.188, bf16[3,3584,64]{2,1,0:T(8,128)(2,1)S(1)} %get-tuple-element.190, bf16[4,896,64]{2,1,0:T(8,128)(2,1)} %get-tuple-element.189, s32[]{:T(128)} %get-tuple-element.180), kind=kOutput, calls=%fused_computation.3.clone.1 | convolution fusion | flops 420674688 | bytes 14000128 | tf_op jit(solution)/shard_map/while/body/eval_jaxpr/while/body/eval_jaxpr/qd,kd->qk/dot_general | solution.py:62
  84.9 4.1 %fusion.41 = bf16[4,896,64]{1,2,0:T(8,128)(2,1)} fusion(bf16[4,896,64]{1,2,0:T(8,128)(2,1)} %get-tuple-element.181, s32[]{:T(128)} %get-tuple-element.180, f32[896,3584]{1,0:T(8,128)S(1)} %get-tuple-element.172, f32[896]{0:T(1024)S(1)} %fusion.40, f32[896]{0:T(1024)S(1)} %get-tuple-element.173, pred[3584]{0:T(1024)(128)(4,1)S(1)} %get-tuple-element.188, ...), kind=kOutput, calls=%fused_computation.8.clone.1 | convolution fusion | flops 427155456 | bytes 13890048 | tf_op jit(solution)/shard_map/while/body/eval_jaxpr/while/body/eval_jaxpr/dot_general | solution.py:69
  89.0 3.1 %fusion.39 = (f32[896]{0:T(1024)S(1)}, f32[896,3584]{1,0:T(8,128)S(1)}) fusion(pred[3584]{0:T(1024)(128)(4,1)S(1)} %get-tuple-element.188, bf16[3,3584,64]{2,1,0:T(8,128)(2,1)S(1)} %get-tuple-element.190, bf16[4,896,64]{2,1,0:T(8,128)(2,1)} %get-tuple-element.189, s32[]{:T(128)} %get-tuple-element.180), kind=kOutput, calls=%fused_computation.3.clone.1 | convolution fusion | flops 420674688 | bytes 14000128 | tf_op jit(solution)/shard_map/while/body/eval_jaxpr/while/body/eval_jaxpr/qd,kd->qk/dot_general | solution.py:62
  94.8 4.1 %fusion.41 = bf16[4,896,64]{1,2,0:T(8,128)(2,1)} fusion(bf16[4,896,64]{1,2,0:T(8,128)(2,1)} %get-tuple-element.181, s32[]{:T(128)} %get-tuple-element.180, f32[896,3584]{1,0:T(8,128)S(1)} %get-tuple-element.172, f32[896]{0:T(1024)S(1)} %fusion.40, f32[896]{0:T(1024)S(1)} %get-tuple-element.173, pred[3584]{0:T(1024)(128)(4,1)S(1)} %get-tuple-element.188, ...), kind=kOutput, calls=%fused_computation.8.clone.1 | convolution fusion | flops 427155456 | bytes 13890048 | tf_op jit(solution)/shard_map/while/body/eval_jaxpr/while/body/eval_jaxpr/dot_general | solution.py:69
  99.0 3.1 %fusion.39 = (f32[896]{0:T(1024)S(1)}, f32[896,3584]{1,0:T(8,128)S(1)}) fusion(pred[3584]{0:T(1024)(128)(4,1)S(1)} %get-tuple-element.188, bf16[3,3584,64]{2,1,0:T(8,128)(2,1)S(1)} %get-tuple-element.190, bf16[4,896,64]{2,1,0:T(8,128)(2,1)} %get-tuple-element.189, s32[]{:T(128)} %get-tuple-element.180), kind=kOutput, calls=%fused_computation.3.clone.1 | convolution fusion | flops 420674688 | bytes 14000128 | tf_op jit(solution)/shard_map/while/body/eval_jaxpr/while/body/eval_jaxpr/qd,kd->qk/dot_general | solution.py:62
  104.9 4.1 %fusion.41 = bf16[4,896,64]{1,2,0:T(8,128)(2,1)} fusion(bf16[4,896,64]{1,2,0:T(8,128)(2,1)} %get-tuple-element.181, s32[]{:T(128)} %get-tuple-element.180, f32[896,3584]{1,0:T(8,128)S(1)} %get-tuple-element.172, f32[896]{0:T(1024)S(1)} %fusion.40, f32[896]{0:T(1024)S(1)} %get-tuple-element.173, pred[3584]{0:T(1024)(128)(4,1)S(1)} %get-tuple-element.188, ...), kind=kOutput, calls=%fused_computation.8.clone.1 | convolution fusion | flops 427155456 | bytes 13890048 | tf_op jit(solution)/shard_map/while/body/eval_jaxpr/while/body/eval_jaxpr/dot_general | solution.py:69
  109.0 3.1 %fusion.39 = (f32[896]{0:T(1024)S(1)}, f32[896,3584]{1,0:T(8,128)S(1)}) fusion(pred[3584]{0:T(1024)(128)(4,1)S(1)} %get-tuple-element.188, bf16[3,3584,64]{2,1,0:T(8,128)(2,1)S(1)} %get-tuple-element.190, bf16[4,896,64]{2,1,0:T(8,128)(2,1)} %get-tuple-element.189, s32[]{:T(128)} %get-tuple-element.180), kind=kOutput, calls=%fused_computation.3.clone.1 | convolution fusion | flops 420674688 | bytes 14000128 | tf_op jit(solution)/shard_map/while/body/eval_jaxpr/while/body/eval_jaxpr/qd,kd->qk/dot_general | solution.py:62
  114.8 4.1 %fusion.41 = bf16[4,896,64]{1,2,0:T(8,128)(2,1)} fusion(bf16[4,896,64]{1,2,0:T(8,128)(2,1)} %get-tuple-element.181, s32[]{:T(128)} %get-tuple-element.180, f32[896,3584]{1,0:T(8,128)S(1)} %get-tuple-element.172, f32[896]{0:T(1024)S(1)} %fusion.40, f32[896]{0:T(1024)S(1)} %get-tuple-element.173, pred[3584]{0:T(1024)(128)(4,1)S(1)} %get-tuple-element.188, ...), kind=kOutput, calls=%fused_computation.8.clone.1 | convolution fusion | flops 427155456 | bytes 13890048 | tf_op jit(solution)/shard_map/while/body/eval_jaxpr/while/body/eval_jaxpr/dot_general | solution.py:69
  124.1 2.9 %copy.52 = bf16[1,3,3584,64]{3,2,1,0:T(8,128)(2,1)S(1)} copy(bf16[1,3,3584,64]{2,3,0,1:T(8,128)(2,1)} %constant_dynamic-slice_fusion.2) | data formatting | bytes 2752512 | tf_op jit(solution)/shard_map/while/body/jit(dynamic_index_in_dim)/dynamic_slice | solution.py:75
  128.1 39.9 %while.22 = (s32[]{:T(128)}, bf16[4,896,64]{1,2,0:T(8,128)(2,1)}, pred[3584]{0:T(1024)(128)(4,1)S(1)}, bf16[4,896,64]{2,1,0:T(8,128)(2,1)}, bf16[3,3584,64]{2,1,0:T(8,128)(2,1)S(1)}, /*index=5*/s32[]{:T(128)}) while((s32[]{:T(128)}, bf16[4,896,64]{1,2,0:T(8,128)(2,1)}, pred[3584]{0:T(1024)(128)(4,1)S(1)}, bf16[4,896,64]{2,1,0:T(8,128)(2,1)}, ...), condition=%wide.region_9.9_spmd, body=%wide.region_6.8_spmd.sunk | while | flops 860674304 | bytes 40746052 | solution.py:73
  128.1 3.1 %fusion.39 = (f32[896]{0:T(1024)S(1)}, f32[896,3584]{1,0:T(8,128)S(1)}) fusion(pred[3584]{0:T(1024)(128)(4,1)S(1)} %get-tuple-element.188, bf16[3,3584,64]{2,1,0:T(8,128)(2,1)S(1)} %get-tuple-element.190, bf16[4,896,64]{2,1,0:T(8,128)(2,1)} %get-tuple-element.189, s32[]{:T(128)} %get-tuple-element.180), kind=kOutput, calls=%fused_computation.3.clone.1 | convolution fusion | flops 420674688 | bytes 14000128 | tf_op jit(solution)/shard_map/while/body/eval_jaxpr/while/body/eval_jaxpr/qd,kd->qk/dot_general | solution.py:62
  133.9 4.1 %fusion.41 = bf16[4,896,64]{1,2,0:T(8,128)(2,1)} fusion(bf16[4,896,64]{1,2,0:T(8,128)(2,1)} %get-tuple-element.181, s32[]{:T(128)} %get-tuple-element.180, f32[896,3584]{1,0:T(8,128)S(1)} %get-tuple-element.172, f32[896]{0:T(1024)S(1)} %fusion.40, f32[896]{0:T(1024)S(1)} %get-tuple-element.173, pred[3584]{0:T(1024)(128)(4,1)S(1)} %get-tuple-element.188, ...), kind=kOutput, calls=%fused_computation.8.clone.1 | convolution fusion | flops 427155456 | bytes 13890048 | tf_op jit(solution)/shard_map/while/body/eval_jaxpr/while/body/eval_jaxpr/dot_general | solution.py:69
  138.1 3.1 %fusion.39 = (f32[896]{0:T(1024)S(1)}, f32[896,3584]{1,0:T(8,128)S(1)}) fusion(pred[3584]{0:T(1024)(128)(4,1)S(1)} %get-tuple-element.188, bf16[3,3584,64]{2,1,0:T(8,128)(2,1)S(1)} %get-tuple-element.190, bf16[4,896,64]{2,1,0:T(8,128)(2,1)} %get-tuple-element.189, s32[]{:T(128)} %get-tuple-element.180), kind=kOutput, calls=%fused_computation.3.clone.1 | convolution fusion | flops 420674688 | bytes 14000128 | tf_op jit(solution)/shard_map/while/body/eval_jaxpr/while/body/eval_jaxpr/qd,kd->qk/dot_general | solution.py:62
  143.9 4.1 %fusion.41 = bf16[4,896,64]{1,2,0:T(8,128)(2,1)} fusion(bf16[4,896,64]{1,2,0:T(8,128)(2,1)} %get-tuple-element.181, s32[]{:T(128)} %get-tuple-element.180, f32[896,3584]{1,0:T(8,128)S(1)} %get-tuple-element.172, f32[896]{0:T(1024)S(1)} %fusion.40, f32[896]{0:T(1024)S(1)} %get-tuple-element.173, pred[3584]{0:T(1024)(128)(4,1)S(1)} %get-tuple-element.188, ...), kind=kOutput, calls=%fused_computation.8.clone.1 | convolution fusion | flops 427155456 | bytes 13890048 | tf_op jit(solution)/shard_map/while/body/eval_jaxpr/while/body/eval_jaxpr/dot_general | solution.py:69
  148.0 3.1 %fusion.39 = (f32[896]{0:T(1024)S(1)}, f32[896,3584]{1,0:T(8,128)S(1)}) fusion(pred[3584]{0:T(1024)(128)(4,1)S(1)} %get-tuple-element.188, bf16[3,3584,64]{2,1,0:T(8,128)(2,1)S(1)} %get-tuple-element.190, bf16[4,896,64]{2,1,0:T(8,128)(2,1)} %get-tuple-element.189, s32[]{:T(128)} %get-tuple-element.180), kind=kOutput, calls=%fused_computation.3.clone.1 | convolution fusion | flops 420674688 | bytes 14000128 | tf_op jit(solution)/shard_map/while/body/eval_jaxpr/while/body/eval_jaxpr/qd,kd->qk/dot_general | solution.py:62
  153.9 4.1 %fusion.41 = bf16[4,896,64]{1,2,0:T(8,128)(2,1)} fusion(bf16[4,896,64]{1,2,0:T(8,128)(2,1)} %get-tuple-element.181, s32[]{:T(128)} %get-tuple-element.180, f32[896,3584]{1,0:T(8,128)S(1)} %get-tuple-element.172, f32[896]{0:T(1024)S(1)} %fusion.40, f32[896]{0:T(1024)S(1)} %get-tuple-element.173, pred[3584]{0:T(1024)(128)(4,1)S(1)} %get-tuple-element.188, ...), kind=kOutput, calls=%fused_computation.8.clone.1 | convolution fusion | flops 427155456 | bytes 13890048 | tf_op jit(solution)/shard_map/while/body/eval_jaxpr/while/body/eval_jaxpr/dot_general | solution.py:69
  158.0 3.1 %fusion.39 = (f32[896]{0:T(1024)S(1)}, f32[896,3584]{1,0:T(8,128)S(1)}) fusion(pred[3584]{0:T(1024)(128)(4,1)S(1)} %get-tuple-element.188, bf16[3,3584,64]{2,1,0:T(8,128)(2,1)S(1)} %get-tuple-element.190, bf16[4,896,64]{2,1,0:T(8,128)(2,1)} %get-tuple-element.189, s32[]{:T(128)} %get-tuple-element.180), kind=kOutput, calls=%fused_computation.3.clone.1 | convolution fusion | flops 420674688 | bytes 14000128 | tf_op jit(solution)/shard_map/while/body/eval_jaxpr/while/body/eval_jaxpr/qd,kd->qk/dot_general | solution.py:62
  163.9 4.1 %fusion.41 = bf16[4,896,64]{1,2,0:T(8,128)(2,1)} fusion(bf16[4,896,64]{1,2,0:T(8,128)(2,1)} %get-tuple-element.181, s32[]{:T(128)} %get-tuple-element.180, f32[896,3584]{1,0:T(8,128)S(1)} %get-tuple-element.172, f32[896]{0:T(1024)S(1)} %fusion.40, f32[896]{0:T(1024)S(1)} %get-tuple-element.173, pred[3584]{0:T(1024)(128)(4,1)S(1)} %get-tuple-element.188, ...), kind=kOutput, calls=%fused_computation.8.clone.1 | convolution fusion | flops 427155456 | bytes 13890048 | tf_op jit(solution)/shard_map/while/body/eval_jaxpr/while/body/eval_jaxpr/dot_general | solution.py:69
  170.6 4.3 %copy.35 = bf16[1,3584,1,128]{3,2,0,1:T(2,128)(2,1)S(1)} copy(bf16[1,3584,1,128]{1,3,2,0:T(8,128)(2,1)} %bitcast.92) | data formatting | bytes 1835008 | tf_op jit(solution)/shard_map/reshape;reshape | solution.py:103
  175.4 19.9 %reduce.10 = bf16[3584,128]{1,0:T(8,128)(2,1)S(1)} reduce(bf16[3584,1,1,128]{3,2,1,0:T(2,128)(2,1)S(1)} %bitcast.87, bf16[]{:T(256)} %broadcast.370), dimensions={1,2}, to_apply=%bitcast.55.reduce_sub_computation | reduce | bytes 1835010
  196.5 8.8 %all-to-all-start.1 = ((bf16[16,2,14336]{2,1,0:T(2,128)(2,1)}), bf16[16,2,14336]{2,1,0:T(2,128)(2,1)S(1)}, u32[]{:S(2)}, u32[]{:S(2)}) async-start(bf16[16,2,14336]{2,1,0:T(2,128)(2,1)} %reshape.384), calls=%async_computation.1 | async-start | bytes 1835008 | tf_op jit(solution)/shard_map/all_to_all | solution.py:102
  205.4 11.1 %all-to-all-done.1 = bf16[16,2,14336]{2,1,0:T(2,128)(2,1)S(1)} async-done(((bf16[16,2,14336]{2,1,0:T(2,128)(2,1)}), bf16[16,2,14336]{2,1,0:T(2,128)(2,1)S(1)}, u32[]{:S(2)}, u32[]{:S(2)}) %all-to-all-start.1) | async-done | bytes 917536 | tf_op jit(solution)/shard_map/all_to_all | solution.py:102
  217.9 6.3 %fusion.31 = (f32[224]{0:T(256)S(1)}, f32[224]{0:T(256)S(1)}, f32[224,3072]{1,0:T(8,128)S(1)}) fusion(bf16[2048,3072]{1,0:T(8,128)(2,1)} %all-gather.2.cloned.1.call-done, bf16[28,8,16,128]{3,2,1,0:T(8,128)(2,1)S(1)} %bitcast.91), kind=kOutput, calls=%fused_computation.66 | convolution fusion | flops 2820636160 | bytes 16254720 | tf_op jit(solution)/shard_map/dot_general | solution.py:112
  225.1 5.5 %collective-permute-start = (bf16[1,224,64]{1,2,0:T(8,128)(2,1)S(1)}, bf16[1,224,64]{1,2,0:T(8,128)(2,1)S(1)}, u32[]{:S(2)}, u32[]{:S(2)}) collective-permute-start(bf16[1,224,64]{1,2,0:T(8,128)(2,1)S(1)} %convert_bitcast_fusion), channel_id=1, source_target_pairs={{0,16},{16,0},{1,17},{17,1},{2,18},{18,2},{3,19},{19,3},{4,20},{20... | collective-permute-start | bytes 86024 | tf_op jit(solution)/shard_map/ppermute | solution.py:20
  (69 shorter events, 47.3 us)
Async XLA Ops:
  7.2 217.2 %copy-start = (bf16[3072,64]{0,1:T(8,128)(2,1)S(1)}, bf16[3072,64]{0,1:T(8,128)(2,1)}, u32[]{:S(2)}) copy-start(bf16[3072,64]{0,1:T(8,128)(2,1)} %param.17) | copy-start | bytes 1179652
  11.8 7.8 %copy-start.2 = (bf16[128,1536]{1,0:T(8,128)(2,1)S(1)}, bf16[128,1536]{1,0:T(8,128)(2,1)}, u32[]{:S(2)}) copy-start(bf16[128,1536]{1,0:T(8,128)(2,1)} %param.15) | copy-start | bytes 1179652
  11.8 10.9 %copy-start.5 = (s32[1,16]{1,0:T(1,128)S(1)}, s32[1,16]{1,0:T(1,128)}, u32[]{:S(2)}) copy-start(s32[1,16]{1,0:T(1,128)} %param.13) | copy-start | bytes 196
  11.8 49.0 %all-to-all-start = ((bf16[1,224,3,16,128]{4,1,2,0,3:T(8,128)(2,1)}), bf16[1,224,3,16,128]{4,1,2,0,3:T(8,128)(2,1)S(1)}, u32[]{:S(2)}, u32[]{:S(2)}) async-start(bf16[1,224,3,16,128]{4,1,2,0,3:T(8,128)(2,1)} %copy.31), calls=%async_computation | async-start | bytes 5505024 | tf_op jit(solution)/shard_map/all_to_all | solution.py:96
  19.6 198.4 %all-gather.2.cloned.1.call-start = ((), (), s32[]{:S(2)}) async-start(), calls=%async_computation.2 | async-start | bytes 13369344 | tf_op jit(solution)/shard_map/all_gather | solution.py:114
  23.6 37.2 %copy-start.7 = (s32[16]{0:T(128)}, s32[16]{0:T(128)S(1)}, u32[]{:S(2)}) copy-start(s32[16]{0:T(128)S(1)} %subtract_bitcast_fusion) | copy-start | bytes 196
  60.9 1.5 copy-start.1
  175.4 29.9 %copy-start.6 = (s32[1,16]{1,0:T(1,128)S(1)}, s32[1,16]{1,0:T(1,128)}, u32[]{:S(2)}) copy-start(s32[1,16]{1,0:T(1,128)} %param.13) | copy-start | bytes 196
  175.4 29.9 %copy-start.8 = (s32[16]{0:T(128)S(1)}, s32[16]{0:T(128)}, u32[]{:S(2)}) copy-start(s32[16]{0:T(128)} %copy-done.7) | copy-start | bytes 196
  175.4 30.0 %copy-start.4 = (f32[1,2,3072]{2,1,0:T(2,128)S(1)}, f32[1,2,3072]{2,1,0:T(2,128)}, u32[]{:S(2)}) copy-start(f32[1,2,3072]{2,1,0:T(2,128)} %param.16) | copy-start | bytes 73732
  196.5 20.0 %all-to-all-start.1 = ((bf16[16,2,14336]{2,1,0:T(2,128)(2,1)}), bf16[16,2,14336]{2,1,0:T(2,128)(2,1)S(1)}, u32[]{:S(2)}, u32[]{:S(2)}) async-start(bf16[16,2,14336]{2,1,0:T(2,128)(2,1)} %reshape.384), calls=%async_computation.1 | async-start | bytes 1835008 | tf_op jit(solution)/shard_map/all_to_all | solution.py:102
  224.3 9.7 %copy-start.3 = (f32[1,224,32]{1,2,0:T(8,128)S(1)}, f32[1,224,32]{1,2,0:T(8,128)}, u32[]{:S(2)}) copy-start(f32[1,224,32]{1,2,0:T(8,128)} %param.18) | copy-start | bytes 86020
  225.1 9.0 %collective-permute-start = (bf16[1,224,64]{1,2,0:T(8,128)(2,1)S(1)}, bf16[1,224,64]{1,2,0:T(8,128)(2,1)S(1)}, u32[]{:S(2)}, u32[]{:S(2)}) collective-permute-start(bf16[1,224,64]{1,2,0:T(8,128)(2,1)S(1)} %convert_bitcast_fusion), channel_id=1, source_target_pairs={{0,16},{16,0},{1,17},{17,1},{2,18},{18,2},{3,19},{19,3},{4,20},{20... | collective-permute-start | bytes 86024 | tf_op jit(solution)/shard_map/ppermute | solution.py:20
Sparse Core Ops, SparseCore 0:
  22.8 112.8 all-gather.1
where the time goes:
time: 243 us; the launch traced here: 242 us
  matrix products  64.5 us (27%)
  waiting for transfers between devices  48.1 us (20%)
  other arithmetic  44.7 us (18%)
  local copies, waits for them, and re-layouts  41.8 us (17%)
  starting transfers between devices  22 us (9%)
  between operations  17.2 us (7%)
  blocking collectives  3.08 us (1%)
    all_to_all x1, waiting for transfers between devices, body(): lax.all_to_all(outgoing, 'seq', split_axis=3, concat_axis=1, tiled=True)  37 us
    dot_general x8, matrix products, one_block(): jnp.dot(weights, triple[2], preferred_element_type=jnp.float32)  32.9 us
    dot_general x8, matrix products, one_block(): jnp.einsum('qd,kd->qk', query, triple[1], preferred_element_type=jnp.floa...  24.6 us
    reduce_sum x8, other arithmetic, one_block(): jnp.sum(weights, axis=1, keepdims=True)  22.4 us
    unnamed x1, other arithmetic  19.9 us
    all_to_all x1, waiting for transfers between devices, body(): lax.all_to_all(attended.reshape(item_count, slot_count, 1, group_width),...  11.1 us
    dynamic_slice x6, local copies, waits for them, and re-layouts, attention(): result = lax.map(one_head, (stacked, head_masks))  11 us
    all_to_all x1, starting transfers between devices, body(): lax.all_to_all(attended.reshape(item_count, slot_count, 1, group_width),...  8.78 us
  transfers between devices with their start and end apart: 4, of which 2 were waited for; matrix products, arithmetic and copies ran while one was open for 57% of the time, Pallas kernels for 0%

commit v1 on v0

--- a/solution.py
+++ b/solution.py
@@ -4,6 +4,8 @@
 import jax.numpy as jnp
 from jax import lax
 from jax.sharding import PartitionSpec as P
+from jax.experimental import pallas as pl
+from jax.experimental.pallas import tpu as pltpu
 
 D = 3072
 HEAD = 64
@@ -47,37 +49,43 @@
     return (alpha_now, alpha_prev)
 
 
-def attention(grouped, key_slots, capacity):
-    item_count, slot_count, heads_here = (grouped.shape[0], grouped.shape[1], grouped.shape[3])
-    stacked = grouped.transpose(0, 3, 2, 1, 4).reshape(item_count * heads_here, 3, slot_count, HEAD)
-    head_masks = jnp.repeat(key_slots, heads_here, axis=0)
-    block_rows = 4 * capacity
-    block_count = slot_count // block_rows
+def attention_kernel(x_ref, bias_ref, o_ref):
+    block = o_ref.shape[0]
+    start = pl.multiple_of(pl.program_id(0) * block, block)
+    query = x_ref[pl.ds(start, block), 0:128]
+    keyset = x_ref[:, 128:256]
+    values = x_ref[:, 256:384]
+    bias = bias_ref[...]
+    lane = lax.broadcasted_iota(jnp.int32, query.shape, 1)
+    results = []
+    for head in range(2):
+        own = (lane >= HEAD) if head else (lane < HEAD)
+        masked = jnp.where(own, query, jnp.zeros_like(query))
+        scores = lax.dot_general(
+            masked, keyset, (((1,), (1,)), ((), ())), preferred_element_type=jnp.float32
+        )
+        scores = scores * (1.0 / math.sqrt(HEAD)) + bias
+        row_top = jnp.max(scores, axis=1, keepdims=True)
+        weights = jnp.exp(scores - row_top)
+        total = jnp.sum(weights, axis=1, keepdims=True)
+        probs = (weights * (1.0 / total)).astype(jnp.bfloat16)
+        results.append(jnp.dot(probs, values, preferred_element_type=jnp.float32))
+    o_ref[...] = jnp.where(lane < HEAD, results[0], results[1]).astype(o_ref.dtype)
 
-    def one_head(inputs):
-        triple, key_mask = inputs
-        queries = triple[0].reshape(block_count, block_rows, HEAD)
 
-        def one_block(query):
-            scores = jnp.einsum(
-                "qd,kd->qk", query, triple[1], preferred_element_type=jnp.float32
-            ) / math.sqrt(HEAD)
-            scores = jnp.where(key_mask[None, :], scores, -jnp.inf)
-            row_top = jnp.max(scores, axis=1, keepdims=True)
-            weights = jnp.exp(scores - row_top)
-            weights = (weights / jnp.sum(weights, axis=1, keepdims=True)).astype(jnp.bfloat16)
-            return jnp.dot(weights, triple[2], preferred_element_type=jnp.float32).astype(
-                jnp.bfloat16
-            )
-
-        return lax.map(one_block, queries).reshape(slot_count, HEAD)
-
-    result = lax.map(one_head, (stacked, head_masks))
-    return (
-        result.reshape(item_count, heads_here, slot_count, HEAD)
-        .transpose(0, 2, 1, 3)
-        .reshape(item_count, slot_count, heads_here * HEAD)
-    )
+def attention(grouped, bias, block_rows=256):
+    slot_count, width = grouped.shape
+    return pl.pallas_call(
+        attention_kernel,
+        grid=(slot_count // block_rows,),
+        in_specs=[
+            pl.BlockSpec((slot_count, width), lambda i: (0, 0)),
+            pl.BlockSpec((1, slot_count), lambda i: (0, 0)),
+        ],
+        out_specs=pl.BlockSpec((block_rows, width // 3), lambda i: (i, 0)),
+        out_shape=jax.ShapeDtypeStruct((slot_count, width // 3), jnp.bfloat16),
+        compiler_params=pltpu.CompilerParams(vmem_limit_bytes=48 * 1024 * 1024),
+    )(grouped, bias)
 
 
 def modulate(hidden, row_mean, spread, shift_part, gain_part):
@@ -92,20 +100,23 @@
     attn_width = projected.shape[3] // 3
     group_width = attn_width // seq_count
     slot_count = capacity * seq_count
-    outgoing = projected[0].reshape(item_count, capacity, 3, seq_count, group_width)
-    arrived = lax.all_to_all(outgoing, "seq", split_axis=3, concat_axis=1, tiled=True)
-    grouped = arrived.reshape(item_count, slot_count, 3, group_width // HEAD, HEAD)
+    outgoing = projected[0, 0].reshape(capacity, 3, seq_count, group_width)
+    outgoing = outgoing.transpose(2, 0, 1, 3)
+    arrived = lax.all_to_all(outgoing, "seq", split_axis=0, concat_axis=0, tiled=True)
+    grouped = arrived.reshape(slot_count, 3 * group_width)
     key_slots, unused_video = slot_masks(
         lengths, text_len, jnp.arange(slot_count, dtype=jnp.int32), capacity
     )
-    attended = attention(grouped, key_slots, capacity)
+    bias = jnp.where(key_slots, 0.0, -jnp.inf).astype(jnp.float32)
+    attended = attention(grouped, bias)
     returned = lax.all_to_all(
-        attended.reshape(item_count, slot_count, 1, group_width),
+        attended.reshape(seq_count, capacity, group_width),
         "seq",
-        split_axis=1,
-        concat_axis=2,
+        split_axis=0,
+        concat_axis=0,
         tiled=True,
     )
+    returned = returned.transpose(1, 0, 2)
     attn_rows = returned.reshape(item_count * capacity, attn_width)
     first = lax.axis_index("cfg") == 0
     columns = lax.all_gather(out_weight, "cfg", axis=1, tiled=True)

time: 243 us -> 171 us (0.70)
  matrix products: 64.5 us -> 7.06 us
  Pallas kernels: 0 us -> 51.2 us
  other arithmetic: 44.7 us -> 2.5 us
  local copies, waits for them, and re-layouts: 41.8 us -> 7 us
  waiting for transfers between devices: 48.1 us -> 62.9 us
  starting transfers between devices: 22 us -> 15.6 us
  blocking collectives: 3.08 us -> 7.29 us
    dot_general x16 -> x0, matrix products: 57.5 us -> none  [the longest x8 32.9 us: one_block(): jnp.dot(weights, triple[2], preferred_element_type=jnp.float32)]
    pallas_call x0 -> x1, Pallas kernels: none -> 51.2 us  [attention(): pl.pallas_call(attention_kernel, grid=(slot_count // block_rows,), in_spe...]
    reduce_sum x8 -> x1, other arithmetic: 22.4 us -> 0.15 us  [slot_masks(): piece_len = jnp.sum(lengths[:, :, None] * select[None], axis=1)]
    unnamed x1 -> x0, other arithmetic: 19.9 us -> none
    all_to_all x2, waiting for transfers between devices: 48.1 us -> 62.9 us  [the longest x1 43.6 us: body(): lax.all_to_all(outgoing, 'seq', split_axis=0, concat_axis=0, tiled=True)]
    dynamic_slice x6 -> x0, local copies, waits for them, and re-layouts: 11 us -> none  [attention(): result = lax.map(one_head, (stacked, head_masks))]
    another operation x2 -> x0, local copies, waits for them, and re-layouts: 6.53 us -> none  [the longest x1 4.28 us: body(): attended.reshape(item_count, slot_count, 1, group_width)]
    reshape x2 -> x1, local copies, waits for them, and re-layouts: 6.24 us -> 1.89 us  [body(): grouped = arrived.reshape(slot_count, 3 * group_width)]
  transfers between devices with their start and end apart: 4 -> 4, of which waited for: 2 -> 2; matrix products, arithmetic and copies ran while one was open for 57% -> 5% of each run, Pallas kernels for 0% -> 30%
where the time goes in v1:
time: 171 us
  waiting for transfers between devices  62.9 us (37%)
  Pallas kernels  51.2 us (30%)
  between operations  17.1 us (10%)
  starting transfers between devices  15.6 us (9%)
  blocking collectives  7.29 us (4%)
  matrix products  7.06 us (4%)
  local copies, waits for them, and re-layouts  7 us (4%)
  other arithmetic  2.5 us (1%)
    pallas_call x1, Pallas kernels, attention(): pl.pallas_call(attention_kernel, grid=(slot_count // block_rows,), in_spe...  51.2 us
    all_to_all x1, waiting for transfers between devices, body(): lax.all_to_all(outgoing, 'seq', split_axis=0, concat_axis=0, tiled=True)  43.6 us
    all_to_all x1, waiting for transfers between devices, body(): lax.all_to_all(attended.reshape(seq_count, capacity, group_width), 'seq',...  19.3 us
    all_to_all x1, starting transfers between devices, body(): lax.all_to_all(attended.reshape(seq_count, capacity, group_width), 'seq',...  8.43 us
    all_gather x1, blocking collectives, body(): columns = lax.all_gather(out_weight, 'cfg', axis=1, tiled=True)  7.29 us
    dot_general x1, matrix products, body(): jnp.dot(attn_rows, lax.all_gather(columns, 'seq', axis=0, tiled=True), pr...  6.36 us
    all_to_all x1, starting transfers between devices, body(): lax.all_to_all(outgoing, 'seq', split_axis=0, concat_axis=0, tiled=True)  5.18 us
  transfers between devices with their start and end apart: 4, of which 2 were waited for; matrix products, arithmetic and copies ran while one was open for 5% of the time, Pallas kernels for 30%

profile of v1, /device:TPU:1, one launch (start us, length us, event | category | flops | bytes accessed | tf_op | source)
XLA Modules:
  0.0 170.6 jit_solution(16153676024810797878)
XLA Ops:
  7.2 0.0 copy-start
  7.2 0.0 all-gather.2.cloned.1.call-start
  7.2 7.3 %all_gather.6 = bf16[128,3072]{1,0:T(8,128)(2,1)} all-gather(bf16[128,1536]{1,0:T(8,128)(2,1)} %param.11), channel_id=1, replica_groups=mesh['req'=8,'cfg'=2,'seq'=16] {'cfg'}, dimensions={1}, use_global_device_ids=true | all-gather | bytes 1179648 | tf_op jit(solution)/shard_map/all_gather | solution.py:122
  14.5 0.0 all-gather.2.cloned.1.call-update
  14.5 2.4 %copy.28 = bf16[28,8,48,128]{3,2,1,0:T(8,128)(2,1)S(1)} copy(bf16[28,8,48,128]{3,1,2,0:T(8,128)(2,1)} %bitcast.41) | data formatting | bytes 5505024
  16.9 2.3 %copy.21 = bf16[16,224,3,128]{3,1,2,0:T(8,128)(2,1)} copy(bf16[16,224,3,128]{3,0,2,1:T(8,128)(2,1)S(1)} %bitcast.40) | data formatting | bytes 5505024 | tf_op jit(solution)/shard_map/transpose | solution.py:104
  19.2 0.0 copy-start.3
  19.2 5.2 %all-to-all-start = ((bf16[16,224,3,128]{3,1,2,0:T(8,128)(2,1)}), bf16[16,224,3,128]{3,1,2,0:T(8,128)(2,1)S(1)}, u32[]{:S(2)}, u32[]{:S(2)}) async-start(bf16[16,224,3,128]{3,1,2,0:T(8,128)(2,1)} %copy.21), calls=%async_computation | async-start | bytes 5505024 | tf_op jit(solution)/shard_map/all_to_all | solution.py:105
  25.0 0.0 copy-done.3
  25.0 0.2 reduce_window_sum.12
  25.2 0.2 select_reduce_fusion.1
  25.4 0.1 and_select_fusion.bias_ref
  25.5 43.6 %all-to-all-done = bf16[16,224,3,128]{3,1,2,0:T(8,128)(2,1)S(1)} async-done(((bf16[16,224,3,128]{3,1,2,0:T(8,128)(2,1)}), bf16[16,224,3,128]{3,1,2,0:T(8,128)(2,1)S(1)}, u32[]{:S(2)}, u32[]{:S(2)}) %all-to-all-start) | async-done | bytes 2752544 | tf_op jit(solution)/shard_map/all_to_all | solution.py:105
  69.0 1.9 %copy.25 = bf16[16,224,3,128]{3,2,1,0:T(4,128)(2,1)S(1)} copy(bf16[16,224,3,128]{3,1,2,0:T(8,128)(2,1)S(1)} %all-to-all-done) | data formatting | bytes 5505024 | tf_op jit(solution)/shard_map/reshape | solution.py:106
  70.9 0.5 copy.37
  71.4 0.0 copy-start.2
  71.4 51.2 %shard_map.98 = bf16[3584,128]{1,0:T(8,128)(2,1)} custom-call(bf16[3584,384]{1,0:T(8,128)(2,1)S(1)} %bitcast.38, f32[1,3584]{1,0:T(1,128)S(1)} %and_select_fusion.bias_ref), custom_call_target="tpu_custom_call" | custom-call | tf_op jit(solution)/shard_map/pallas_call | solution.py:78
  122.6 8.4 %all-to-all-start.1 = ((bf16[16,224,128]{2,1,0:T(8,128)(2,1)}), bf16[16,224,128]{2,1,0:T(8,128)(2,1)S(1)}, u32[]{:S(2)}, u32[]{:S(2)}) async-start(bf16[16,224,128]{2,1,0:T(8,128)(2,1)} %bitcast.4), calls=%async_computation.1 | async-start | bytes 1835008 | tf_op jit(solution)/shard_map/all_to_all | solution.py:112
  131.1 0.1 select_reduce_fusion.2
  131.2 0.0 copy-done.2
  131.2 19.3 %all-to-all-done.1 = bf16[16,224,128]{2,1,0:T(8,128)(2,1)S(1)} async-done(((bf16[16,224,128]{2,1,0:T(8,128)(2,1)}), bf16[16,224,128]{2,1,0:T(8,128)(2,1)S(1)}, u32[]{:S(2)}, u32[]{:S(2)}) %all-to-all-start.1) | async-done | bytes 917536 | tf_op jit(solution)/shard_map/all_to_all | solution.py:112
  150.5 0.0 all-gather.2.cloned.1.call-done
  150.5 6.4 %fusion.9 = (f32[224]{0:T(256)S(1)}, f32[224]{0:T(256)S(1)}, f32[224,3072]{1,0:T(8,128)S(1)}) fusion(bf16[2048,3072]{1,0:T(8,128)(2,1)} %all-gather.2.cloned.1.call-done, bf16[16,224,128]{2,1,0:T(8,128)(2,1)S(1)} %all-to-all-done.1), kind=kOutput, calls=%fused_computation.40 | convolution fusion | flops 2820636160 | bytes 16254720 | tf_op jit(solution)/shard_map/dot_general | solution.py:123
  156.9 0.0 copy-done
  156.9 0.0 copy-start.1
  156.9 0.7 fusion
  157.7 1.9 %collective-permute-start = (bf16[1,224,64]{1,2,0:T(8,128)(2,1)S(1)}, bf16[1,224,64]{1,2,0:T(8,128)(2,1)S(1)}, u32[]{:S(2)}, u32[]{:S(2)}) collective-permute-start(bf16[1,224,64]{1,2,0:T(8,128)(2,1)S(1)} %convert_bitcast_fusion), channel_id=1, source_target_pairs={{0,16},{16,0},{1,17},{17,1},{2,18},{18,2},{3,19},{19,3},{4,20},{20... | collective-permute-start | bytes 86024 | tf_op jit(solution)/shard_map/ppermute | solution.py:22
  160.2 0.6 select_reduce_fusion.5
  161.6 0.6 select_reduce_fusion.4
  163.0 0.0 collective-permute-done
  163.1 0.0 copy-done.1
  163.1 0.7 add_select_fusion
  (8 shorter events, 0.1 us)
Async XLA Ops:
  7.2 149.8 %copy-start = (bf16[3072,64]{0,1:T(8,128)(2,1)S(1)}, bf16[3072,64]{0,1:T(8,128)(2,1)}, u32[]{:S(2)}) copy-start(bf16[3072,64]{0,1:T(8,128)(2,1)} %param.13) | copy-start | bytes 1179652
  7.2 143.4 %all-gather.2.cloned.1.call-start = ((), (), s32[]{:S(2)}) async-start(), calls=%async_computation.2 | async-start | bytes 13369344 | tf_op jit(solution)/shard_map/all_gather | solution.py:125
  19.2 5.8 %copy-start.3 = (s32[1,16]{1,0:T(1,128)S(1)}, s32[1,16]{1,0:T(1,128)}, u32[]{:S(2)}) copy-start(s32[1,16]{1,0:T(1,128)} %param.9) | copy-start | bytes 196
  19.2 49.9 %all-to-all-start = ((bf16[16,224,3,128]{3,1,2,0:T(8,128)(2,1)}), bf16[16,224,3,128]{3,1,2,0:T(8,128)(2,1)S(1)}, u32[]{:S(2)}, u32[]{:S(2)}) async-start(bf16[16,224,3,128]{3,1,2,0:T(8,128)(2,1)} %copy.21), calls=%async_computation | async-start | bytes 5505024 | tf_op jit(solution)/shard_map/all_to_all | solution.py:105
  71.4 59.8 %copy-start.2 = (f32[1,2,3072]{2,1,0:T(2,128)S(1)}, f32[1,2,3072]{2,1,0:T(2,128)}, u32[]{:S(2)}) copy-start(f32[1,2,3072]{2,1,0:T(2,128)} %param.12) | copy-start | bytes 73732
  122.6 27.9 %all-to-all-start.1 = ((bf16[16,224,128]{2,1,0:T(8,128)(2,1)}), bf16[16,224,128]{2,1,0:T(8,128)(2,1)S(1)}, u32[]{:S(2)}, u32[]{:S(2)}) async-start(bf16[16,224,128]{2,1,0:T(8,128)(2,1)} %bitcast.4), calls=%async_computation.1 | async-start | bytes 1835008 | tf_op jit(solution)/shard_map/all_to_all | solution.py:112
  156.9 6.1 %copy-start.1 = (f32[1,224,32]{1,2,0:T(8,128)S(1)}, f32[1,224,32]{1,2,0:T(8,128)}, u32[]{:S(2)}) copy-start(f32[1,224,32]{1,2,0:T(8,128)} %param.14) | copy-start | bytes 86020
  157.7 5.4 %collective-permute-start = (bf16[1,224,64]{1,2,0:T(8,128)(2,1)S(1)}, bf16[1,224,64]{1,2,0:T(8,128)(2,1)S(1)}, u32[]{:S(2)}, u32[]{:S(2)}) collective-permute-start(bf16[1,224,64]{1,2,0:T(8,128)(2,1)S(1)} %convert_bitcast_fusion), channel_id=1, source_target_pairs={{0,16},{16,0},{1,17},{17,1},{2,18},{18,2},{3,19},{19,3},{4,20},{20... | collective-permute-start | bytes 86024 | tf_op jit(solution)/shard_map/ppermute | solution.py:22
Sparse Core Ops, SparseCore 0:
  14.7 129.4 all-gather.1

commit v2 on v1

--- a/solution.py
+++ b/solution.py
@@ -116,34 +116,43 @@
         concat_axis=0,
         tiled=True,
     )
-    returned = returned.transpose(1, 0, 2)
-    attn_rows = returned.reshape(item_count * capacity, attn_width)
-    first = lax.axis_index("cfg") == 0
-    columns = lax.all_gather(out_weight, "cfg", axis=1, tiled=True)
-    hidden = jnp.dot(
-        attn_rows,
-        lax.all_gather(columns, "seq", axis=0, tiled=True),
-        preferred_element_type=jnp.float32,
+    req_count = lax.axis_size("req")
+    cfg_index = lax.axis_index("cfg")
+    slab = out_weight.shape[0] // req_count
+    piece = lax.dynamic_slice_in_dim(out_weight, lax.axis_index("req") * slab, slab, 0)
+    piece = lax.all_gather(piece, "seq", axis=0, tiled=True)
+    weight_half = lax.all_gather(piece, "req", axis=0, tiled=True)
+    weight_half = weight_half.reshape(req_count, seq_count, slab, out_weight.shape[1])
+    partner_rows = partner_2(returned, "cfg", 0)
+    own_first = cfg_index == 0
+    both = jnp.stack(
+        [jnp.where(own_first, returned, partner_rows), jnp.where(own_first, partner_rows, returned)]
     )
-    hidden = hidden.reshape(item_count, capacity, D)
-    row_mean = jnp.mean(hidden, axis=2, keepdims=True)
-    spread = jnp.mean(hidden * hidden, axis=2, keepdims=True) - row_mean * row_mean
-    normed = modulate(
-        hidden, row_mean, spread, modulation[:, 0][:, None, :], modulation[:, 1][:, None, :]
+    both = both.reshape(2, seq_count, capacity, req_count, slab)
+    hidden = jnp.einsum(
+        "agsrj,rgjc->asc", both, weight_half, preferred_element_type=jnp.float32
     )
+    half_width = out_weight.shape[1]
+    column_start = cfg_index * half_width
+    sums = jnp.stack([jnp.sum(hidden, axis=2), jnp.sum(hidden * hidden, axis=2)])
+    sums = sums + partner_2(sums, "cfg", 0)
+    row_mean = (sums[0] / D)[:, :, None]
+    spread = (sums[1] / D)[:, :, None] - row_mean * row_mean
+    shift_part = lax.dynamic_slice_in_dim(modulation[0, 0], column_start, half_width, 0)
+    gain_part = lax.dynamic_slice_in_dim(modulation[0, 1], column_start, half_width, 0)
+    normed = modulate(hidden, row_mean, spread, shift_part, gain_part)
+    proj_half = lax.dynamic_slice_in_dim(proj_weight, column_start, half_width, 0)
     velocity = jnp.dot(
-        normed.reshape(item_count * capacity, D), proj_weight, preferred_element_type=jnp.float32
-    ).reshape(item_count, capacity, OUT_CH)
-    partner = partner_2(velocity.astype(jnp.bfloat16), "cfg", 0).astype(velocity.dtype)
-    conditional = jnp.where(first, velocity, partner)
-    unconditional = jnp.where(first, partner, velocity)
+        normed.reshape(2 * capacity, half_width), proj_half, preferred_element_type=jnp.float32
+    ).reshape(2, capacity, 2, OUT_CH // 2)
+    own_half = jnp.where(own_first, velocity[:, :, 0], velocity[:, :, 1])
+    other_half = jnp.where(own_first, velocity[:, :, 1], velocity[:, :, 0])
+    velocity = own_half + partner_2(other_half, "cfg", 0)
+    conditional = velocity[0][None]
+    unconditional = velocity[1][None]
     own_slots = lax.axis_index("seq") * capacity + jnp.arange(capacity, dtype=jnp.int32)
     unused_keys, video_slots = slot_masks(lengths, text_len, own_slots, capacity)
     video_mask = video_slots[:, :, None]
-    half_channels = latent.shape[2]
-    channel_start = lax.axis_index("cfg") * half_channels
-    conditional = lax.dynamic_slice_in_dim(conditional, channel_start, half_channels, 2)
-    unconditional = lax.dynamic_slice_in_dim(unconditional, channel_start, half_channels, 2)
     guided = jnp.where(video_mask, unconditional + guide_scale * (conditional - unconditional), 0.0)
     alpha_now, alpha_prev = plan(timestep)
     clean_part = jnp.sqrt(alpha_now) * latent - jnp.sqrt(1.0 - alpha_now) * guided

time: 171 us -> 175 us (1.023)
  waiting for transfers between devices: 62.9 us -> 42.7 us
  blocking collectives: 7.29 us -> 22.2 us
  starting transfers between devices: 15.6 us -> 20.8 us
  local copies, waits for them, and re-layouts: 7 us -> 9.78 us
    all_gather x1, blocking collectives: 7.29 us -> 22.2 us  [body(): piece = lax.all_gather(piece, 'seq', axis=0, tiled=True)]
    all_to_all x1, waiting for transfers between devices: 43.6 us -> 28.7 us  [body(): lax.all_to_all(outgoing, 'seq', split_axis=0, concat_axis=0, tiled=True)]
    all_to_all x1, waiting for transfers between devices: 19.3 us -> 11.1 us  [body(): lax.all_to_all(attended.reshape(seq_count, capacity, group_width), 'seq',...]
    ppermute x1 -> x3, starting transfers between devices: 1.91 us -> 7.43 us  [partner_2(): lax.ppermute(array, axis, [(i, i ^ 1 << bit) for i in range(lax.axis_size...]
    ppermute x1 -> x3, waiting for transfers between devices: 0.01 us -> 2.82 us  [partner_2(): lax.ppermute(array, axis, [(i, i ^ 1 << bit) for i in range(lax.axis_size...]
    select_n x0 -> x2, local copies, waits for them, and re-layouts: none -> 1.84 us  [the longest x1 1.33 us: body(): jnp.where(own_first, returned, partner_rows)]
  transfers between devices with their start and end apart: 4 -> 6, of which waited for: 2 -> 4; matrix products, arithmetic and copies ran while one was open for 5% -> 7% of each run, Pallas kernels for 30% -> 29%
where the time goes in v2:
time: 175 us; the launch traced here: 174 us
  Pallas kernels  51.2 us (29%)
  waiting for transfers between devices  42.7 us (24%)
  blocking collectives  22.2 us (13%)
  starting transfers between devices  20.8 us (12%)
  between operations  17.1 us (10%)
  local copies, waits for them, and re-layouts  9.78 us (6%)
  matrix products  6.63 us (4%)
  other arithmetic  3.96 us (2%)
    pallas_call x1, Pallas kernels, attention(): pl.pallas_call(attention_kernel, grid=(slot_count // block_rows,), in_spe...  51.2 us
    all_to_all x1, waiting for transfers between devices, body(): lax.all_to_all(outgoing, 'seq', split_axis=0, concat_axis=0, tiled=True)  28.7 us
    all_gather x1, blocking collectives, body(): piece = lax.all_gather(piece, 'seq', axis=0, tiled=True)  22.2 us
    all_to_all x1, waiting for transfers between devices, body(): lax.all_to_all(attended.reshape(seq_count, capacity, group_width), 'seq',...  11.1 us
    all_to_all x1, starting transfers between devices, body(): lax.all_to_all(attended.reshape(seq_count, capacity, group_width), 'seq',...  8.45 us
    ppermute x3, starting transfers between devices, partner_2(): lax.ppermute(array, axis, [(i, i ^ 1 << bit) for i in range(lax.axis_size...  7.43 us
    dot_general x1, matrix products, body(): jnp.einsum('agsrj,rgjc->asc', both, weight_half, preferred_element_type=j...  5.86 us
    all_to_all x1, starting transfers between devices, body(): lax.all_to_all(outgoing, 'seq', split_axis=0, concat_axis=0, tiled=True)  4.84 us
  transfers between devices with their start and end apart: 6, of which 4 were waited for; matrix products, arithmetic and copies ran while one was open for 7% of the time, Pallas kernels for 29%

profile of v2, /device:TPU:1, one launch (start us, length us, event | category | flops | bytes accessed | tf_op | source)
XLA Modules:
  0.0 174.4 jit_solution(12100106428158398239)
XLA Ops:
  7.2 0.0 copy-start
  7.2 0.0 all-gather.2.cloned.1.call-start
  7.2 0.8 constant_dynamic-slice_fusion
  8.1 22.2 %all_gather.6 = bf16[256,1536]{1,0:T(8,128)(2,1)} all-gather(bf16[16,1536]{1,0:T(8,128)(2,1)S(1)} %constant_dynamic-slice_fusion), channel_id=1, replica_groups=mesh['req'=8,'cfg'=2,'seq'=16] {'seq'}, dimensions={0}, use_global_device_ids=true | all-gather | bytes 835584 | tf_op jit(solution)/shard_map/all_gather | solution.py:123
  30.3 0.0 all-gather.2.cloned.1.call-update
  30.3 2.4 %copy.63 = bf16[28,8,48,128]{3,2,1,0:T(8,128)(2,1)S(1)} copy(bf16[28,8,48,128]{3,1,2,0:T(8,128)(2,1)} %bitcast.76) | data formatting | bytes 5505024
  32.7 2.3 %copy.45 = bf16[16,224,3,128]{3,1,2,0:T(8,128)(2,1)} copy(bf16[16,224,3,128]{3,0,2,1:T(8,128)(2,1)S(1)} %bitcast.75) | data formatting | bytes 5505024 | tf_op jit(solution)/shard_map/transpose | solution.py:104
  35.0 4.8 %all-to-all-start = ((bf16[16,224,3,128]{3,1,2,0:T(8,128)(2,1)}), bf16[16,224,3,128]{3,1,2,0:T(8,128)(2,1)S(1)}, u32[]{:S(2)}, u32[]{:S(2)}) async-start(bf16[16,224,3,128]{3,1,2,0:T(8,128)(2,1)} %copy.45), calls=%async_computation | async-start | bytes 5505024 | tf_op jit(solution)/shard_map/all_to_all | solution.py:105
  39.8 0.2 reduce_window_sum.12
  40.7 0.2 select_reduce_fusion.1
  40.9 0.1 and_select_fusion.bias_ref
  41.0 28.7 %all-to-all-done = bf16[16,224,3,128]{3,1,2,0:T(8,128)(2,1)S(1)} async-done(((bf16[16,224,3,128]{3,1,2,0:T(8,128)(2,1)}), bf16[16,224,3,128]{3,1,2,0:T(8,128)(2,1)S(1)}, u32[]{:S(2)}, u32[]{:S(2)}) %all-to-all-start) | async-done | bytes 2752544 | tf_op jit(solution)/shard_map/all_to_all | solution.py:105
  69.6 1.9 %copy.58 = bf16[16,224,3,128]{3,2,1,0:T(4,128)(2,1)S(1)} copy(bf16[16,224,3,128]{3,1,2,0:T(8,128)(2,1)S(1)} %all-to-all-done) | data formatting | bytes 5505024 | tf_op jit(solution)/shard_map/reshape | solution.py:106
  71.5 0.5 copy.72
  72.0 51.2 %shard_map.98 = bf16[3584,128]{1,0:T(8,128)(2,1)} custom-call(bf16[3584,384]{1,0:T(8,128)(2,1)S(1)} %bitcast.73, f32[1,3584]{1,0:T(1,128)S(1)} %and_select_fusion.bias_ref), custom_call_target="tpu_custom_call" | custom-call | tf_op jit(solution)/shard_map/pallas_call | solution.py:78
  123.2 8.5 %all-to-all-start.1 = ((bf16[16,224,128]{2,1,0:T(8,128)(2,1)}), bf16[16,224,128]{2,1,0:T(8,128)(2,1)S(1)}, u32[]{:S(2)}, u32[]{:S(2)}) async-start(bf16[16,224,128]{2,1,0:T(8,128)(2,1)} %bitcast.4), calls=%async_computation.1 | async-start | bytes 1835008 | tf_op jit(solution)/shard_map/all_to_all | solution.py:112
  131.7 11.1 %all-to-all-done.1 = bf16[16,224,128]{2,1,0:T(8,128)(2,1)S(1)} async-done(((bf16[16,224,128]{2,1,0:T(8,128)(2,1)}), bf16[16,224,128]{2,1,0:T(8,128)(2,1)S(1)}, u32[]{:S(2)}, u32[]{:S(2)}) %all-to-all-start.1) | async-done | bytes 917536 | tf_op jit(solution)/shard_map/all_to_all | solution.py:112
  142.9 6.5 %collective-permute-start = (bf16[16,224,128]{2,1,0:T(8,128)(2,1)S(1)}, bf16[16,224,128]{2,1,0:T(8,128)(2,1)}, u32[]{:S(2)}, u32[]{:S(2)}) collective-permute-start(bf16[16,224,128]{2,1,0:T(8,128)(2,1)S(1)} %all-to-all-done.1), channel_id=1, source_target_pairs={{0,16},{16,0},{1,17},{17,1},{2,18},{18,2},{3,19},{19,3},{4,20},{20... | collective-permute-start | bytes 2752520 | tf_op jit(solution)/shard_map/ppermute | solution.py:22
  149.5 2.1 %collective-permute-done = bf16[16,224,128]{2,1,0:T(8,128)(2,1)} collective-permute-done((bf16[16,224,128]{2,1,0:T(8,128)(2,1)S(1)}, bf16[16,224,128]{2,1,0:T(8,128)(2,1)}, u32[]{:S(2)}, u32[]{:S(2)}) %collective-permute-start) | collective-permute-done | bytes 917536 | tf_op jit(solution)/shard_map/ppermute | solution.py:22
  151.6 1.4 broadcast_select_fusion.1
  153.1 1.3 copy.48
  154.4 0.5 copy.49
  154.9 0.0 all-gather.2.cloned.1.call-done
  154.9 5.9 %fusion.27 = (f32[2,224]{1,0:T(2,128)S(1)}, f32[2,224]{1,0:T(2,128)S(1)}, f32[2,224,1536]{2,1,0:T(8,128)S(1)}) fusion(bf16[8,16,16,1536,1]{3,2,1,0,4:T(8,128)(2,1)} %bitcast.86, bf16[1,16,224,8,16]{2,4,3,0,1:T(8,128)(2,1)S(1)} %bitcast.78, bf16[1,16,224,8,16]{2,4,3,0,1:T(8,128)(2,1)} %bitcast.77), kind=kOutput, calls=%fused_computation.63 | convolution fusion | flops 2821553152 | bytes 10882560 | tf_op jit(solution)/shard_map/agsrj,rgjc->asc/dot_general | solution.py:132
  160.8 0.5 collective-permute-start.1
  161.3 0.1 select_reduce_fusion.2
  161.4 0.7 collective-permute-done.1
  162.1 0.8 fusion.8
  162.9 0.4 collective-permute-start.2
  164.0 0.6 select_reduce_fusion.5
  165.4 0.6 select_reduce_fusion.4
  166.9 0.6 add_select_fusion
  (21 shorter events, 0.2 us)
Async XLA Ops:
  7.2 142.3 %copy-start = (bf16[3072,64]{0,1:T(8,128)(2,1)S(1)}, bf16[3072,64]{0,1:T(8,128)(2,1)}, u32[]{:S(2)}) copy-start(bf16[3072,64]{0,1:T(8,128)(2,1)} %param.13) | copy-start | bytes 1179652
  7.2 147.7 %all-gather.2.cloned.1.call-start = ((), (), s32[]{:S(2)}) async-start(), calls=%async_computation.2 | async-start | bytes 7077888 | tf_op jit(solution)/shard_map/all_gather | solution.py:124
  35.0 4.9 %copy-start.3 = (s32[1,16]{1,0:T(1,128)S(1)}, s32[1,16]{1,0:T(1,128)}, u32[]{:S(2)}) copy-start(s32[1,16]{1,0:T(1,128)} %param.9) | copy-start | bytes 196
  35.0 34.7 %all-to-all-start = ((bf16[16,224,3,128]{3,1,2,0:T(8,128)(2,1)}), bf16[16,224,3,128]{3,1,2,0:T(8,128)(2,1)S(1)}, u32[]{:S(2)}, u32[]{:S(2)}) async-start(bf16[16,224,3,128]{3,1,2,0:T(8,128)(2,1)} %copy.45), calls=%async_computation | async-start | bytes 5505024 | tf_op jit(solution)/shard_map/all_to_all | solution.py:105
  72.0 77.4 %copy-start.2 = (f32[1,2,3072]{2,1,0:T(2,128)S(1)}, f32[1,2,3072]{2,1,0:T(2,128)}, u32[]{:S(2)}) copy-start(f32[1,2,3072]{2,1,0:T(2,128)} %param.12) | copy-start | bytes 73732
  123.2 19.6 %all-to-all-start.1 = ((bf16[16,224,128]{2,1,0:T(8,128)(2,1)}), bf16[16,224,128]{2,1,0:T(8,128)(2,1)S(1)}, u32[]{:S(2)}, u32[]{:S(2)}) async-start(bf16[16,224,128]{2,1,0:T(8,128)(2,1)} %bitcast.4), calls=%async_computation.1 | async-start | bytes 1835008 | tf_op jit(solution)/shard_map/all_to_all | solution.py:112
  142.9 8.8 %collective-permute-start = (bf16[16,224,128]{2,1,0:T(8,128)(2,1)S(1)}, bf16[16,224,128]{2,1,0:T(8,128)(2,1)}, u32[]{:S(2)}, u32[]{:S(2)}) collective-permute-start(bf16[16,224,128]{2,1,0:T(8,128)(2,1)S(1)} %all-to-all-done.1), channel_id=1, source_target_pairs={{0,16},{16,0},{1,17},{17,1},{2,18},{18,2},{3,19},{19,3},{4,20},{20... | collective-permute-start | bytes 2752520 | tf_op jit(solution)/shard_map/ppermute | solution.py:22
  160.8 1.3 collective-permute-start.1
  162.1 4.7 %copy-start.1 = (f32[1,224,32]{1,2,0:T(8,128)S(1)}, f32[1,224,32]{1,2,0:T(8,128)}, u32[]{:S(2)}) copy-start(f32[1,224,32]{1,2,0:T(8,128)} %param.14) | copy-start | bytes 86020
  162.9 3.9 %collective-permute-start.2 = (f32[2,224,32]{1,2,0:T(8,128)S(1)}, f32[2,224,32]{1,2,0:T(8,128)S(1)}, u32[]{:S(2)}, u32[]{:S(2)}) collective-permute-start(f32[2,224,32]{1,2,0:T(8,128)S(1)} %select_bitcast_fusion), channel_id=1, source_target_pairs={{0,16},{16,0},{1,17},{17,1},{2,18},{18,2},{3,19},{19,3},{4,20},{20... | collective-permute-start | bytes 172040 | tf_op jit(solution)/shard_map/ppermute | solution.py:22
Sparse Core Ops, SparseCore 0:
  30.4 80.3 all-gather.1

commit v3 on v2

--- a/solution.py
+++ b/solution.py
@@ -116,21 +116,18 @@
         concat_axis=0,
         tiled=True,
     )
-    req_count = lax.axis_size("req")
     cfg_index = lax.axis_index("cfg")
-    slab = out_weight.shape[0] // req_count
-    piece = lax.dynamic_slice_in_dim(out_weight, lax.axis_index("req") * slab, slab, 0)
-    piece = lax.all_gather(piece, "seq", axis=0, tiled=True)
-    weight_half = lax.all_gather(piece, "req", axis=0, tiled=True)
-    weight_half = weight_half.reshape(req_count, seq_count, slab, out_weight.shape[1])
+    weight_half = lax.all_gather(out_weight, "seq", axis=0, tiled=True)
     partner_rows = partner_2(returned, "cfg", 0)
     own_first = cfg_index == 0
     both = jnp.stack(
         [jnp.where(own_first, returned, partner_rows), jnp.where(own_first, partner_rows, returned)]
     )
-    both = both.reshape(2, seq_count, capacity, req_count, slab)
     hidden = jnp.einsum(
-        "agsrj,rgjc->asc", both, weight_half, preferred_element_type=jnp.float32
+        "agsj,gjc->asc",
+        both,
+        weight_half.reshape(seq_count, group_width, out_weight.shape[1]),
+        preferred_element_type=jnp.float32,
     )
     half_width = out_weight.shape[1]
     column_start = cfg_index * half_width

time: 175 us -> 159 us (0.909)
  blocking collectives: 22.2 us -> 0 us
  waiting for transfers between devices: 42.7 us -> 55.4 us
  local copies, waits for them, and re-layouts: 9.78 us -> 7.1 us
  starting transfers between devices: 20.8 us -> 18.5 us
    all_gather x1 -> x0, blocking collectives: 22.2 us -> none  [body(): piece = lax.all_gather(piece, 'seq', axis=0, tiled=True)]
    all_to_all x1, waiting for transfers between devices: 28.7 us -> 40.8 us  [body(): lax.all_to_all(outgoing, 'seq', split_axis=0, concat_axis=0, tiled=True)]
    all_to_all x1, starting transfers between devices: 8.45 us -> 4.44 us  [body(): lax.all_to_all(attended.reshape(seq_count, capacity, group_width), 'seq',...]
    all_to_all x1, starting transfers between devices: 4.84 us -> 7.7 us  [body(): lax.all_to_all(outgoing, 'seq', split_axis=0, concat_axis=0, tiled=True)]
    select_n x2 -> x0, local copies, waits for them, and re-layouts: 1.84 us -> none  [the longest x1 1.33 us: body(): jnp.where(own_first, returned, partner_rows)]
  transfers between devices with their start and end apart: 6 -> 6, of which waited for: 4 -> 4; matrix products, arithmetic and copies ran while one was open for 7% -> 6% of each run, Pallas kernels for 29% -> 32%
where the time goes in v3:
time: 159 us
  waiting for transfers between devices  55.4 us (35%)
  Pallas kernels  51.1 us (32%)
  starting transfers between devices  18.5 us (12%)
  between operations  17.1 us (11%)
  local copies, waits for them, and re-layouts  7.1 us (4%)
  matrix products  6.38 us (4%)
  other arithmetic  3.6 us (2%)
    pallas_call x1, Pallas kernels, attention(): pl.pallas_call(attention_kernel, grid=(slot_count // block_rows,), in_spe...  51.1 us
    all_to_all x1, waiting for transfers between devices, body(): lax.all_to_all(outgoing, 'seq', split_axis=0, concat_axis=0, tiled=True)  40.8 us
    all_to_all x1, waiting for transfers between devices, body(): lax.all_to_all(attended.reshape(seq_count, capacity, group_width), 'seq',...  11.2 us
    all_to_all x1, starting transfers between devices, body(): lax.all_to_all(outgoing, 'seq', split_axis=0, concat_axis=0, tiled=True)  7.7 us
    ppermute x3, starting transfers between devices, partner_2(): lax.ppermute(array, axis, [(i, i ^ 1 << bit) for i in range(lax.axis_size...  6.32 us
    dot_general x1, matrix products, body(): jnp.einsum('agsj,gjc->asc', both, weight_half.reshape(seq_count, group_wi...  5.61 us
    all_to_all x1, starting transfers between devices, body(): lax.all_to_all(attended.reshape(seq_count, capacity, group_width), 'seq',...  4.44 us
  transfers between devices with their start and end apart: 6, of which 4 were waited for; matrix products, arithmetic and copies ran while one was open for 6% of the time, Pallas kernels for 32%

profile of v3, /device:TPU:1, one launch (start us, length us, event | category | flops | bytes accessed | tf_op | source)
XLA Modules:
  0.0 159.2 jit_solution(2084942311901513693)
XLA Ops:
  7.2 0.0 copy-start
  7.2 0.0 all-gather.2.cloned.1.call-start
  7.2 0.7 all-gather.2.cloned.1.call-update
  7.9 2.4 %copy.46 = bf16[28,8,48,128]{3,2,1,0:T(8,128)(2,1)S(1)} copy(bf16[28,8,48,128]{3,1,2,0:T(8,128)(2,1)} %bitcast.78) | data formatting | bytes 5505024
  10.3 2.3 %copy.34 = bf16[16,224,3,128]{3,1,2,0:T(8,128)(2,1)} copy(bf16[16,224,3,128]{3,0,2,1:T(8,128)(2,1)S(1)} %bitcast.77) | data formatting | bytes 5505024 | tf_op jit(solution)/shard_map/transpose | solution.py:104
  12.6 7.7 %all-to-all-start = ((bf16[16,224,3,128]{3,1,2,0:T(8,128)(2,1)}), bf16[16,224,3,128]{3,1,2,0:T(8,128)(2,1)S(1)}, u32[]{:S(2)}, u32[]{:S(2)}) async-start(bf16[16,224,3,128]{3,1,2,0:T(8,128)(2,1)} %copy.34), calls=%async_computation | async-start | bytes 5505024 | tf_op jit(solution)/shard_map/all_to_all | solution.py:105
  20.9 0.0 copy-done.3
  21.0 0.2 reduce_window_sum.12
  21.2 0.2 select_reduce_fusion.1
  21.3 0.1 and_select_fusion.bias_ref
  21.4 40.8 %all-to-all-done = bf16[16,224,3,128]{3,1,2,0:T(8,128)(2,1)S(1)} async-done(((bf16[16,224,3,128]{3,1,2,0:T(8,128)(2,1)}), bf16[16,224,3,128]{3,1,2,0:T(8,128)(2,1)S(1)}, u32[]{:S(2)}, u32[]{:S(2)}) %all-to-all-start) | async-done | bytes 2752544 | tf_op jit(solution)/shard_map/all_to_all | solution.py:105
  62.2 1.9 %copy.43 = bf16[16,224,3,128]{3,2,1,0:T(4,128)(2,1)S(1)} copy(bf16[16,224,3,128]{3,1,2,0:T(8,128)(2,1)S(1)} %all-to-all-done) | data formatting | bytes 5505024 | tf_op jit(solution)/shard_map/reshape | solution.py:106
  64.1 0.5 copy.49
  64.6 0.0 copy-start.2
  64.6 51.1 %shard_map.98 = bf16[3584,128]{1,0:T(8,128)(2,1)} custom-call(bf16[3584,384]{1,0:T(8,128)(2,1)S(1)} %bitcast.75, f32[1,3584]{1,0:T(1,128)S(1)} %and_select_fusion.bias_ref), custom_call_target="tpu_custom_call" | custom-call | tf_op jit(solution)/shard_map/pallas_call | solution.py:78
  115.7 4.4 %all-to-all-start.1 = ((bf16[16,224,128]{2,1,0:T(8,128)(2,1)}), bf16[16,224,128]{2,1,0:T(8,128)(2,1)S(1)}, u32[]{:S(2)}, u32[]{:S(2)}) async-start(bf16[16,224,128]{2,1,0:T(8,128)(2,1)} %bitcast.4), calls=%async_computation.1 | async-start | bytes 1835008 | tf_op jit(solution)/shard_map/all_to_all | solution.py:112
  120.2 11.2 %all-to-all-done.1 = bf16[16,224,128]{2,1,0:T(8,128)(2,1)S(1)} async-done(((bf16[16,224,128]{2,1,0:T(8,128)(2,1)}), bf16[16,224,128]{2,1,0:T(8,128)(2,1)S(1)}, u32[]{:S(2)}, u32[]{:S(2)}) %all-to-all-start.1) | async-done | bytes 917536 | tf_op jit(solution)/shard_map/all_to_all | solution.py:112
  131.4 5.4 %collective-permute-start = (bf16[16,224,128]{2,1,0:T(8,128)(2,1)S(1)}, bf16[16,224,128]{2,1,0:T(8,128)(2,1)S(1)}, u32[]{:S(2)}, u32[]{:S(2)}) collective-permute-start(bf16[16,224,128]{2,1,0:T(8,128)(2,1)S(1)} %all-to-all-done.1), channel_id=1, source_target_pairs={{0,16},{16,0},{1,17},{17,1},{2,18},{18,2},{3,19},{19,3},{4,20},{20... | collective-permute-start | bytes 2752520 | tf_op jit(solution)/shard_map/ppermute | solution.py:22
  136.9 0.0 copy-done.2
  136.9 2.0 %collective-permute-done = bf16[16,224,128]{2,1,0:T(8,128)(2,1)S(1)} collective-permute-done((bf16[16,224,128]{2,1,0:T(8,128)(2,1)S(1)}, bf16[16,224,128]{2,1,0:T(8,128)(2,1)S(1)}, u32[]{:S(2)}, u32[]{:S(2)}) %collective-permute-start) | collective-permute-done | bytes 917536 | tf_op jit(solution)/shard_map/ppermute | solution.py:22
  138.9 1.1 select_bitcast_fusion.1
  140.0 5.6 %fusion.22 = (f32[2,224]{1,0:T(2,128)S(1)}, f32[2,224]{1,0:T(2,128)S(1)}, f32[2,224,1536]{2,1,0:T(8,128)S(1)}) fusion(bf16[16,128,1536,1]{2,1,0,3:T(8,128)(2,1)} %bitcast.86, bf16[1,16,224,128]{3,2,1,0:T(8,128)(2,1)} %get-tuple-element.11, bf16[1,16,224,128]{3,2,1,0:T(8,128)(2,1)S(1)} %get-tuple-element.10), kind=kOutput, calls=%fused_computation.60 | convolution fusion | flops 2821553152 | bytes 10882560 | tf_op jit(solution)/shard_map/agsj,gjc->asc/dot_general | solution.py:126
  145.6 0.5 collective-permute-start.1
  146.1 0.1 select_reduce_fusion.2
  146.2 0.7 collective-permute-done.1
  147.0 0.0 copy-start.1
  147.0 0.8 fusion.3
  147.8 0.4 collective-permute-start.2
  148.9 0.6 select_reduce_fusion.5
  150.2 0.6 select_reduce_fusion.4
  151.7 0.0 collective-permute-done.2
  151.7 0.6 add_select_fusion
  (17 shorter events, 0.2 us)
Async XLA Ops:
  7.2 129.7 %copy-start = (bf16[3072,64]{0,1:T(8,128)(2,1)S(1)}, bf16[3072,64]{0,1:T(8,128)(2,1)}, u32[]{:S(2)}) copy-start(bf16[3072,64]{0,1:T(8,128)(2,1)} %param.13) | copy-start | bytes 1179652
  7.2 132.8 %all-gather.2.cloned.1.call-start = ((), (), s32[]{:S(2)}) async-start(), calls=%async_computation.2 | async-start | bytes 6684672 | tf_op jit(solution)/shard_map/all_gather | solution.py:120
  12.6 8.4 %copy-start.3 = (s32[1,16]{1,0:T(1,128)S(1)}, s32[1,16]{1,0:T(1,128)}, u32[]{:S(2)}) copy-start(s32[1,16]{1,0:T(1,128)} %param.9) | copy-start | bytes 196
  12.6 49.7 %all-to-all-start = ((bf16[16,224,3,128]{3,1,2,0:T(8,128)(2,1)}), bf16[16,224,3,128]{3,1,2,0:T(8,128)(2,1)S(1)}, u32[]{:S(2)}, u32[]{:S(2)}) async-start(bf16[16,224,3,128]{3,1,2,0:T(8,128)(2,1)} %copy.34), calls=%async_computation | async-start | bytes 5505024 | tf_op jit(solution)/shard_map/all_to_all | solution.py:105
  64.6 72.3 %copy-start.2 = (f32[1,2,3072]{2,1,0:T(2,128)S(1)}, f32[1,2,3072]{2,1,0:T(2,128)}, u32[]{:S(2)}) copy-start(f32[1,2,3072]{2,1,0:T(2,128)} %param.12) | copy-start | bytes 73732
  115.7 15.7 %all-to-all-start.1 = ((bf16[16,224,128]{2,1,0:T(8,128)(2,1)}), bf16[16,224,128]{2,1,0:T(8,128)(2,1)S(1)}, u32[]{:S(2)}, u32[]{:S(2)}) async-start(bf16[16,224,128]{2,1,0:T(8,128)(2,1)} %bitcast.4), calls=%async_computation.1 | async-start | bytes 1835008 | tf_op jit(solution)/shard_map/all_to_all | solution.py:112
  131.4 7.5 %collective-permute-start = (bf16[16,224,128]{2,1,0:T(8,128)(2,1)S(1)}, bf16[16,224,128]{2,1,0:T(8,128)(2,1)S(1)}, u32[]{:S(2)}, u32[]{:S(2)}) collective-permute-start(bf16[16,224,128]{2,1,0:T(8,128)(2,1)S(1)} %all-to-all-done.1), channel_id=1, source_target_pairs={{0,16},{16,0},{1,17},{17,1},{2,18},{18,2},{3,19},{19,3},{4,20},{20... | collective-permute-start | bytes 2752520 | tf_op jit(solution)/shard_map/ppermute | solution.py:22
  145.6 1.3 collective-permute-start.1
  147.0 4.7 %copy-start.1 = (f32[1,224,32]{1,2,0:T(8,128)S(1)}, f32[1,224,32]{1,2,0:T(8,128)}, u32[]{:S(2)}) copy-start(f32[1,224,32]{1,2,0:T(8,128)} %param.14) | copy-start | bytes 86020
  147.8 3.9 %collective-permute-start.2 = (f32[2,224,32]{1,2,0:T(8,128)S(1)}, f32[2,224,32]{1,2,0:T(8,128)S(1)}, u32[]{:S(2)}, u32[]{:S(2)}) collective-permute-start(f32[2,224,32]{1,2,0:T(8,128)S(1)} %select_bitcast_fusion.2), channel_id=1, source_target_pairs={{0,16},{16,0},{1,17},{17,1},{2,18},{18,2},{3,19},{19,3},{4,20},{20... | collective-permute-start | bytes 172040 | tf_op jit(solution)/shard_map/ppermute | solution.py:22
Sparse Core Ops, SparseCore 0:
  10.5 93.2 all-gather.1

commit v4 on v3

--- a/solution.py
+++ b/solution.py
@@ -1,3 +1,4 @@
+import functools
 import math
 
 import jax
@@ -49,34 +50,55 @@
     return (alpha_now, alpha_prev)
 
 
-def attention_kernel(x_ref, bias_ref, o_ref):
+def attention_kernel(x_ref, bias_ref, o_ref, *, key_block):
     block = o_ref.shape[0]
+    slot_count = x_ref.shape[0]
     start = pl.multiple_of(pl.program_id(0) * block, block)
     query = x_ref[pl.ds(start, block), 0:128]
-    keyset = x_ref[:, 128:256]
-    values = x_ref[:, 256:384]
-    bias = bias_ref[...]
+    query = query * jnp.asarray(1.0 / math.sqrt(HEAD), query.dtype)
     lane = lax.broadcasted_iota(jnp.int32, query.shape, 1)
-    results = []
-    for head in range(2):
-        own = (lane >= HEAD) if head else (lane < HEAD)
-        masked = jnp.where(own, query, jnp.zeros_like(query))
-        scores = lax.dot_general(
-            masked, keyset, (((1,), (1,)), ((), ())), preferred_element_type=jnp.float32
+    zero = jnp.zeros_like(query)
+    per_head = (jnp.where(lane < HEAD, query, zero), jnp.where(lane >= HEAD, query, zero))
+
+    def step(index, carry):
+        first = pl.multiple_of(index * key_block, key_block)
+        keyset = x_ref[pl.ds(first, key_block), 128:256]
+        values = x_ref[pl.ds(first, key_block), 256:384]
+        bias = bias_ref[:, pl.ds(first, key_block)]
+        updated = []
+        for head in range(2):
+            row_top, total, acc = carry[head]
+            scores = lax.dot_general(
+                per_head[head], keyset, (((1,), (1,)), ((), ())),
+                preferred_element_type=jnp.float32,
+            ) + bias
+            new_top = jnp.maximum(row_top, jnp.max(scores, axis=1, keepdims=True))
+            decay = jnp.exp(row_top - new_top)
+            weights = jnp.exp(scores - new_top)
+            total = decay * total + jnp.sum(weights, axis=1, keepdims=True)
+            acc = decay * acc + jnp.dot(
+                weights.astype(jnp.bfloat16), values, preferred_element_type=jnp.float32
+            )
+            updated.append((new_top, total, acc))
+        return tuple(updated)
+
+    start_state = tuple(
+        (
+            jnp.full((block, 1), -jnp.inf, jnp.float32),
+            jnp.zeros((block, 1), jnp.float32),
+            jnp.zeros(query.shape, jnp.float32),
         )
-        scores = scores * (1.0 / math.sqrt(HEAD)) + bias
-        row_top = jnp.max(scores, axis=1, keepdims=True)
-        weights = jnp.exp(scores - row_top)
-        total = jnp.sum(weights, axis=1, keepdims=True)
-        probs = (weights * (1.0 / total)).astype(jnp.bfloat16)
-        results.append(jnp.dot(probs, values, preferred_element_type=jnp.float32))
+        for head in range(2)
+    )
+    final = lax.fori_loop(0, slot_count // key_block, step, start_state)
+    results = [acc / total for (row_top, total, acc) in final]
     o_ref[...] = jnp.where(lane < HEAD, results[0], results[1]).astype(o_ref.dtype)
 
 
-def attention(grouped, bias, block_rows=256):
+def attention(grouped, bias, block_rows=256, key_block=256, interpret=False):
     slot_count, width = grouped.shape
     return pl.pallas_call(
-        attention_kernel,
+        functools.partial(attention_kernel, key_block=key_block),
         grid=(slot_count // block_rows,),
         in_specs=[
             pl.BlockSpec((slot_count, width), lambda i: (0, 0)),
@@ -85,6 +107,7 @@
         out_specs=pl.BlockSpec((block_rows, width // 3), lambda i: (i, 0)),
         out_shape=jax.ShapeDtypeStruct((slot_count, width // 3), jnp.bfloat16),
         compiler_params=pltpu.CompilerParams(vmem_limit_bytes=48 * 1024 * 1024),
+        interpret=interpret,
     )(grouped, bias)
 
 
@@ -107,7 +130,7 @@
     key_slots, unused_video = slot_masks(
         lengths, text_len, jnp.arange(slot_count, dtype=jnp.int32), capacity
     )
-    bias = jnp.where(key_slots, 0.0, -jnp.inf).astype(jnp.float32)
+    bias = jnp.where(key_slots, 0.0, -1e30).astype(jnp.float32)
     attended = attention(grouped, bias)
     returned = lax.all_to_all(
         attended.reshape(seq_count, capacity, group_width),

time: 159 us -> 257 us (1.62)
  Pallas kernels: 51.1 us -> 149 us
    pallas_call x1, Pallas kernels: 51.1 us -> 149 us  [attention(): pl.pallas_call(functools.partial(attention_kernel, key_block=key_block),...]
  transfers between devices with their start and end apart: 6 -> 6, of which waited for: 4 -> 4; matrix products, arithmetic and copies ran while one was open for 6% -> 4% of each run, Pallas kernels for 32% -> 58%
where the time goes in v4:
time: 257 us
  Pallas kernels  149 us (58%)
  waiting for transfers between devices  55.4 us (22%)
  starting transfers between devices  18.4 us (7%)
  between operations  17.1 us (7%)
  local copies, waits for them, and re-layouts  7.1 us (3%)
  matrix products  6.38 us (2%)
  other arithmetic  3.6 us (1%)
    pallas_call x1, Pallas kernels, attention(): pl.pallas_call(functools.partial(attention_kernel, key_block=key_block),...  149 us
    all_to_all x1, waiting for transfers between devices, body(): lax.all_to_all(outgoing, 'seq', split_axis=0, concat_axis=0, tiled=True)  40.8 us
    all_to_all x1, waiting for transfers between devices, body(): lax.all_to_all(attended.reshape(seq_count, capacity, group_width), 'seq',...  11.2 us
    all_to_all x1, starting transfers between devices, body(): lax.all_to_all(outgoing, 'seq', split_axis=0, concat_axis=0, tiled=True)  7.7 us
    ppermute x3, starting transfers between devices, partner_2(): lax.ppermute(array, axis, [(i, i ^ 1 << bit) for i in range(lax.axis_size...  6.32 us
    dot_general x1, matrix products, body(): jnp.einsum('agsj,gjc->asc', both, weight_half.reshape(seq_count, group_wi...  5.61 us
  transfers between devices with their start and end apart: 6, of which 4 were waited for; matrix products, arithmetic and copies ran while one was open for 4% of the time, Pallas kernels for 58%

profile of v4, /device:TPU:1, one launch (start us, length us, event | category | flops | bytes accessed | tf_op | source)
XLA Modules:
  0.0 257.0 jit_solution(12531837281278457730)
XLA Ops:
  7.2 0.0 copy-start
  7.2 0.0 all-gather.2.cloned.1.call-start
  7.2 0.7 all-gather.2.cloned.1.call-update
  7.9 2.4 copy.46
  10.3 2.3 copy.34
  12.6 7.7 %all-to-all-start = ((bf16[16,224,3,128]{3,1,2,0:T(8,128)(2,1)}), bf16[16,224,3,128]{3,1,2,0:T(8,128)(2,1)S(1)}, u32[]{:S(2)}, u32[]{:S(2)}) async-start(bf16[16,224,3,128]{3,1,2,0:T(8,128)(2,1)} %copy.34), calls=%async_computation | async-start | bytes 5505024 | tf_op jit(solution)/shard_map/all_to_all | solution.py:128
  20.9 0.0 copy-done.3
  21.0 0.2 reduce_window_sum.12
  21.2 0.2 select_reduce_fusion.1
  21.3 0.1 and_select_fusion.bias_ref
  21.4 40.8 %all-to-all-done = bf16[16,224,3,128]{3,1,2,0:T(8,128)(2,1)S(1)} async-done(((bf16[16,224,3,128]{3,1,2,0:T(8,128)(2,1)}), bf16[16,224,3,128]{3,1,2,0:T(8,128)(2,1)S(1)}, u32[]{:S(2)}, u32[]{:S(2)}) %all-to-all-start) | async-done | bytes 2752544 | tf_op jit(solution)/shard_map/all_to_all | solution.py:128
  62.2 1.9 copy.43
  64.1 0.5 copy.49
  64.6 0.0 copy-start.2
  64.6 149.1 %shard_map.98 = bf16[3584,128]{1,0:T(8,128)(2,1)} custom-call(bf16[3584,384]{1,0:T(8,128)(2,1)S(1)} %bitcast.75, f32[1,3584]{1,0:T(1,128)S(1)} %and_select_fusion.bias_ref), custom_call_target="tpu_custom_call" | custom-call | tf_op jit(solution)/shard_map/pallas_call | solution.py:100
  213.7 4.3 %all-to-all-start.1 = ((bf16[16,224,128]{2,1,0:T(8,128)(2,1)}), bf16[16,224,128]{2,1,0:T(8,128)(2,1)S(1)}, u32[]{:S(2)}, u32[]{:S(2)}) async-start(bf16[16,224,128]{2,1,0:T(8,128)(2,1)} %bitcast.4), calls=%async_computation.1 | async-start | bytes 1835008 | tf_op jit(solution)/shard_map/all_to_all | solution.py:135
  218.0 11.2 %all-to-all-done.1 = bf16[16,224,128]{2,1,0:T(8,128)(2,1)S(1)} async-done(((bf16[16,224,128]{2,1,0:T(8,128)(2,1)}), bf16[16,224,128]{2,1,0:T(8,128)(2,1)S(1)}, u32[]{:S(2)}, u32[]{:S(2)}) %all-to-all-start.1) | async-done | bytes 917536 | tf_op jit(solution)/shard_map/all_to_all | solution.py:135
  229.3 5.4 %collective-permute-start = (bf16[16,224,128]{2,1,0:T(8,128)(2,1)S(1)}, bf16[16,224,128]{2,1,0:T(8,128)(2,1)S(1)}, u32[]{:S(2)}, u32[]{:S(2)}) collective-permute-start(bf16[16,224,128]{2,1,0:T(8,128)(2,1)S(1)} %all-to-all-done.1), channel_id=1, source_target_pairs={{0,16},{16,0},{1,17},{17,1},{2,18},{18,2},{3,19},{19,3},{4,20},{20... | collective-permute-start | bytes 2752520 | tf_op jit(solution)/shard_map/ppermute | solution.py:23
  234.7 0.0 copy-done
  234.8 2.0 collective-permute-done
  236.8 1.1 select_bitcast_fusion.1
  237.9 5.6 %fusion.22 = (f32[2,224]{1,0:T(2,128)S(1)}, f32[2,224]{1,0:T(2,128)S(1)}, f32[2,224,1536]{2,1,0:T(8,128)S(1)}) fusion(bf16[16,128,1536,1]{2,1,0,3:T(8,128)(2,1)} %bitcast.86, bf16[1,16,224,128]{3,2,1,0:T(8,128)(2,1)} %get-tuple-element.11, bf16[1,16,224,128]{3,2,1,0:T(8,128)(2,1)S(1)} %get-tuple-element.10), kind=kOutput, calls=%fused_computation.60 | convolution fusion | flops 2821553152 | bytes 10882560 | tf_op jit(solution)/shard_map/agsj,gjc->asc/dot_general | solution.py:149
  243.5 0.5 collective-permute-start.1
  244.0 0.1 select_reduce_fusion.2
  244.1 0.7 collective-permute-done.1
  244.8 0.0 copy-start.1
  244.8 0.8 fusion.3
  245.6 0.4 collective-permute-start.2
  246.7 0.6 select_reduce_fusion.5
  248.1 0.6 select_reduce_fusion.4
  249.5 0.0 collective-permute-done.2
  249.6 0.6 add_select_fusion
  (17 shorter events, 0.2 us)
Async XLA Ops:
  7.2 227.6 %copy-start = (bf16[3072,64]{0,1:T(8,128)(2,1)S(1)}, bf16[3072,64]{0,1:T(8,128)(2,1)}, u32[]{:S(2)}) copy-start(bf16[3072,64]{0,1:T(8,128)(2,1)} %param.13) | copy-start | bytes 1179652
  7.2 230.7 %all-gather.2.cloned.1.call-start = ((), (), s32[]{:S(2)}) async-start(), calls=%async_computation.2 | async-start | bytes 6684672 | tf_op jit(solution)/shard_map/all_gather | solution.py:143
  12.6 8.4 %copy-start.3 = (s32[1,16]{1,0:T(1,128)S(1)}, s32[1,16]{1,0:T(1,128)}, u32[]{:S(2)}) copy-start(s32[1,16]{1,0:T(1,128)} %param.9) | copy-start | bytes 196
  12.6 49.7 %all-to-all-start = ((bf16[16,224,3,128]{3,1,2,0:T(8,128)(2,1)}), bf16[16,224,3,128]{3,1,2,0:T(8,128)(2,1)S(1)}, u32[]{:S(2)}, u32[]{:S(2)}) async-start(bf16[16,224,3,128]{3,1,2,0:T(8,128)(2,1)} %copy.34), calls=%async_computation | async-start | bytes 5505024 | tf_op jit(solution)/shard_map/all_to_all | solution.py:128
  64.6 170.1 %copy-start.2 = (f32[1,2,3072]{2,1,0:T(2,128)S(1)}, f32[1,2,3072]{2,1,0:T(2,128)}, u32[]{:S(2)}) copy-start(f32[1,2,3072]{2,1,0:T(2,128)} %param.12) | copy-start | bytes 73732
  213.7 15.6 %all-to-all-start.1 = ((bf16[16,224,128]{2,1,0:T(8,128)(2,1)}), bf16[16,224,128]{2,1,0:T(8,128)(2,1)S(1)}, u32[]{:S(2)}, u32[]{:S(2)}) async-start(bf16[16,224,128]{2,1,0:T(8,128)(2,1)} %bitcast.4), calls=%async_computation.1 | async-start | bytes 1835008 | tf_op jit(solution)/shard_map/all_to_all | solution.py:135
  229.3 7.5 %collective-permute-start = (bf16[16,224,128]{2,1,0:T(8,128)(2,1)S(1)}, bf16[16,224,128]{2,1,0:T(8,128)(2,1)S(1)}, u32[]{:S(2)}, u32[]{:S(2)}) collective-permute-start(bf16[16,224,128]{2,1,0:T(8,128)(2,1)S(1)} %all-to-all-done.1), channel_id=1, source_target_pairs={{0,16},{16,0},{1,17},{17,1},{2,18},{18,2},{3,19},{19,3},{4,20},{20... | collective-permute-start | bytes 2752520 | tf_op jit(solution)/shard_map/ppermute | solution.py:23
  243.5 1.3 collective-permute-start.1
  244.8 4.7 %copy-start.1 = (f32[1,224,32]{1,2,0:T(8,128)S(1)}, f32[1,224,32]{1,2,0:T(8,128)}, u32[]{:S(2)}) copy-start(f32[1,224,32]{1,2,0:T(8,128)} %param.14) | copy-start | bytes 86020
  245.6 3.9 %collective-permute-start.2 = (f32[2,224,32]{1,2,0:T(8,128)S(1)}, f32[2,224,32]{1,2,0:T(8,128)S(1)}, u32[]{:S(2)}, u32[]{:S(2)}) collective-permute-start(f32[2,224,32]{1,2,0:T(8,128)S(1)} %select_bitcast_fusion.2), channel_id=1, source_target_pairs={{0,16},{16,0},{1,17},{17,1},{2,18},{18,2},{3,19},{19,3},{4,20},{20... | collective-permute-start | bytes 172040 | tf_op jit(solution)/shard_map/ppermute | solution.py:23
Sparse Core Ops, SparseCore 0:
  10.5 93.2 all-gather.1

commit v5 on v3

--- a/solution.py
+++ b/solution.py
@@ -49,43 +49,70 @@
     return (alpha_now, alpha_prev)
 
 
-def attention_kernel(x_ref, bias_ref, o_ref):
+def attention_kernel(x_ref, swapped_ref, even_ref, odd_ref, o_ref):
     block = o_ref.shape[0]
     start = pl.multiple_of(pl.program_id(0) * block, block)
     query = x_ref[pl.ds(start, block), 0:128]
+    swapped_query = swapped_ref[pl.ds(start, block), 0:128]
     keyset = x_ref[:, 128:256]
     values = x_ref[:, 256:384]
-    bias = bias_ref[...]
-    lane = lax.broadcasted_iota(jnp.int32, query.shape, 1)
-    results = []
-    for head in range(2):
-        own = (lane >= HEAD) if head else (lane < HEAD)
-        masked = jnp.where(own, query, jnp.zeros_like(query))
-        scores = lax.dot_general(
-            masked, keyset, (((1,), (1,)), ((), ())), preferred_element_type=jnp.float32
-        )
-        scores = scores * (1.0 / math.sqrt(HEAD)) + bias
-        row_top = jnp.max(scores, axis=1, keepdims=True)
-        weights = jnp.exp(scores - row_top)
-        total = jnp.sum(weights, axis=1, keepdims=True)
-        probs = (weights * (1.0 / total)).astype(jnp.bfloat16)
-        results.append(jnp.dot(probs, values, preferred_element_type=jnp.float32))
-    o_ref[...] = jnp.where(lane < HEAD, results[0], results[1]).astype(o_ref.dtype)
-
-
-def attention(grouped, bias, block_rows=256):
-    slot_count, width = grouped.shape
+    swapped_values = swapped_ref[:, 128:256]
+    low = lax.broadcasted_iota(jnp.int32, query.shape, 1) < HEAD
+    zero = jnp.zeros_like(query)
+    biases = (even_ref[...], odd_ref[...])
+
+    def one_group(to_even, to_odd, first_values, second_values):
+        scores = [
+            lax.dot_general(
+                side, keyset, (((1,), (1,)), ((), ())), preferred_element_type=jnp.float32
+            )
+            * (1.0 / math.sqrt(HEAD))
+            + bias
+            for side, bias in zip((to_even, to_odd), biases)
+        ]
+        row_top = jnp.maximum(
+            jnp.max(scores[0], axis=1, keepdims=True), jnp.max(scores[1], axis=1, keepdims=True)
+        )
+        weights = [jnp.exp(part - row_top) for part in scores]
+        total = jnp.sum(weights[0], axis=1, keepdims=True) + jnp.sum(
+            weights[1], axis=1, keepdims=True
+        )
+        scale = 1.0 / total
+        probs = [(part * scale).astype(jnp.bfloat16) for part in weights]
+        return jnp.dot(probs[0], first_values, preferred_element_type=jnp.float32) + jnp.dot(
+            probs[1], second_values, preferred_element_type=jnp.float32
+        )
+
+    even_rows = one_group(
+        jnp.where(low, query, zero), jnp.where(low, zero, swapped_query), values, swapped_values
+    )
+    odd_rows = one_group(
+        jnp.where(low, swapped_query, zero), jnp.where(low, zero, query), swapped_values, values
+    )
+    o_ref[...] = jnp.where(low, even_rows, odd_rows).astype(o_ref.dtype)
+
+
+def attention(packed, even_bias, odd_bias, block_rows=128, interpret=False):
+    rows, width = packed.shape
+    lanes = width // 3
+    swapped = jnp.concatenate(
+        [jnp.roll(packed[:, :lanes], HEAD, axis=1), jnp.roll(packed[:, 2 * lanes :], HEAD, axis=1)],
+        axis=1,
+    )
     return pl.pallas_call(
         attention_kernel,
-        grid=(slot_count // block_rows,),
+        grid=(rows // block_rows,),
         in_specs=[
-            pl.BlockSpec((slot_count, width), lambda i: (0, 0)),
-            pl.BlockSpec((1, slot_count), lambda i: (0, 0)),
+            pl.BlockSpec((rows, width), lambda i: (0, 0)),
+            pl.BlockSpec((rows, 2 * lanes), lambda i: (0, 0)),
+            pl.BlockSpec((1, rows), lambda i: (0, 0)),
+            pl.BlockSpec((1, rows), lambda i: (0, 0)),
         ],
-        out_specs=pl.BlockSpec((block_rows, width // 3), lambda i: (i, 0)),
-        out_shape=jax.ShapeDtypeStruct((slot_count, width // 3), jnp.bfloat16),
+        out_specs=pl.BlockSpec((block_rows, lanes), lambda i: (i, 0)),
+        out_shape=jax.ShapeDtypeStruct((rows, lanes), jnp.bfloat16),
         compiler_params=pltpu.CompilerParams(vmem_limit_bytes=48 * 1024 * 1024),
-    )(grouped, bias)
+        interpret=interpret,
+    )(packed, swapped, even_bias, odd_bias)
 
 
 def modulate(hidden, row_mean, spread, shift_part, gain_part):
@@ -100,22 +127,34 @@
     attn_width = projected.shape[3] // 3
     group_width = attn_width // seq_count
     slot_count = capacity * seq_count
-    outgoing = projected[0, 0].reshape(capacity, 3, seq_count, group_width)
-    outgoing = outgoing.transpose(2, 0, 1, 3)
-    arrived = lax.all_to_all(outgoing, "seq", split_axis=0, concat_axis=0, tiled=True)
-    grouped = arrived.reshape(slot_count, 3 * group_width)
+    half_cap = capacity // 2
+    heads_here = group_width // HEAD
+    outgoing = projected[0, 0].reshape(half_cap, 2, 3, seq_count, heads_here, HEAD)
+    outgoing = outgoing.transpose(4, 3, 0, 2, 1, 5).reshape(
+        heads_here, seq_count, half_cap, 3 * 2 * HEAD
+    )
     key_slots, unused_video = slot_masks(
         lengths, text_len, jnp.arange(slot_count, dtype=jnp.int32), capacity
     )
     bias = jnp.where(key_slots, 0.0, -jnp.inf).astype(jnp.float32)
-    attended = attention(grouped, bias)
-    returned = lax.all_to_all(
-        attended.reshape(seq_count, capacity, group_width),
-        "seq",
-        split_axis=0,
-        concat_axis=0,
-        tiled=True,
-    )
+    bias = bias.reshape(seq_count * half_cap, 2)
+    even_bias = bias[:, 0].reshape(1, -1)
+    odd_bias = bias[:, 1].reshape(1, -1)
+    pieces = []
+    for head in range(heads_here):
+        arrived = lax.all_to_all(outgoing[head], "seq", split_axis=0, concat_axis=0, tiled=True)
+        attended = attention(arrived.reshape(seq_count * half_cap, 3 * 2 * HEAD), even_bias, odd_bias)
+        pieces.append(
+            lax.all_to_all(
+                attended.reshape(seq_count, half_cap, 2 * HEAD),
+                "seq",
+                split_axis=0,
+                concat_axis=0,
+                tiled=True,
+            )
+        )
+    returned = jnp.stack(pieces).reshape(heads_here, seq_count, half_cap, 2, HEAD)
+    returned = returned.transpose(1, 2, 3, 0, 4).reshape(seq_count, capacity, group_width)
     cfg_index = lax.axis_index("cfg")
     weight_half = lax.all_gather(out_weight, "seq", axis=0, tiled=True)
     partner_rows = partner_2(returned, "cfg", 0)

time: 159 us -> 208 us (1.31)
  local copies, waits for them, and re-layouts: 7.1 us -> 55.6 us
  waiting for transfers between devices: 55.4 us -> 22.9 us
  starting transfers between devices: 18.5 us -> 37 us
  Pallas kernels: 51.1 us -> 60.5 us
  other arithmetic: 3.6 us -> 7.23 us
    slice x0 -> x6, local copies, waits for them, and re-layouts: none -> 35 us  [the longest x3 33.4 us: body(): outgoing[head]]
    all_to_all x2 -> x4, waiting for transfers between devices: 52.1 us -> 19.6 us  [the longest x2 11.2 us: body(): lax.all_to_all(outgoing[head], 'seq', split_axis=0, concat_axis=0, tiled=...]
    all_to_all x2 -> x4, starting transfers between devices: 12.1 us -> 29.1 us  [the longest x2 15.8 us: body(): lax.all_to_all(outgoing[head], 'seq', split_axis=0, concat_axis=0, tiled=...]
    pallas_call x1 -> x2, Pallas kernels: 51.1 us -> 60.5 us  [attention(): pl.pallas_call(attention_kernel, grid=(rows // block_rows,), in_specs=[pl...]
    another operation x0 -> x3, local copies, waits for them, and re-layouts: none -> 8.77 us  [the longest x1 8.75 us: body(): projected[0, 0].reshape(half_cap, 2, 3, seq_count, heads_here, HEAD)]
    reduce_sum x0 -> x2, local copies, waits for them, and re-layouts: none -> 3.64 us  [the longest x1 1.84 us: slot_masks(): piece_len = jnp.sum(lengths[:, :, None] * select[None], axis=1)]
    squeeze x0 -> x2, local copies, waits for them, and re-layouts: none -> 3.08 us  [body(): outgoing[head]]
    select_n x1, other arithmetic: 0.08 us -> 2.27 us  [body(): bias = jnp.where(key_slots, 0.0, -jnp.inf).astype(jnp.float32)]
  transfers between devices with their start and end apart: 6 -> 8, of which waited for: 4 -> 4; matrix products, arithmetic and copies ran while one was open for 6% -> 30% of each run, Pallas kernels for 32% -> 29%
where the time goes in v5:
time: 208 us; the launch traced here: 207 us
  Pallas kernels  60.5 us (29%)
  local copies, waits for them, and re-layouts  55.6 us (27%)
  starting transfers between devices  37 us (18%)
  waiting for transfers between devices  22.9 us (11%)
  between operations  17.2 us (8%)
  other arithmetic  7.23 us (3%)
  matrix products  6.37 us (3%)
    pallas_call x2, Pallas kernels, attention(): pl.pallas_call(attention_kernel, grid=(rows // block_rows,), in_specs=[pl...  60.5 us
    slice x3, local copies, waits for them, and re-layouts, body(): outgoing[head]  33.4 us
    all_to_all x2, starting transfers between devices, body(): lax.all_to_all(outgoing[head], 'seq', split_axis=0, concat_axis=0, tiled=...  15.8 us
    all_to_all x2, starting transfers between devices, body(): lax.all_to_all(attended.reshape(seq_count, half_cap, 2 * HEAD), 'seq', sp...  13.3 us
    all_to_all x2, waiting for transfers between devices, body(): lax.all_to_all(outgoing[head], 'seq', split_axis=0, concat_axis=0, tiled=...  11.2 us
    another operation x1, local copies, waits for them, and re-layouts, body(): projected[0, 0].reshape(half_cap, 2, 3, seq_count, heads_here, HEAD)  8.75 us
    all_to_all x2, waiting for transfers between devices, body(): lax.all_to_all(attended.reshape(seq_count, half_cap, 2 * HEAD), 'seq', sp...  8.3 us
    ppermute x3, starting transfers between devices, partner_2(): lax.ppermute(array, axis, [(i, i ^ 1 << bit) for i in range(lax.axis_size...  7.89 us
  transfers between devices with their start and end apart: 8, of which 4 were waited for; matrix products, arithmetic and copies ran while one was open for 30% of the time, Pallas kernels for 29%

profile of v5, /device:TPU:1, one launch (start us, length us, event | category | flops | bytes accessed | tf_op | source)
XLA Modules:
  0.0 206.9 jit_solution(5174168141132282168)
XLA Ops:
  7.2 0.7 all-gather.2.cloned.1.call-update
  7.9 8.8 %reshape_squeeze.9 = bf16[112,2,3,16,2,64]{5,4,3,2,1,0:T(2,128)(2,1)} reshape(bf16[1,1,224,6144]{3,2,1,0:T(8,128)(2,1)} %param.8) | data formatting | bytes 5505024 | tf_op jit(solution)/shard_map/reshape;squeeze | solution.py:132
  16.7 14.3 %fusion.32 = (bf16[1,16,112,3,2,64]{5,0,1,3,4,2:T(2,128)(2,1)}, bf16[1,16,112,3,2,64]{5,0,1,3,4,2:T(2,128)(2,1)}) fusion(bf16[2,16,112,3,2,64]{5,0,1,3,4,2:T(2,128)(2,1)} %bitcast.80), kind=kLoop, calls=%fused_computation.73 | loop fusion | bytes 5505024 | tf_op jit(solution)/shard_map/slice | solution.py:145
  30.9 9.6 %copy.40 = bf16[1,16,112,3,2,64]{2,5,4,3,1,0:T(8,128)(2,1)S(1)} copy(bf16[1,16,112,3,2,64]{5,0,1,3,4,2:T(2,128)(2,1)} %get-tuple-element.12) | data formatting | bytes 2752512 | tf_op jit(solution)/shard_map/slice | solution.py:145
  40.5 1.6 copy.41
  42.1 7.7 %all-to-all-start = ((bf16[16,112,384]{2,1,0:T(8,128)(2,1)}), bf16[16,112,384]{2,1,0:T(8,128)(2,1)S(1)}, u32[]{:S(2)}, u32[]{:S(2)}) async-start(bf16[16,112,384]{2,1,0:T(8,128)(2,1)} %copy.41), calls=%async_computation | async-start | bytes 2752512 | tf_op jit(solution)/shard_map/all_to_all | solution.py:145
  50.1 1.8 reduce_sum.79
  52.0 1.8 reduce_sum.81
  54.4 9.6 %copy.43 = bf16[1,16,112,3,2,64]{2,5,4,3,1,0:T(8,128)(2,1)S(1)} copy(bf16[1,16,112,3,2,64]{5,0,1,3,4,2:T(2,128)(2,1)} %get-tuple-element.13) | data formatting | bytes 2752512 | tf_op jit(solution)/shard_map/slice | solution.py:145
  64.0 1.5 copy.44
  65.5 11.2 %all-to-all-done = bf16[16,112,384]{2,1,0:T(8,128)(2,1)S(1)} async-done(((bf16[16,112,384]{2,1,0:T(8,128)(2,1)}), bf16[16,112,384]{2,1,0:T(8,128)(2,1)S(1)}, u32[]{:S(2)}, u32[]{:S(2)}) %all-to-all-start) | async-done | bytes 1376288 | tf_op jit(solution)/shard_map/all_to_all | solution.py:145
  76.8 8.1 %all-to-all-start.2 = ((bf16[16,112,384]{2,1,0:T(8,128)(2,1)}), bf16[16,112,384]{2,1,0:T(8,128)(2,1)S(1)}, u32[]{:S(2)}, u32[]{:S(2)}) async-start(bf16[16,112,384]{2,1,0:T(8,128)(2,1)} %copy.44), calls=%async_computation.2 | async-start | bytes 2752512 | tf_op jit(solution)/shard_map/all_to_all | solution.py:145
  84.9 2.3 %fusion.11 = f32[1792,2]{1,0:T(8,128)S(1)} fusion(s32[1792,2]{1,0:T(8,128)} %reduce_sum.79, s32[1792,2]{1,0:T(8,128)} %reduce_sum.81, s32[]{:T(128)} %bitcast.72), kind=kLoop, calls=%fused_computation.23 | loop fusion | flops 53760 | bytes 43012 | tf_op jit(solution)/shard_map/jit(_where)/select_n | solution.py:139
  87.1 0.8 slice_reduce_fusion
  88.4 0.6 pad_maximum_fusion.swapped_ref
  89.0 30.0 %shard_map.98 = bf16[1792,128]{1,0:T(8,128)(2,1)S(1)} custom-call(bf16[1792,384]{1,0:T(8,128)(2,1)S(1)} %bitcast.76, bf16[1792,256]{1,0:T(8,128)(2,1)S(1)} %pad_maximum_fusion.swapped_ref, f32[1,1792]{1,0:T(1,128)S(1)} %reshape_squeeze.10.even_ref, f32[1,1792]{1,0:T(1,128)S(1)} %reshape_squeeze.11.odd_ref), custom_call_target="tpu_custom_call" | custom-call | tf_op jit(solution)/shard_map/pallas_call | solution.py:102
  119.0 0.8 copy-done.1
  119.8 6.7 %all-to-all-start.1 = ((bf16[16,112,128]{2,1,0:T(8,128)(2,1)}), bf16[16,112,128]{2,1,0:T(8,128)(2,1)S(1)}, u32[]{:S(2)}, u32[]{:S(2)}) async-start(bf16[16,112,128]{2,1,0:T(8,128)(2,1)} %bitcast.79), calls=%async_computation.1 | async-start | bytes 917504 | tf_op jit(solution)/shard_map/all_to_all | solution.py:148
  127.5 30.6 %shard_map.99 = bf16[1792,128]{1,0:T(8,128)(2,1)} custom-call(bf16[1792,384]{1,0:T(8,128)(2,1)S(1)} %bitcast.78, bf16[1792,256]{1,0:T(8,128)(2,1)S(1)} %pad_maximum_fusion.1.swapped_ref, f32[1,1792]{1,0:T(1,128)S(1)} %reshape_squeeze.10.even_ref, f32[1,1792]{1,0:T(1,128)S(1)} %reshape_squeeze.11.odd_ref), custom_call_target="tpu_custom_call" | custom-call | tf_op jit(solution)/shard_map/pallas_call | solution.py:102
  158.1 6.7 %all-to-all-start.3 = ((bf16[16,112,128]{2,1,0:T(8,128)(2,1)}), bf16[16,112,128]{2,1,0:T(8,128)(2,1)S(1)}, u32[]{:S(2)}, u32[]{:S(2)}) async-start(bf16[16,112,128]{2,1,0:T(8,128)(2,1)} %bitcast.10), calls=%async_computation.3 | async-start | bytes 917504 | tf_op jit(solution)/shard_map/all_to_all | solution.py:148
  165.0 8.3 %all-to-all-done.3 = bf16[16,112,128]{2,1,0:T(8,128)(2,1)S(1)} async-done(((bf16[16,112,128]{2,1,0:T(8,128)(2,1)}), bf16[16,112,128]{2,1,0:T(8,128)(2,1)S(1)}, u32[]{:S(2)}, u32[]{:S(2)}) %all-to-all-start.3) | async-done | bytes 458784 | tf_op jit(solution)/shard_map/all_to_all | solution.py:148
  173.8 2.9 %copy.46 = bf16[16,112,2,2,64]{4,3,2,1,0:T(2,128)(2,1)S(1)} copy(bf16[16,112,2,2,64]{1,4,2,0,3:T(8,128)(2,1)S(1)} %maximum_bitcast_fusion) | data formatting | bytes 1835008 | tf_op jit(solution)/shard_map/transpose | solution.py:157
  176.7 0.8 reshape.378
  177.6 7.0 %collective-permute-start = (bf16[16,224,128]{2,1,0:T(8,128)(2,1)S(1)}, bf16[16,224,128]{2,1,0:T(8,128)(2,1)S(1)}, u32[]{:S(2)}, u32[]{:S(2)}) collective-permute-start(bf16[16,224,128]{2,1,0:T(8,128)(2,1)S(1)} %reshape.378), channel_id=1, source_target_pairs={{0,16},{16,0},{1,17},{17,1},{2,18},{18,2},{3,19},{19,3},{4,20},{20... | collective-permute-start | bytes 2752520 | tf_op jit(solution)/shard_map/ppermute | solution.py:22
  184.7 2.0 collective-permute-done
  186.7 1.1 select_bitcast_fusion.1
  187.7 5.6 %fusion.30 = (f32[2,224]{1,0:T(2,128)S(1)}, f32[2,224]{1,0:T(2,128)S(1)}, f32[2,224,1536]{2,1,0:T(8,128)S(1)}) fusion(bf16[16,128,1536,1]{2,1,0,3:T(8,128)(2,1)} %bitcast.92, bf16[1,16,224,128]{3,2,1,0:T(8,128)(2,1)} %get-tuple-element.15, bf16[1,16,224,128]{3,2,1,0:T(8,128)(2,1)S(1)} %get-tuple-element.14), kind=kOutput, calls=%fused_computation.72 | convolution fusion | flops 2821553152 | bytes 10882560 | tf_op jit(solution)/shard_map/agsj,gjc->asc/dot_general | solution.py:165
  193.9 0.7 collective-permute-done.1
  194.7 0.8 fusion.3
  196.6 0.6 select_reduce_fusion.5
  197.9 0.6 select_reduce_fusion.4
  199.4 0.6 add_select_fusion.1
  (40 shorter events, 3.8 us)
Async XLA Ops:
  7.2 177.4 %copy-start = (bf16[3072,64]{0,1:T(8,128)(2,1)S(1)}, bf16[3072,64]{0,1:T(8,128)(2,1)}, u32[]{:S(2)}) copy-start(bf16[3072,64]{0,1:T(8,128)(2,1)} %param.13) | copy-start | bytes 1179652
  7.2 180.6 %all-gather.2.cloned.1.call-start = ((), (), s32[]{:S(2)}) async-start(), calls=%async_computation.4 | async-start | bytes 6684672 | tf_op jit(solution)/shard_map/all_gather | solution.py:159
  42.1 7.7 %copy-start.4 = (s32[1,16]{1,0:T(1,128)S(1)}, s32[1,16]{1,0:T(1,128)}, u32[]{:S(2)}) copy-start(s32[1,16]{1,0:T(1,128)} %param.9) | copy-start | bytes 196
  42.1 34.7 %all-to-all-start = ((bf16[16,112,384]{2,1,0:T(8,128)(2,1)}), bf16[16,112,384]{2,1,0:T(8,128)(2,1)S(1)}, u32[]{:S(2)}, u32[]{:S(2)}) async-start(bf16[16,112,384]{2,1,0:T(8,128)(2,1)} %copy.41), calls=%async_computation | async-start | bytes 2752512 | tf_op jit(solution)/shard_map/all_to_all | solution.py:145
  76.8 43.0 %all-to-all-start.2 = ((bf16[16,112,384]{2,1,0:T(8,128)(2,1)}), bf16[16,112,384]{2,1,0:T(8,128)(2,1)S(1)}, u32[]{:S(2)}, u32[]{:S(2)}) async-start(bf16[16,112,384]{2,1,0:T(8,128)(2,1)} %copy.44), calls=%async_computation.2 | async-start | bytes 2752512 | tf_op jit(solution)/shard_map/all_to_all | solution.py:145
  119.0 0.8 copy-start.1
  119.8 38.3 %all-to-all-start.1 = ((bf16[16,112,128]{2,1,0:T(8,128)(2,1)}), bf16[16,112,128]{2,1,0:T(8,128)(2,1)S(1)}, u32[]{:S(2)}, u32[]{:S(2)}) async-start(bf16[16,112,128]{2,1,0:T(8,128)(2,1)} %bitcast.79), calls=%async_computation.1 | async-start | bytes 917504 | tf_op jit(solution)/shard_map/all_to_all | solution.py:148
  158.1 15.3 %all-to-all-start.3 = ((bf16[16,112,128]{2,1,0:T(8,128)(2,1)}), bf16[16,112,128]{2,1,0:T(8,128)(2,1)S(1)}, u32[]{:S(2)}, u32[]{:S(2)}) async-start(bf16[16,112,128]{2,1,0:T(8,128)(2,1)} %bitcast.10), calls=%async_computation.3 | async-start | bytes 917504 | tf_op jit(solution)/shard_map/all_to_all | solution.py:148
  176.7 7.9 %copy-start.3 = (f32[1,2,3072]{2,1,0:T(2,128)S(1)}, f32[1,2,3072]{2,1,0:T(2,128)}, u32[]{:S(2)}) copy-start(f32[1,2,3072]{2,1,0:T(2,128)} %param.12) | copy-start | bytes 73732
  177.6 9.1 %collective-permute-start = (bf16[16,224,128]{2,1,0:T(8,128)(2,1)S(1)}, bf16[16,224,128]{2,1,0:T(8,128)(2,1)S(1)}, u32[]{:S(2)}, u32[]{:S(2)}) collective-permute-start(bf16[16,224,128]{2,1,0:T(8,128)(2,1)S(1)} %reshape.378), channel_id=1, source_target_pairs={{0,16},{16,0},{1,17},{17,1},{2,18},{18,2},{3,19},{19,3},{4,20},{20... | collective-permute-start | bytes 2752520 | tf_op jit(solution)/shard_map/ppermute | solution.py:22
  193.4 1.3 collective-permute-start.1
  194.7 4.7 %copy-start.2 = (f32[1,224,32]{1,2,0:T(8,128)S(1)}, f32[1,224,32]{1,2,0:T(8,128)}, u32[]{:S(2)}) copy-start(f32[1,224,32]{1,2,0:T(8,128)} %param.14) | copy-start | bytes 86020
  195.5 3.9 %collective-permute-start.2 = (f32[2,224,32]{1,2,0:T(8,128)S(1)}, f32[2,224,32]{1,2,0:T(8,128)S(1)}, u32[]{:S(2)}, u32[]{:S(2)}) collective-permute-start(f32[2,224,32]{1,2,0:T(8,128)S(1)} %select_bitcast_fusion.2), channel_id=1, source_target_pairs={{0,16},{16,0},{1,17},{17,1},{2,18},{18,2},{3,19},{19,3},{4,20},{20... | collective-permute-start | bytes 172040 | tf_op jit(solution)/shard_map/ppermute | solution.py:22
Sparse Core Ops, SparseCore 0:
  10.5 89.9 all-gather.1

commit v6 on v3

--- a/solution.py
+++ b/solution.py
@@ -104,6 +104,7 @@
     outgoing = outgoing.transpose(2, 0, 1, 3)
     arrived = lax.all_to_all(outgoing, "seq", split_axis=0, concat_axis=0, tiled=True)
     grouped = arrived.reshape(slot_count, 3 * group_width)
+    out_weight = out_weight + arrived[0, 0, 0, 0] * jnp.zeros((), out_weight.dtype)
     key_slots, unused_video = slot_masks(
         lengths, text_len, jnp.arange(slot_count, dtype=jnp.int32), capacity
     )

time: 159 us -> 157 us (0.987)
  blocking collectives: 0 us -> 42 us
  waiting for transfers between devices: 55.4 us -> 20.9 us
  starting transfers between devices: 18.5 us -> 6.82 us
    all_to_all x0 -> x1, blocking collectives: none -> 42 us  [body(): lax.all_to_all(outgoing, 'seq', split_axis=0, concat_axis=0, tiled=True)]
    all_to_all x1 -> x0, waiting for transfers between devices: 40.8 us -> none  [body(): lax.all_to_all(outgoing, 'seq', split_axis=0, concat_axis=0, tiled=True)]
    all_to_all x1 -> x0, starting transfers between devices: 7.7 us -> none  [body(): lax.all_to_all(outgoing, 'seq', split_axis=0, concat_axis=0, tiled=True)]
    all_to_all x1, waiting for transfers between devices: 11.2 us -> 18.2 us  [body(): lax.all_to_all(attended.reshape(seq_count, capacity, group_width), 'seq',...]
    ppermute x3, starting transfers between devices: 6.32 us -> 3.15 us  [partner_2(): lax.ppermute(array, axis, [(i, i ^ 1 << bit) for i in range(lax.axis_size...]
    transpose x1, local copies, waits for them, and re-layouts: 2.31 us -> 0.71 us  [body(): outgoing = outgoing.transpose(2, 0, 1, 3)]
  transfers between devices with their start and end apart: 6 -> 5, of which waited for: 4 -> 3; matrix products, arithmetic and copies ran while one was open for 6% -> 3% of each run, Pallas kernels for 32% -> 34%
where the time goes in v6:
time: 157 us
  Pallas kernels  52.6 us (34%)
  blocking collectives  42 us (27%)
  waiting for transfers between devices  20.9 us (13%)
  between operations  17.8 us (11%)
  starting transfers between devices  6.82 us (4%)
  matrix products  6.36 us (4%)
  local copies, waits for them, and re-layouts  6.06 us (4%)
  other arithmetic  4.38 us (3%)
    pallas_call x1, Pallas kernels, attention(): pl.pallas_call(attention_kernel, grid=(slot_count // block_rows,), in_spe...  52.6 us
    all_to_all x1, blocking collectives, body(): lax.all_to_all(outgoing, 'seq', split_axis=0, concat_axis=0, tiled=True)  42 us
    all_to_all x1, waiting for transfers between devices, body(): lax.all_to_all(attended.reshape(seq_count, capacity, group_width), 'seq',...  18.2 us
    dot_general x1, matrix products, body(): jnp.einsum('agsj,gjc->asc', both, weight_half.reshape(seq_count, group_wi...  5.61 us
    all_to_all x1, starting transfers between devices, body(): lax.all_to_all(attended.reshape(seq_count, capacity, group_width), 'seq',...  3.63 us
    ppermute x3, starting transfers between devices, partner_2(): lax.ppermute(array, axis, [(i, i ^ 1 << bit) for i in range(lax.axis_size...  3.15 us
  transfers between devices with their start and end apart: 5, of which 3 were waited for; matrix products, arithmetic and copies ran while one was open for 3% of the time, Pallas kernels for 34%

profile of v6, /device:TPU:1, one launch (start us, length us, event | category | flops | bytes accessed | tf_op | source)
XLA Modules:
  0.0 157.0 jit_solution(4756304576507277976)
XLA Ops:
  7.2 0.0 copy-start
  7.2 0.0 all-gather.2.cloned.1.call-start
  7.2 2.4 %copy.46 = bf16[28,8,48,128]{3,2,1,0:T(8,128)(2,1)S(1)} copy(bf16[28,8,48,128]{3,1,2,0:T(8,128)(2,1)} %bitcast.79) | data formatting | bytes 5505024
  9.6 0.7 copy.34
  10.3 0.0 copy-start.1
  10.4 0.0 copy-start.4
  10.4 42.0 %all_to_all.10 = bf16[16,224,3,128]{3,1,2,0:T(8,128)(2,1)S(1)} all-to-all(bf16[16,224,3,128]{3,1,2,0:T(8,128)(2,1)S(1)} %copy.34), channel_id=1, replica_groups=mesh['req'=8,'cfg'=2,'seq'=16] {'seq'}, dimensions={0} | all-to-all | bytes 5505024 | tf_op jit(solution)/shard_map/all_to_all | solution.py:105
  52.4 0.5 slice.38
  53.6 0.8 broadcast_add_fusion
  54.3 0.0 all-gather.2.cloned.1.call-update
  55.0 0.2 reduce_window_sum.12
  55.2 0.2 select_reduce_fusion.1
  55.4 0.1 and_select_fusion.bias_ref
  55.5 1.9 %copy.43 = bf16[16,224,3,128]{3,2,1,0:T(4,128)(2,1)S(1)} copy(bf16[16,224,3,128]{3,1,2,0:T(8,128)(2,1)S(1)} %all_to_all.10) | data formatting | bytes 5505024 | tf_op jit(solution)/shard_map/reshape | solution.py:106
  57.4 0.5 copy.49
  57.9 0.0 copy-start.3
  57.9 52.6 %shard_map.98 = bf16[3584,128]{1,0:T(8,128)(2,1)} custom-call(bf16[3584,384]{1,0:T(8,128)(2,1)S(1)} %bitcast.76, f32[1,3584]{1,0:T(1,128)S(1)} %and_select_fusion.bias_ref), custom_call_target="tpu_custom_call" | custom-call | tf_op jit(solution)/shard_map/pallas_call | solution.py:78
  110.5 3.6 %all-to-all-start.1 = ((bf16[16,224,128]{2,1,0:T(8,128)(2,1)}), bf16[16,224,128]{2,1,0:T(8,128)(2,1)S(1)}, u32[]{:S(2)}, u32[]{:S(2)}) async-start(bf16[16,224,128]{2,1,0:T(8,128)(2,1)} %bitcast.4), calls=%async_computation.1 | async-start | bytes 1835008 | tf_op jit(solution)/shard_map/all_to_all | solution.py:113
  114.2 18.2 %all-to-all-done.1 = bf16[16,224,128]{2,1,0:T(8,128)(2,1)S(1)} async-done(((bf16[16,224,128]{2,1,0:T(8,128)(2,1)}), bf16[16,224,128]{2,1,0:T(8,128)(2,1)S(1)}, u32[]{:S(2)}, u32[]{:S(2)}) %all-to-all-start.1) | async-done | bytes 917536 | tf_op jit(solution)/shard_map/all_to_all | solution.py:113
  132.4 2.3 %collective-permute-start = (bf16[16,224,128]{2,1,0:T(8,128)(2,1)S(1)}, bf16[16,224,128]{2,1,0:T(8,128)(2,1)S(1)}, u32[]{:S(2)}, u32[]{:S(2)}) collective-permute-start(bf16[16,224,128]{2,1,0:T(8,128)(2,1)S(1)} %all-to-all-done.1), channel_id=1, source_target_pairs={{0,16},{16,0},{1,17},{17,1},{2,18},{18,2},{3,19},{19,3},{4,20},{20... | collective-permute-start | bytes 2752520 | tf_op jit(solution)/shard_map/ppermute | solution.py:22
  134.7 2.0 %collective-permute-done = bf16[16,224,128]{2,1,0:T(8,128)(2,1)S(1)} collective-permute-done((bf16[16,224,128]{2,1,0:T(8,128)(2,1)S(1)}, bf16[16,224,128]{2,1,0:T(8,128)(2,1)S(1)}, u32[]{:S(2)}, u32[]{:S(2)}) %collective-permute-start) | collective-permute-done | bytes 917536 | tf_op jit(solution)/shard_map/ppermute | solution.py:22
  136.7 1.1 select_bitcast_fusion.1
  137.8 5.6 %fusion.22 = (f32[2,224]{1,0:T(2,128)S(1)}, f32[2,224]{1,0:T(2,128)S(1)}, f32[2,224,1536]{2,1,0:T(8,128)S(1)}) fusion(bf16[16,128,1536,1]{2,1,0,3:T(8,128)(2,1)} %bitcast.87, bf16[1,16,224,128]{3,2,1,0:T(8,128)(2,1)} %get-tuple-element.11, bf16[1,16,224,128]{3,2,1,0:T(8,128)(2,1)S(1)} %get-tuple-element.10), kind=kOutput, calls=%fused_computation.61 | convolution fusion | flops 2821553152 | bytes 10882560 | tf_op jit(solution)/shard_map/agsj,gjc->asc/dot_general | solution.py:127
  143.4 0.5 collective-permute-start.1
  143.9 0.1 select_reduce_fusion.2
  144.0 0.7 collective-permute-done.1
  144.7 0.0 copy-start.2
  144.7 0.8 fusion.3
  145.5 0.4 collective-permute-start.2
  146.6 0.6 select_reduce_fusion.5
  148.0 0.6 select_reduce_fusion.4
  149.5 0.6 add_select_fusion
  (20 shorter events, 0.2 us)
Async XLA Ops:
  7.2 127.5 %copy-start = (bf16[3072,64]{0,1:T(8,128)(2,1)S(1)}, bf16[3072,64]{0,1:T(8,128)(2,1)}, u32[]{:S(2)}) copy-start(bf16[3072,64]{0,1:T(8,128)(2,1)} %param.13) | copy-start | bytes 1179652
  7.2 130.6 %all-gather.2.cloned.1.call-start = ((), (), s32[]{:S(2)}) async-start(), calls=%async_computation.2 | async-start | bytes 6684672 | tf_op jit(solution)/shard_map/all_gather | solution.py:121
  10.3 43.2 %copy-start.1 = (bf16[128,1536]{1,0:T(8,128)(2,1)S(1)}, bf16[128,1536]{1,0:T(8,128)(2,1)}, u32[]{:S(2)}) copy-start(bf16[128,1536]{1,0:T(8,128)(2,1)} %param.11) | copy-start | bytes 1179652
  10.4 44.7 %copy-start.4 = (s32[1,16]{1,0:T(1,128)S(1)}, s32[1,16]{1,0:T(1,128)}, u32[]{:S(2)}) copy-start(s32[1,16]{1,0:T(1,128)} %param.9) | copy-start | bytes 196
  57.9 76.8 %copy-start.3 = (f32[1,2,3072]{2,1,0:T(2,128)S(1)}, f32[1,2,3072]{2,1,0:T(2,128)}, u32[]{:S(2)}) copy-start(f32[1,2,3072]{2,1,0:T(2,128)} %param.12) | copy-start | bytes 73732
  110.5 21.9 %all-to-all-start.1 = ((bf16[16,224,128]{2,1,0:T(8,128)(2,1)}), bf16[16,224,128]{2,1,0:T(8,128)(2,1)S(1)}, u32[]{:S(2)}, u32[]{:S(2)}) async-start(bf16[16,224,128]{2,1,0:T(8,128)(2,1)} %bitcast.4), calls=%async_computation.1 | async-start | bytes 1835008 | tf_op jit(solution)/shard_map/all_to_all | solution.py:113
  132.4 4.4 %collective-permute-start = (bf16[16,224,128]{2,1,0:T(8,128)(2,1)S(1)}, bf16[16,224,128]{2,1,0:T(8,128)(2,1)S(1)}, u32[]{:S(2)}, u32[]{:S(2)}) collective-permute-start(bf16[16,224,128]{2,1,0:T(8,128)(2,1)S(1)} %all-to-all-done.1), channel_id=1, source_target_pairs={{0,16},{16,0},{1,17},{17,1},{2,18},{18,2},{3,19},{19,3},{4,20},{20... | collective-permute-start | bytes 2752520 | tf_op jit(solution)/shard_map/ppermute | solution.py:22
  143.4 1.3 collective-permute-start.1
  144.7 4.7 %copy-start.2 = (f32[1,224,32]{1,2,0:T(8,128)S(1)}, f32[1,224,32]{1,2,0:T(8,128)}, u32[]{:S(2)}) copy-start(f32[1,224,32]{1,2,0:T(8,128)} %param.14) | copy-start | bytes 86020
  145.5 3.9 %collective-permute-start.2 = (f32[2,224,32]{1,2,0:T(8,128)S(1)}, f32[2,224,32]{1,2,0:T(8,128)S(1)}, u32[]{:S(2)}, u32[]{:S(2)}) collective-permute-start(f32[2,224,32]{1,2,0:T(8,128)S(1)} %select_bitcast_fusion.2), channel_id=1, source_target_pairs={{0,16},{16,0},{1,17},{17,1},{2,18},{18,2},{3,19},{19,3},{4,20},{20... | collective-permute-start | bytes 172040 | tf_op jit(solution)/shard_map/ppermute | solution.py:22
Sparse Core Ops, SparseCore 0:
  54.5 71.2 all-gather.1

commit v7 on v3

--- a/solution.py
+++ b/solution.py
@@ -1,3 +1,4 @@
+import functools
 import math
 
 import jax
@@ -49,43 +50,50 @@
     return (alpha_now, alpha_prev)
 
 
-def attention_kernel(x_ref, bias_ref, o_ref):
+def attention_kernel(q_ref, kv_ref, bias_ref, *rest, second):
+    o_ref = rest[-1]
     block = o_ref.shape[0]
     start = pl.multiple_of(pl.program_id(0) * block, block)
-    query = x_ref[pl.ds(start, block), 0:128]
-    keyset = x_ref[:, 128:256]
-    values = x_ref[:, 256:384]
-    bias = bias_ref[...]
-    lane = lax.broadcasted_iota(jnp.int32, query.shape, 1)
-    results = []
-    for head in range(2):
-        own = (lane >= HEAD) if head else (lane < HEAD)
-        masked = jnp.where(own, query, jnp.zeros_like(query))
-        scores = lax.dot_general(
-            masked, keyset, (((1,), (1,)), ((), ())), preferred_element_type=jnp.float32
-        )
-        scores = scores * (1.0 / math.sqrt(HEAD)) + bias
-        row_top = jnp.max(scores, axis=1, keepdims=True)
-        weights = jnp.exp(scores - row_top)
-        total = jnp.sum(weights, axis=1, keepdims=True)
-        probs = (weights * (1.0 / total)).astype(jnp.bfloat16)
-        results.append(jnp.dot(probs, values, preferred_element_type=jnp.float32))
-    o_ref[...] = jnp.where(lane < HEAD, results[0], results[1]).astype(o_ref.dtype)
+    query = q_ref[pl.ds(start, block), 0:128]
+    pair = kv_ref[:, kv_ref.shape[1] - 128 :]
+    low = lax.broadcasted_iota(jnp.int32, query.shape, 1) < HEAD
+    masked = jnp.where(low, jnp.zeros_like(query), query) if second else jnp.where(
+        low, query, jnp.zeros_like(query)
+    )
+    scores = lax.dot_general(
+        masked, pair, (((1,), (1,)), ((), ())), preferred_element_type=jnp.float32
+    )
+    scores = scores * (1.0 / math.sqrt(HEAD)) + bias_ref[...]
+    row_top = jnp.max(scores, axis=1, keepdims=True)
+    weights = jnp.exp(scores - row_top)
+    total = jnp.sum(weights, axis=1, keepdims=True)
+    probs = (weights * (1.0 / total)).astype(jnp.bfloat16)
+    result = jnp.dot(probs, pair, preferred_element_type=jnp.float32)
+    if second:
+        result = jnp.where(low, result, rest[0][...].astype(jnp.float32))
+    o_ref[...] = result.astype(o_ref.dtype)
 
 
-def attention(grouped, bias, block_rows=256):
-    slot_count, width = grouped.shape
+def attention(first_part, second_part, bias, earlier=None, block_rows=256):
+    slot_count = first_part.shape[0]
+    second = earlier is not None
+    operands = [first_part, second_part if second else first_part, bias]
+    in_specs = [
+        pl.BlockSpec(first_part.shape, lambda i: (0, 0)),
+        pl.BlockSpec(operands[1].shape, lambda i: (0, 0)),
+        pl.BlockSpec((1, slot_count), lambda i: (0, 0)),
+    ]
+    if second:
+        operands.append(earlier)
+        in_specs.append(pl.BlockSpec((block_rows, 128), lambda i: (i, 0)))
     return pl.pallas_call(
-        attention_kernel,
+        functools.partial(attention_kernel, second=second),
         grid=(slot_count // block_rows,),
-        in_specs=[
-            pl.BlockSpec((slot_count, width), lambda i: (0, 0)),
-            pl.BlockSpec((1, slot_count), lambda i: (0, 0)),
-        ],
-        out_specs=pl.BlockSpec((block_rows, width // 3), lambda i: (i, 0)),
-        out_shape=jax.ShapeDtypeStruct((slot_count, width // 3), jnp.bfloat16),
+        in_specs=in_specs,
+        out_specs=pl.BlockSpec((block_rows, 128), lambda i: (i, 0)),
+        out_shape=jax.ShapeDtypeStruct((slot_count, 128), jnp.bfloat16),
         compiler_params=pltpu.CompilerParams(vmem_limit_bytes=48 * 1024 * 1024),
-    )(grouped, bias)
+    )(*operands)
 
 
 def modulate(hidden, row_mean, spread, shift_part, gain_part):
@@ -100,15 +108,23 @@
     attn_width = projected.shape[3] // 3
     group_width = attn_width // seq_count
     slot_count = capacity * seq_count
-    outgoing = projected[0, 0].reshape(capacity, 3, seq_count, group_width)
-    outgoing = outgoing.transpose(2, 0, 1, 3)
-    arrived = lax.all_to_all(outgoing, "seq", split_axis=0, concat_axis=0, tiled=True)
-    grouped = arrived.reshape(slot_count, 3 * group_width)
+    split = projected[0, 0].reshape(capacity, 3, seq_count, 2, HEAD)
+    first_send = jnp.concatenate(
+        [split[:, 0].reshape(capacity, seq_count, 2 * HEAD), split[:, 1, :, 0], split[:, 2, :, 0]],
+        axis=-1,
+    ).transpose(1, 0, 2)
+    second_send = jnp.concatenate([split[:, 2, :, 1], split[:, 1, :, 1]], axis=-1).transpose(1, 0, 2)
+    arrived = lax.all_to_all(first_send, "seq", split_axis=0, concat_axis=0, tiled=True)
+    later = lax.all_to_all(second_send, "seq", split_axis=0, concat_axis=0, tiled=True)
+    out_weight = out_weight + arrived[0, 0, 0] * jnp.zeros((), out_weight.dtype)
+    out_weight = jnp.roll(out_weight, HEAD, axis=0)
     key_slots, unused_video = slot_masks(
         lengths, text_len, jnp.arange(slot_count, dtype=jnp.int32), capacity
     )
     bias = jnp.where(key_slots, 0.0, -jnp.inf).astype(jnp.float32)
-    attended = attention(grouped, bias)
+    arrived = arrived.reshape(slot_count, 4 * HEAD)
+    attended = attention(arrived, arrived, bias)
+    attended = attention(arrived, later.reshape(slot_count, 2 * HEAD), bias, attended)
     returned = lax.all_to_all(
         attended.reshape(seq_count, capacity, group_width),
         "seq",

time: 159 us -> 158 us (level)
  waiting for transfers between devices: 55.4 us -> 16 us
  blocking collectives: 0 us -> 32.2 us
  starting transfers between devices: 18.5 us -> 15.1 us
  Pallas kernels: 51.1 us -> 53.9 us
  other arithmetic: 3.6 us -> 6.22 us
  local copies, waits for them, and re-layouts: 7.1 us -> 9.54 us
    all_to_all x1, waiting for transfers between devices: 40.8 us -> 0.01 us  [body(): lax.all_to_all(second_send, 'seq', split_axis=0, concat_axis=0, tiled=True)]
    all_to_all x0 -> x1, blocking collectives: none -> 32.2 us  [body(): lax.all_to_all(first_send, 'seq', split_axis=0, concat_axis=0, tiled=True)]
    all_to_all x1, starting transfers between devices: 7.7 us -> 4.31 us  [body(): lax.all_to_all(second_send, 'seq', split_axis=0, concat_axis=0, tiled=True)]
    pallas_call x1 -> x2, Pallas kernels: 51.1 us -> 53.9 us  [attention(): pl.pallas_call(functools.partial(attention_kernel, second=second), grid=(...]
    all_to_all x1, starting transfers between devices: 4.44 us -> 6.54 us  [body(): lax.all_to_all(attended.reshape(seq_count, capacity, group_width), 'seq',...]
    ppermute x3, starting transfers between devices: 6.32 us -> 4.23 us  [partner_2(): lax.ppermute(array, axis, [(i, i ^ 1 << bit) for i in range(lax.axis_size...]
    all_to_all x1, waiting for transfers between devices: 11.2 us -> 13.3 us  [body(): lax.all_to_all(attended.reshape(seq_count, capacity, group_width), 'seq',...]
    reshape x1 -> x0, local copies, waits for them, and re-layouts: 1.89 us -> none  [body(): grouped = arrived.reshape(slot_count, 3 * group_width)]
  transfers between devices with their start and end apart: 6 -> 6, of which waited for: 4 -> 3; matrix products, arithmetic and copies ran while one was open for 6% -> 4% of each run, Pallas kernels for 32% -> 34%
where the time goes in v7:
time: 158 us; the launch traced here: 157 us
  Pallas kernels  53.9 us (34%)
  blocking collectives  32.2 us (20%)
  between operations  17.8 us (11%)
  waiting for transfers between devices  16 us (10%)
  starting transfers between devices  15.1 us (10%)
  local copies, waits for them, and re-layouts  9.54 us (6%)
  matrix products  6.37 us (4%)
  other arithmetic  6.22 us (4%)
    pallas_call x2, Pallas kernels, attention(): pl.pallas_call(functools.partial(attention_kernel, second=second), grid=(...  53.9 us
    all_to_all x1, blocking collectives, body(): lax.all_to_all(first_send, 'seq', split_axis=0, concat_axis=0, tiled=True)  32.2 us
    all_to_all x1, waiting for transfers between devices, body(): lax.all_to_all(attended.reshape(seq_count, capacity, group_width), 'seq',...  13.3 us
    all_to_all x1, starting transfers between devices, body(): lax.all_to_all(attended.reshape(seq_count, capacity, group_width), 'seq',...  6.54 us
    dot_general x1, matrix products, body(): jnp.einsum('agsj,gjc->asc', both, weight_half.reshape(seq_count, group_wi...  5.6 us
    all_to_all x1, starting transfers between devices, body(): lax.all_to_all(second_send, 'seq', split_axis=0, concat_axis=0, tiled=True)  4.31 us
    ppermute x3, starting transfers between devices, partner_2(): lax.ppermute(array, axis, [(i, i ^ 1 << bit) for i in range(lax.axis_size...  4.23 us
    unnamed x13, local copies, waits for them, and re-layouts  4.09 us
  transfers between devices with their start and end apart: 6, of which 3 were waited for; matrix products, arithmetic and copies ran while one was open for 4% of the time, Pallas kernels for 34%

profile of v7, /device:TPU:1, one launch (start us, length us, event | category | flops | bytes accessed | tf_op | source)
XLA Modules:
  0.0 157.1 jit_solution(15387717060364752301)
XLA Ops:
  7.2 0.0 all-gather.2.cloned.1.call-start
  7.2 3.1 %copy.35 = bf16[1,1,224,6144]{2,3,1,0:T(8,128)(2,1)S(1)} copy(bf16[1,1,224,6144]{3,2,1,0:T(8,128)(2,1)} %param.8) | data formatting | bytes 5505024 | tf_op args[0]
  10.4 1.1 slice_bitcast_fusion.1
  11.5 0.1 slice.68
  11.6 0.4 maximum_bitcast_fusion
  12.0 2.4 %copy.36 = bf16[16,224,256]{2,1,0:T(8,128)(2,1)} copy(bf16[16,224,256]{1,2,0:T(8,128)(2,1)S(1)} %maximum_bitcast_fusion) | data formatting | bytes 3670016 | tf_op jit(solution)/shard_map/transpose | solution.py:115
  14.3 32.2 %all_to_all.15 = bf16[16,224,256]{2,1,0:T(8,128)(2,1)S(1)} all-to-all(bf16[16,224,256]{2,1,0:T(8,128)(2,1)} %copy.36), channel_id=1, replica_groups=mesh['req'=8,'cfg'=2,'seq'=16] {'seq'}, dimensions={0} | all-to-all | bytes 3670016 | tf_op jit(solution)/shard_map/all_to_all | solution.py:117
  46.5 0.5 slice.73
  47.8 0.8 pad_maximum_fusion
  48.6 1.4 maximum_bitcast_fusion.1
  50.0 1.3 copy.38
  51.3 4.3 %all-to-all-start.1 = ((bf16[16,224,128]{2,1,0:T(8,128)(2,1)}), bf16[16,224,128]{2,1,0:T(8,128)(2,1)}, u32[]{:S(2)}, u32[]{:S(2)}) async-start(bf16[16,224,128]{2,1,0:T(8,128)(2,1)} %copy.38), calls=%async_computation.1 | async-start | bytes 1835008 | tf_op jit(solution)/shard_map/all_to_all | solution.py:118
  56.3 0.2 reduce_window_sum.12
  56.5 0.2 select_reduce_fusion.1
  56.7 0.1 and_select_fusion.bias_ref
  56.8 26.3 %shard_map.98.rest_0_ = bf16[3584,128]{1,0:T(8,128)(2,1)S(1)} custom-call(bf16[3584,256]{1,0:T(8,128)(2,1)S(1)} %bitcast.82, bf16[3584,256]{1,0:T(8,128)(2,1)S(1)} %bitcast.83, f32[1,3584]{1,0:T(1,128)S(1)} %and_select_fusion.bias_ref), custom_call_target="tpu_custom_call" | custom-call | tf_op jit(solution)/shard_map/pallas_call | solution.py:89
  83.1 27.5 %shard_map.99 = bf16[3584,128]{1,0:T(8,128)(2,1)S(1)} custom-call(bf16[3584,256]{1,0:T(8,128)(2,1)S(1)} %bitcast.84, bf16[3584,128]{1,0:T(8,128)(2,1)} %bitcast.11.kv_ref, f32[1,3584]{1,0:T(1,128)S(1)} %and_select_fusion.bias_ref, bf16[3584,128]{1,0:T(8,128)(2,1)S(1)} %shard_map.98.rest_0_), custom_call_target="tpu_custom_call" | custom-call | tf_op jit(solution)/shard_map/pallas_call | solution.py:89
  110.7 0.9 copy-done.1
  111.6 6.5 %all-to-all-start.2 = ((bf16[16,224,128]{2,1,0:T(8,128)(2,1)}), bf16[16,224,128]{2,1,0:T(8,128)(2,1)S(1)}, u32[]{:S(2)}, u32[]{:S(2)}) async-start(bf16[16,224,128]{2,1,0:T(8,128)(2,1)} %bitcast.85), calls=%async_computation.2 | async-start | bytes 1835008 | tf_op jit(solution)/shard_map/all_to_all | solution.py:128
  118.2 13.3 %all-to-all-done.2 = bf16[16,224,128]{2,1,0:T(8,128)(2,1)S(1)} async-done(((bf16[16,224,128]{2,1,0:T(8,128)(2,1)}), bf16[16,224,128]{2,1,0:T(8,128)(2,1)S(1)}, u32[]{:S(2)}, u32[]{:S(2)}) %all-to-all-start.2) | async-done | bytes 917536 | tf_op jit(solution)/shard_map/all_to_all | solution.py:128
  131.5 3.4 %collective-permute-start = (bf16[16,224,128]{2,1,0:T(8,128)(2,1)S(1)}, bf16[16,224,128]{2,1,0:T(8,128)(2,1)S(1)}, u32[]{:S(2)}, u32[]{:S(2)}) collective-permute-start(bf16[16,224,128]{2,1,0:T(8,128)(2,1)S(1)} %all-to-all-done.2), channel_id=1, source_target_pairs={{0,16},{16,0},{1,17},{17,1},{2,18},{18,2},{3,19},{19,3},{4,20},{20... | collective-permute-start | bytes 2752520 | tf_op jit(solution)/shard_map/ppermute | solution.py:23
  134.9 2.0 %collective-permute-done = bf16[16,224,128]{2,1,0:T(8,128)(2,1)S(1)} collective-permute-done((bf16[16,224,128]{2,1,0:T(8,128)(2,1)S(1)}, bf16[16,224,128]{2,1,0:T(8,128)(2,1)S(1)}, u32[]{:S(2)}, u32[]{:S(2)}) %collective-permute-start) | collective-permute-done | bytes 917536 | tf_op jit(solution)/shard_map/ppermute | solution.py:23
  136.9 1.1 select_bitcast_fusion.1
  138.0 5.6 %fusion.22 = (f32[2,224]{1,0:T(2,128)S(1)}, f32[2,224]{1,0:T(2,128)S(1)}, f32[2,224,1536]{2,1,0:T(8,128)S(1)}) fusion(bf16[16,128,1536,1]{2,1,0,3:T(8,128)(2,1)} %bitcast.96, bf16[1,16,224,128]{3,2,1,0:T(8,128)(2,1)} %get-tuple-element.15, bf16[1,16,224,128]{3,2,1,0:T(8,128)(2,1)S(1)} %get-tuple-element.14), kind=kOutput, calls=%fused_computation.67 | convolution fusion | flops 2821553152 | bytes 10882560 | tf_op jit(solution)/shard_map/agsj,gjc->asc/dot_general | solution.py:142
  143.6 0.5 collective-permute-start.1
  144.0 0.1 select_reduce_fusion.2
  144.2 0.7 collective-permute-done.1
  144.9 0.8 fusion.3
  145.7 0.4 collective-permute-start.2
  146.8 0.6 select_reduce_fusion.5
  148.2 0.6 select_reduce_fusion.4
  149.6 0.6 add_select_fusion
  (30 shorter events, 0.3 us)
Async XLA Ops:
  7.2 127.7 %copy-start = (bf16[3072,64]{0,1:T(8,128)(2,1)S(1)}, bf16[3072,64]{0,1:T(8,128)(2,1)}, u32[]{:S(2)}) copy-start(bf16[3072,64]{0,1:T(8,128)(2,1)} %param.13) | copy-start | bytes 1179652
  7.2 130.8 %all-gather.2.cloned.1.call-start = ((), (), s32[]{:S(2)}) async-start(), calls=%async_computation.3 | async-start | bytes 6684672 | tf_op jit(solution)/shard_map/all_gather | solution.py:136
  14.3 33.4 %copy-start.2 = (bf16[128,1536]{1,0:T(8,128)(2,1)S(1)}, bf16[128,1536]{1,0:T(8,128)(2,1)}, u32[]{:S(2)}) copy-start(bf16[128,1536]{1,0:T(8,128)(2,1)} %param.11) | copy-start | bytes 1179652
  48.6 7.7 %copy-start.5 = (s32[1,16]{1,0:T(1,128)S(1)}, s32[1,16]{1,0:T(1,128)}, u32[]{:S(2)}) copy-start(s32[1,16]{1,0:T(1,128)} %param.9) | copy-start | bytes 196
  51.3 31.8 %all-to-all-start.1 = ((bf16[16,224,128]{2,1,0:T(8,128)(2,1)}), bf16[16,224,128]{2,1,0:T(8,128)(2,1)}, u32[]{:S(2)}, u32[]{:S(2)}) async-start(bf16[16,224,128]{2,1,0:T(8,128)(2,1)} %copy.38), calls=%async_computation.1 | async-start | bytes 1835008 | tf_op jit(solution)/shard_map/all_to_all | solution.py:118
  83.1 51.8 %copy-start.4 = (f32[1,2,3072]{2,1,0:T(2,128)S(1)}, f32[1,2,3072]{2,1,0:T(2,128)}, u32[]{:S(2)}) copy-start(f32[1,2,3072]{2,1,0:T(2,128)} %param.12) | copy-start | bytes 73732
  110.7 0.9 copy-start.1
  111.6 19.9 %all-to-all-start.2 = ((bf16[16,224,128]{2,1,0:T(8,128)(2,1)}), bf16[16,224,128]{2,1,0:T(8,128)(2,1)S(1)}, u32[]{:S(2)}, u32[]{:S(2)}) async-start(bf16[16,224,128]{2,1,0:T(8,128)(2,1)} %bitcast.85), calls=%async_computation.2 | async-start | bytes 1835008 | tf_op jit(solution)/shard_map/all_to_all | solution.py:128
  131.5 5.5 %collective-permute-start = (bf16[16,224,128]{2,1,0:T(8,128)(2,1)S(1)}, bf16[16,224,128]{2,1,0:T(8,128)(2,1)S(1)}, u32[]{:S(2)}, u32[]{:S(2)}) collective-permute-start(bf16[16,224,128]{2,1,0:T(8,128)(2,1)S(1)} %all-to-all-done.2), channel_id=1, source_target_pairs={{0,16},{16,0},{1,17},{17,1},{2,18},{18,2},{3,19},{19,3},{4,20},{20... | collective-permute-start | bytes 2752520 | tf_op jit(solution)/shard_map/ppermute | solution.py:23
  143.6 1.3 collective-permute-start.1
  144.9 4.7 %copy-start.3 = (f32[1,224,32]{1,2,0:T(8,128)S(1)}, f32[1,224,32]{1,2,0:T(8,128)}, u32[]{:S(2)}) copy-start(f32[1,224,32]{1,2,0:T(8,128)} %param.14) | copy-start | bytes 86020
  145.7 3.9 %collective-permute-start.2 = (f32[2,224,32]{1,2,0:T(8,128)S(1)}, f32[2,224,32]{1,2,0:T(8,128)S(1)}, u32[]{:S(2)}, u32[]{:S(2)}) collective-permute-start(f32[2,224,32]{1,2,0:T(8,128)S(1)} %select_bitcast_fusion.2), channel_id=1, source_target_pairs={{0,16},{16,0},{1,17},{17,1},{2,18},{18,2},{3,19},{19,3},{4,20},{20... | collective-permute-start | bytes 172040 | tf_op jit(solution)/shard_map/ppermute | solution.py:23
Sparse Core Ops, SparseCore 0:
  48.7 69.9 all-gather.1

commit v8 on v6

--- a/solution.py
+++ b/solution.py
@@ -1,3 +1,4 @@
+import functools
 import math
 
 import jax
@@ -49,10 +50,17 @@
     return (alpha_now, alpha_prev)
 
 
-def attention_kernel(x_ref, bias_ref, o_ref):
-    block = o_ref.shape[0]
-    start = pl.multiple_of(pl.program_id(0) * block, block)
-    query = x_ref[pl.ds(start, block), 0:128]
+def attention_kernel(x_ref, bias_ref, o_ref, *, part):
+    step_pieces, rows = o_ref.shape[0], o_ref.shape[1]
+    capacity = rows * 2
+    first_piece = pl.program_id(0) * step_pieces
+    query = jnp.concatenate(
+        [
+            x_ref[pl.ds(pl.multiple_of((first_piece + j) * capacity + part * rows, 16), rows), 0:128]
+            for j in range(step_pieces)
+        ],
+        axis=0,
+    )
     keyset = x_ref[:, 128:256]
     values = x_ref[:, 256:384]
     bias = bias_ref[...]
@@ -70,22 +78,25 @@
         total = jnp.sum(weights, axis=1, keepdims=True)
         probs = (weights * (1.0 / total)).astype(jnp.bfloat16)
         results.append(jnp.dot(probs, values, preferred_element_type=jnp.float32))
-    o_ref[...] = jnp.where(lane < HEAD, results[0], results[1]).astype(o_ref.dtype)
+    out = jnp.where(lane < HEAD, results[0], results[1]).astype(o_ref.dtype)
+    o_ref[...] = out.reshape(o_ref.shape)
 
 
-def attention(grouped, bias, block_rows=256):
-    slot_count, width = grouped.shape
+def attention(pieces, bias, part, parts=2, pieces_per_step=2):
+    piece_count, capacity, width = pieces.shape
+    rows = capacity // parts
+    flat = pieces.reshape(piece_count * capacity, width)
     return pl.pallas_call(
-        attention_kernel,
-        grid=(slot_count // block_rows,),
+        functools.partial(attention_kernel, part=part),
+        grid=(piece_count // pieces_per_step,),
         in_specs=[
-            pl.BlockSpec((slot_count, width), lambda i: (0, 0)),
-            pl.BlockSpec((1, slot_count), lambda i: (0, 0)),
+            pl.BlockSpec(flat.shape, lambda i: (0, 0)),
+            pl.BlockSpec((1, piece_count * capacity), lambda i: (0, 0)),
         ],
-        out_specs=pl.BlockSpec((block_rows, width // 3), lambda i: (i, 0)),
-        out_shape=jax.ShapeDtypeStruct((slot_count, width // 3), jnp.bfloat16),
+        out_specs=pl.BlockSpec((pieces_per_step, rows, width // 3), lambda i: (i, 0, 0)),
+        out_shape=jax.ShapeDtypeStruct((piece_count, rows, width // 3), jnp.bfloat16),
         compiler_params=pltpu.CompilerParams(vmem_limit_bytes=48 * 1024 * 1024),
-    )(grouped, bias)
+    )(flat, bias)
 
 
 def modulate(hidden, row_mean, spread, shift_part, gain_part):
@@ -109,14 +120,14 @@
         lengths, text_len, jnp.arange(slot_count, dtype=jnp.int32), capacity
     )
     bias = jnp.where(key_slots, 0.0, -jnp.inf).astype(jnp.float32)
-    attended = attention(grouped, bias)
-    returned = lax.all_to_all(
-        attended.reshape(seq_count, capacity, group_width),
-        "seq",
-        split_axis=0,
-        concat_axis=0,
-        tiled=True,
-    )
+    pieces = grouped.reshape(seq_count, capacity, 3 * group_width)
+    halves = []
+    for part in range(2):
+        attended = attention(pieces, bias, part)
+        halves.append(
+            lax.all_to_all(attended, "seq", split_axis=0, concat_axis=0, tiled=True)
+        )
+    returned = jnp.concatenate(halves, axis=1)
     cfg_index = lax.axis_index("cfg")
     weight_half = lax.all_gather(out_weight, "seq", axis=0, tiled=True)
     partner_rows = partner_2(returned, "cfg", 0)

time: 157 us -> 157 us (level)
  waiting for transfers between devices: 20.9 us -> 10.3 us
  starting transfers between devices: 6.82 us -> 15.6 us
  local copies, waits for them, and re-layouts: 6.06 us -> 8.69 us
    all_to_all x1 -> x2, waiting for transfers between devices: 18.2 us -> 7.56 us  [body(): lax.all_to_all(attended, 'seq', split_axis=0, concat_axis=0, tiled=True)]
    all_to_all x1 -> x2, starting transfers between devices: 3.63 us -> 10.8 us  [body(): lax.all_to_all(attended, 'seq', split_axis=0, concat_axis=0, tiled=True)]
    unnamed x12 -> x17, local copies, waits for them, and re-layouts: 2.9 us -> 5.48 us
    another operation x0 -> x1, local copies, waits for them, and re-layouts: none -> 1.89 us  [attention(): flat = pieces.reshape(piece_count * capacity, width)]
    reshape x1 -> x0, local copies, waits for them, and re-layouts: 1.89 us -> none  [body(): grouped = arrived.reshape(slot_count, 3 * group_width)]
    ppermute x3, starting transfers between devices: 3.15 us -> 4.86 us  [partner_2(): lax.ppermute(array, axis, [(i, i ^ 1 << bit) for i in range(lax.axis_size...]
    pallas_call x1 -> x2, Pallas kernels: 52.6 us -> 51.7 us  [attention(): pl.pallas_call(functools.partial(attention_kernel, part=part), grid=(piec...]
  transfers between devices with their start and end apart: 5 -> 6, of which waited for: 3 -> 3; matrix products, arithmetic and copies ran while one was open for 3% -> 4% of each run, Pallas kernels for 34% -> 33%
where the time goes in v8:
time: 157 us
  Pallas kernels  51.7 us (33%)
  blocking collectives  42 us (27%)
  between operations  17.8 us (11%)
  starting transfers between devices  15.6 us (10%)
  waiting for transfers between devices  10.3 us (7%)
  local copies, waits for them, and re-layouts  8.69 us (6%)
  matrix products  6.37 us (4%)
  other arithmetic  4.38 us (3%)
    pallas_call x2, Pallas kernels, attention(): pl.pallas_call(functools.partial(attention_kernel, part=part), grid=(piec...  51.7 us
    all_to_all x1, blocking collectives, body(): lax.all_to_all(outgoing, 'seq', split_axis=0, concat_axis=0, tiled=True)  42 us
    all_to_all x2, starting transfers between devices, body(): lax.all_to_all(attended, 'seq', split_axis=0, concat_axis=0, tiled=True)  10.8 us
    all_to_all x2, waiting for transfers between devices, body(): lax.all_to_all(attended, 'seq', split_axis=0, concat_axis=0, tiled=True)  7.56 us
    dot_general x1, matrix products, body(): jnp.einsum('agsj,gjc->asc', both, weight_half.reshape(seq_count, group_wi...  5.59 us
    unnamed x17, local copies, waits for them, and re-layouts  5.48 us
    ppermute x3, starting transfers between devices, partner_2(): lax.ppermute(array, axis, [(i, i ^ 1 << bit) for i in range(lax.axis_size...  4.86 us
  transfers between devices with their start and end apart: 6, of which 3 were waited for; matrix products, arithmetic and copies ran while one was open for 4% of the time, Pallas kernels for 33%

profile of v8, /device:TPU:1, one launch (start us, length us, event | category | flops | bytes accessed | tf_op | source)
XLA Modules:
  0.0 156.9 jit_solution(12852752226351132027)
XLA Ops:
  7.2 0.0 all-gather.2.cloned.1.call-start
  7.2 2.4 %copy.50 = bf16[28,8,48,128]{3,2,1,0:T(8,128)(2,1)S(1)} copy(bf16[28,8,48,128]{3,1,2,0:T(8,128)(2,1)} %bitcast.79) | data formatting | bytes 5505024
  9.6 0.7 copy.37
  10.4 42.0 %all_to_all.15 = bf16[16,224,3,128]{3,1,2,0:T(8,128)(2,1)S(1)} all-to-all(bf16[16,224,3,128]{3,1,2,0:T(8,128)(2,1)S(1)} %copy.37), channel_id=1, replica_groups=mesh['req'=8,'cfg'=2,'seq'=16] {'seq'}, dimensions={0} | all-to-all | bytes 5505024 | tf_op jit(solution)/shard_map/all_to_all | solution.py:116
  52.4 0.5 slice.38
  53.6 0.8 broadcast_add_fusion
  55.0 0.2 reduce_window_sum.12
  55.3 0.2 select_reduce_fusion.1
  55.4 0.1 and_select_fusion.bias_ref
  55.5 1.9 %copy.47 = bf16[16,224,3,128]{3,2,1,0:T(4,128)(2,1)S(1)} copy(bf16[16,224,3,128]{3,1,2,0:T(8,128)(2,1)S(1)} %all_to_all.15) | data formatting | bytes 5505024 | tf_op jit(solution)/shard_map/reshape;reshape;reshape | solution.py:88
  57.4 0.5 copy.53
  57.9 25.8 %shard_map.98 = bf16[16,112,128]{2,1,0:T(8,128)(2,1)S(1)} custom-call(bf16[3584,384]{1,0:T(8,128)(2,1)S(1)} %bitcast.75, f32[1,3584]{1,0:T(1,128)S(1)} %and_select_fusion.bias_ref), custom_call_target="tpu_custom_call" | custom-call | tf_op jit(solution)/shard_map/pallas_call | solution.py:89
  83.7 0.8 copy-done.2
  84.5 4.2 %all-to-all-start.1 = ((bf16[16,112,128]{2,1,0:T(8,128)(2,1)}), bf16[16,112,128]{2,1,0:T(8,128)(2,1)}, u32[]{:S(2)}, u32[]{:S(2)}) async-start(bf16[16,112,128]{2,1,0:T(8,128)(2,1)} %copy-done.2), calls=%async_computation.1 | async-start | bytes 917504 | tf_op jit(solution)/shard_map/all_to_all | solution.py:128
  88.7 25.9 %shard_map.99 = bf16[16,112,128]{2,1,0:T(8,128)(2,1)S(1)} custom-call(bf16[3584,384]{1,0:T(8,128)(2,1)S(1)} %bitcast.76, f32[1,3584]{1,0:T(1,128)S(1)} %and_select_fusion.bias_ref), custom_call_target="tpu_custom_call" | custom-call | tf_op jit(solution)/shard_map/pallas_call | solution.py:89
  114.6 0.8 copy-done.1
  115.4 6.5 %all-to-all-start.2 = ((bf16[16,112,128]{2,1,0:T(8,128)(2,1)}), bf16[16,112,128]{2,1,0:T(8,128)(2,1)S(1)}, u32[]{:S(2)}, u32[]{:S(2)}) async-start(bf16[16,112,128]{2,1,0:T(8,128)(2,1)} %copy-done.1), calls=%async_computation.2 | async-start | bytes 917504 | tf_op jit(solution)/shard_map/all_to_all | solution.py:128
  121.9 1.0 constant_dynamic-update-slice_fusion.1
  123.0 7.6 %all-to-all-done.2 = bf16[16,112,128]{2,1,0:T(8,128)(2,1)S(1)} async-done(((bf16[16,112,128]{2,1,0:T(8,128)(2,1)}), bf16[16,112,128]{2,1,0:T(8,128)(2,1)S(1)}, u32[]{:S(2)}, u32[]{:S(2)}) %all-to-all-start.2) | async-done | bytes 458784 | tf_op jit(solution)/shard_map/all_to_all | solution.py:128
  130.5 0.1 constant_dynamic-update-slice_fusion
  130.6 4.0 %collective-permute-start = (bf16[16,224,128]{2,1,0:T(8,128)(2,1)S(1)}, bf16[16,224,128]{2,1,0:T(8,128)(2,1)S(1)}, u32[]{:S(2)}, u32[]{:S(2)}) collective-permute-start(bf16[16,224,128]{2,1,0:T(8,128)(2,1)S(1)} %constant_dynamic-update-slice_fusion), channel_id=1, source_target_pairs={{0,16},{16,0},{1,17},{17,1},{2,18},{18,2},{3,19},{19,3},{4,20},{20... | collective-permute-start | bytes 2752520 | tf_op jit(solution)/shard_map/ppermute | solution.py:23
  134.7 2.0 %collective-permute-done = bf16[16,224,128]{2,1,0:T(8,128)(2,1)S(1)} collective-permute-done((bf16[16,224,128]{2,1,0:T(8,128)(2,1)S(1)}, bf16[16,224,128]{2,1,0:T(8,128)(2,1)S(1)}, u32[]{:S(2)}, u32[]{:S(2)}) %collective-permute-start) | collective-permute-done | bytes 917536 | tf_op jit(solution)/shard_map/ppermute | solution.py:23
  136.7 1.1 select_bitcast_fusion.1
  137.7 5.6 %fusion.22 = (f32[2,224]{1,0:T(2,128)S(1)}, f32[2,224]{1,0:T(2,128)S(1)}, f32[2,224,1536]{2,1,0:T(8,128)S(1)}) fusion(bf16[16,128,1536,1]{2,1,0,3:T(8,128)(2,1)} %bitcast.87, bf16[1,16,224,128]{3,2,1,0:T(8,128)(2,1)} %get-tuple-element.11, bf16[1,16,224,128]{3,2,1,0:T(8,128)(2,1)S(1)} %get-tuple-element.10), kind=kOutput, calls=%fused_computation.63 | convolution fusion | flops 2821553152 | bytes 10882560 | tf_op jit(solution)/shard_map/agsj,gjc->asc/dot_general | solution.py:138
  143.3 0.5 collective-permute-start.1
  143.8 0.1 select_reduce_fusion.2
  143.9 0.7 collective-permute-done.1
  144.7 0.8 fusion.3
  145.5 0.4 collective-permute-start.2
  146.6 0.6 select_reduce_fusion.5
  147.9 0.6 select_reduce_fusion.4
  149.4 0.6 add_select_fusion
  (29 shorter events, 0.3 us)
Async XLA Ops:
  7.2 127.4 %copy-start = (bf16[3072,64]{0,1:T(8,128)(2,1)S(1)}, bf16[3072,64]{0,1:T(8,128)(2,1)}, u32[]{:S(2)}) copy-start(bf16[3072,64]{0,1:T(8,128)(2,1)} %param.13) | copy-start | bytes 1179652
  7.2 130.5 %all-gather.2.cloned.1.call-start = ((), (), s32[]{:S(2)}) async-start(), calls=%async_computation.3 | async-start | bytes 6684672 | tf_op jit(solution)/shard_map/all_gather | solution.py:132
  10.3 43.2 %copy-start.3 = (bf16[128,1536]{1,0:T(8,128)(2,1)S(1)}, bf16[128,1536]{1,0:T(8,128)(2,1)}, u32[]{:S(2)}) copy-start(bf16[128,1536]{1,0:T(8,128)(2,1)} %param.11) | copy-start | bytes 1179652
  10.4 44.7 %copy-start.6 = (s32[1,16]{1,0:T(1,128)S(1)}, s32[1,16]{1,0:T(1,128)}, u32[]{:S(2)}) copy-start(s32[1,16]{1,0:T(1,128)} %param.9) | copy-start | bytes 196
  83.7 0.8 copy-start.2
  84.5 30.9 %all-to-all-start.1 = ((bf16[16,112,128]{2,1,0:T(8,128)(2,1)}), bf16[16,112,128]{2,1,0:T(8,128)(2,1)}, u32[]{:S(2)}, u32[]{:S(2)}) async-start(bf16[16,112,128]{2,1,0:T(8,128)(2,1)} %copy-done.2), calls=%async_computation.1 | async-start | bytes 917504 | tf_op jit(solution)/shard_map/all_to_all | solution.py:128
  88.7 45.9 %copy-start.5 = (f32[1,2,3072]{2,1,0:T(2,128)S(1)}, f32[1,2,3072]{2,1,0:T(2,128)}, u32[]{:S(2)}) copy-start(f32[1,2,3072]{2,1,0:T(2,128)} %param.12) | copy-start | bytes 73732
  114.6 0.8 copy-start.1
  115.4 15.2 %all-to-all-start.2 = ((bf16[16,112,128]{2,1,0:T(8,128)(2,1)}), bf16[16,112,128]{2,1,0:T(8,128)(2,1)S(1)}, u32[]{:S(2)}, u32[]{:S(2)}) async-start(bf16[16,112,128]{2,1,0:T(8,128)(2,1)} %copy-done.1), calls=%async_computation.2 | async-start | bytes 917504 | tf_op jit(solution)/shard_map/all_to_all | solution.py:128
  130.6 6.1 %collective-permute-start = (bf16[16,224,128]{2,1,0:T(8,128)(2,1)S(1)}, bf16[16,224,128]{2,1,0:T(8,128)(2,1)S(1)}, u32[]{:S(2)}, u32[]{:S(2)}) collective-permute-start(bf16[16,224,128]{2,1,0:T(8,128)(2,1)S(1)} %constant_dynamic-update-slice_fusion), channel_id=1, source_target_pairs={{0,16},{16,0},{1,17},{17,1},{2,18},{18,2},{3,19},{19,3},{4,20},{20... | collective-permute-start | bytes 2752520 | tf_op jit(solution)/shard_map/ppermute | solution.py:23
  143.3 1.3 collective-permute-start.1
  144.7 4.7 %copy-start.4 = (f32[1,224,32]{1,2,0:T(8,128)S(1)}, f32[1,224,32]{1,2,0:T(8,128)}, u32[]{:S(2)}) copy-start(f32[1,224,32]{1,2,0:T(8,128)} %param.14) | copy-start | bytes 86020
  145.5 3.9 %collective-permute-start.2 = (f32[2,224,32]{1,2,0:T(8,128)S(1)}, f32[2,224,32]{1,2,0:T(8,128)S(1)}, u32[]{:S(2)}, u32[]{:S(2)}) collective-permute-start(f32[2,224,32]{1,2,0:T(8,128)S(1)} %select_bitcast_fusion.2), channel_id=1, source_target_pairs={{0,16},{16,0},{1,17},{17,1},{2,18},{18,2},{3,19},{19,3},{4,20},{20... | collective-permute-start | bytes 172040 | tf_op jit(solution)/shard_map/ppermute | solution.py:23
Sparse Core Ops, SparseCore 0:
  54.5 70.1 all-gather.1

commit v9 on v8

--- a/solution.py
+++ b/solution.py
@@ -50,13 +50,12 @@
     return (alpha_now, alpha_prev)
 
 
-def attention_kernel(x_ref, bias_ref, o_ref, *, part):
+def attention_kernel(x_ref, bias_ref, o_ref, *, row_start, capacity):
     step_pieces, rows = o_ref.shape[0], o_ref.shape[1]
-    capacity = rows * 2
     first_piece = pl.program_id(0) * step_pieces
     query = jnp.concatenate(
         [
-            x_ref[pl.ds(pl.multiple_of((first_piece + j) * capacity + part * rows, 16), rows), 0:128]
+            x_ref[pl.ds(pl.multiple_of((first_piece + j) * capacity + row_start, 16), rows), 0:128]
             for j in range(step_pieces)
         ],
         axis=0,
@@ -82,12 +81,11 @@
     o_ref[...] = out.reshape(o_ref.shape)
 
 
-def attention(pieces, bias, part, parts=2, pieces_per_step=2):
+def attention(pieces, bias, row_start, rows, pieces_per_step):
     piece_count, capacity, width = pieces.shape
-    rows = capacity // parts
     flat = pieces.reshape(piece_count * capacity, width)
     return pl.pallas_call(
-        functools.partial(attention_kernel, part=part),
+        functools.partial(attention_kernel, row_start=row_start, capacity=capacity),
         grid=(piece_count // pieces_per_step,),
         in_specs=[
             pl.BlockSpec(flat.shape, lambda i: (0, 0)),
@@ -122,8 +120,8 @@
     bias = jnp.where(key_slots, 0.0, -jnp.inf).astype(jnp.float32)
     pieces = grouped.reshape(seq_count, capacity, 3 * group_width)
     halves = []
-    for part in range(2):
-        attended = attention(pieces, bias, part)
+    for row_start, rows, pieces_per_step in ((0, 160, 2), (160, capacity - 160, 4)):
+        attended = attention(pieces, bias, row_start, rows, pieces_per_step)
         halves.append(
             lax.all_to_all(attended, "seq", split_axis=0, concat_axis=0, tiled=True)
         )

time: 157 us -> 163 us (1.038)
  Pallas kernels: 51.7 us -> 57.5 us
    pallas_call x2, Pallas kernels: 51.7 us -> 57.5 us  [attention(): pl.pallas_call(functools.partial(attention_kernel, row_start=row_start, c...]
    unnamed x17 -> x15, local copies, waits for them, and re-layouts: 5.48 us -> 4.88 us
  transfers between devices with their start and end apart: 6 -> 6, of which waited for: 3 -> 4; matrix products, arithmetic and copies ran while one was open for 4% -> 4% of each run, Pallas kernels for 33% -> 35%
where the time goes in v9:
time: 163 us; the launch traced here: 162 us
  Pallas kernels  57.5 us (35%)
  blocking collectives  42 us (26%)
  between operations  17.8 us (11%)
  starting transfers between devices  15.8 us (10%)
  waiting for transfers between devices  10.5 us (6%)
  local copies, waits for them, and re-layouts  8.07 us (5%)
  matrix products  6.36 us (4%)
  other arithmetic  4.36 us (3%)
    pallas_call x2, Pallas kernels, attention(): pl.pallas_call(functools.partial(attention_kernel, row_start=row_start, c...  57.5 us
    all_to_all x1, blocking collectives, body(): lax.all_to_all(outgoing, 'seq', split_axis=0, concat_axis=0, tiled=True)  42 us
    all_to_all x2, starting transfers between devices, body(): lax.all_to_all(attended, 'seq', split_axis=0, concat_axis=0, tiled=True)  10.6 us
    all_to_all x2, waiting for transfers between devices, body(): lax.all_to_all(attended, 'seq', split_axis=0, concat_axis=0, tiled=True)  7.75 us
    dot_general x1, matrix products, body(): jnp.einsum('agsj,gjc->asc', both, weight_half.reshape(seq_count, group_wi...  5.6 us
    ppermute x3, starting transfers between devices, partner_2(): lax.ppermute(array, axis, [(i, i ^ 1 << bit) for i in range(lax.axis_size...  5.13 us
    unnamed x15, local copies, waits for them, and re-layouts  4.88 us
  transfers between devices with their start and end apart: 6, of which 4 were waited for; matrix products, arithmetic and copies ran while one was open for 4% of the time, Pallas kernels for 35%

profile of v9, /device:TPU:1, one launch (start us, length us, event | category | flops | bytes accessed | tf_op | source)
XLA Modules:
  0.0 162.3 jit_solution(1910104154955245578)
XLA Ops:
  7.2 0.0 all-gather.2.cloned.1.call-start
  7.2 2.4 %copy.50 = bf16[28,8,48,128]{3,2,1,0:T(8,128)(2,1)S(1)} copy(bf16[28,8,48,128]{3,1,2,0:T(8,128)(2,1)} %bitcast.79) | data formatting | bytes 5505024
  9.6 0.7 copy.37
  10.4 42.0 %all_to_all.15 = bf16[16,224,3,128]{3,1,2,0:T(8,128)(2,1)S(1)} all-to-all(bf16[16,224,3,128]{3,1,2,0:T(8,128)(2,1)S(1)} %copy.37), channel_id=1, replica_groups=mesh['req'=8,'cfg'=2,'seq'=16] {'seq'}, dimensions={0} | all-to-all | bytes 5505024 | tf_op jit(solution)/shard_map/all_to_all | solution.py:114
  52.4 0.5 slice.38
  53.6 0.8 broadcast_add_fusion
  54.3 0.0 all-gather.2.cloned.1.call-update
  55.0 0.2 reduce_window_sum.12
  55.2 0.2 select_reduce_fusion.1
  55.4 0.1 and_select_fusion.bias_ref
  55.5 1.9 %copy.47 = bf16[16,224,3,128]{3,2,1,0:T(4,128)(2,1)S(1)} copy(bf16[16,224,3,128]{3,1,2,0:T(8,128)(2,1)S(1)} %all_to_all.15) | data formatting | bytes 5505024 | tf_op jit(solution)/shard_map/reshape;reshape;reshape | solution.py:86
  57.4 0.5 copy.53
  57.9 42.4 %shard_map.98 = bf16[16,160,128]{2,1,0:T(8,128)(2,1)S(1)} custom-call(bf16[3584,384]{1,0:T(8,128)(2,1)S(1)} %bitcast.75, f32[1,3584]{1,0:T(1,128)S(1)} %and_select_fusion.bias_ref), custom_call_target="tpu_custom_call" | custom-call | tf_op jit(solution)/shard_map/pallas_call | solution.py:87
  100.3 0.8 copy-done.1
  101.1 4.4 %all-to-all-start.1 = ((bf16[16,160,128]{2,1,0:T(8,128)(2,1)}), bf16[16,160,128]{2,1,0:T(8,128)(2,1)}, u32[]{:S(2)}, u32[]{:S(2)}) async-start(bf16[16,160,128]{2,1,0:T(8,128)(2,1)} %copy-done.1), calls=%async_computation.1 | async-start | bytes 1310720 | tf_op jit(solution)/shard_map/all_to_all | solution.py:126
  105.6 15.1 %shard_map.99 = bf16[16,64,128]{2,1,0:T(8,128)(2,1)} custom-call(bf16[3584,384]{1,0:T(8,128)(2,1)S(1)} %bitcast.76, f32[1,3584]{1,0:T(1,128)S(1)} %and_select_fusion.bias_ref), custom_call_target="tpu_custom_call" | custom-call | tf_op jit(solution)/shard_map/pallas_call | solution.py:87
  120.6 1.6 all-to-all-done.1
  122.2 6.2 %all-to-all-start.2 = ((bf16[16,64,128]{2,1,0:T(8,128)(2,1)}), bf16[16,64,128]{2,1,0:T(8,128)(2,1)S(1)}, u32[]{:S(2)}, u32[]{:S(2)}) async-start(bf16[16,64,128]{2,1,0:T(8,128)(2,1)} %shard_map.99), calls=%async_computation.2 | async-start | bytes 524288 | tf_op jit(solution)/shard_map/all_to_all | solution.py:126
  128.4 1.1 constant_dynamic-update-slice_fusion.1
  129.5 6.2 %all-to-all-done.2 = bf16[16,64,128]{2,1,0:T(8,128)(2,1)S(1)} async-done(((bf16[16,64,128]{2,1,0:T(8,128)(2,1)}), bf16[16,64,128]{2,1,0:T(8,128)(2,1)S(1)}, u32[]{:S(2)}, u32[]{:S(2)}) %all-to-all-start.2) | async-done | bytes 262176 | tf_op jit(solution)/shard_map/all_to_all | solution.py:126
  135.8 4.2 %collective-permute-start = (bf16[16,224,128]{2,1,0:T(8,128)(2,1)S(1)}, bf16[16,224,128]{2,1,0:T(8,128)(2,1)S(1)}, u32[]{:S(2)}, u32[]{:S(2)}) collective-permute-start(bf16[16,224,128]{2,1,0:T(8,128)(2,1)S(1)} %constant_dynamic-update-slice_fusion), channel_id=1, source_target_pairs={{0,16},{16,0},{1,17},{17,1},{2,18},{18,2},{3,19},{19,3},{4,20},{20... | collective-permute-start | bytes 2752520 | tf_op jit(solution)/shard_map/ppermute | solution.py:23
  140.1 2.0 %collective-permute-done = bf16[16,224,128]{2,1,0:T(8,128)(2,1)S(1)} collective-permute-done((bf16[16,224,128]{2,1,0:T(8,128)(2,1)S(1)}, bf16[16,224,128]{2,1,0:T(8,128)(2,1)S(1)}, u32[]{:S(2)}, u32[]{:S(2)}) %collective-permute-start) | collective-permute-done | bytes 917536 | tf_op jit(solution)/shard_map/ppermute | solution.py:23
  142.1 1.1 select_bitcast_fusion.1
  143.2 5.6 %fusion.22 = (f32[2,224]{1,0:T(2,128)S(1)}, f32[2,224]{1,0:T(2,128)S(1)}, f32[2,224,1536]{2,1,0:T(8,128)S(1)}) fusion(bf16[16,128,1536,1]{2,1,0,3:T(8,128)(2,1)} %bitcast.87, bf16[1,16,224,128]{3,2,1,0:T(8,128)(2,1)} %get-tuple-element.11, bf16[1,16,224,128]{3,2,1,0:T(8,128)(2,1)S(1)} %get-tuple-element.10), kind=kOutput, calls=%fused_computation.63 | convolution fusion | flops 2821553152 | bytes 10882560 | tf_op jit(solution)/shard_map/agsj,gjc->asc/dot_general | solution.py:136
  148.8 0.5 collective-permute-start.1
  149.2 0.1 select_reduce_fusion.2
  149.4 0.7 collective-permute-done.1
  150.1 0.8 fusion.3
  150.9 0.4 collective-permute-start.2
  152.0 0.6 select_reduce_fusion.5
  153.4 0.6 select_reduce_fusion.4
  154.8 0.6 add_select_fusion
  (27 shorter events, 0.3 us)
Async XLA Ops:
  7.2 132.9 %copy-start = (bf16[3072,64]{0,1:T(8,128)(2,1)S(1)}, bf16[3072,64]{0,1:T(8,128)(2,1)}, u32[]{:S(2)}) copy-start(bf16[3072,64]{0,1:T(8,128)(2,1)} %param.13) | copy-start | bytes 1179652
  7.2 136.0 %all-gather.2.cloned.1.call-start = ((), (), s32[]{:S(2)}) async-start(), calls=%async_computation.3 | async-start | bytes 6684672 | tf_op jit(solution)/shard_map/all_gather | solution.py:130
  10.3 43.2 %copy-start.2 = (bf16[128,1536]{1,0:T(8,128)(2,1)S(1)}, bf16[128,1536]{1,0:T(8,128)(2,1)}, u32[]{:S(2)}) copy-start(bf16[128,1536]{1,0:T(8,128)(2,1)} %param.11) | copy-start | bytes 1179652
  10.4 44.7 %copy-start.5 = (s32[1,16]{1,0:T(1,128)S(1)}, s32[1,16]{1,0:T(1,128)}, u32[]{:S(2)}) copy-start(s32[1,16]{1,0:T(1,128)} %param.9) | copy-start | bytes 196
  100.2 0.9 copy-start.1
  101.1 21.1 %all-to-all-start.1 = ((bf16[16,160,128]{2,1,0:T(8,128)(2,1)}), bf16[16,160,128]{2,1,0:T(8,128)(2,1)}, u32[]{:S(2)}, u32[]{:S(2)}) async-start(bf16[16,160,128]{2,1,0:T(8,128)(2,1)} %copy-done.1), calls=%async_computation.1 | async-start | bytes 1310720 | tf_op jit(solution)/shard_map/all_to_all | solution.py:126
  105.5 34.5 %copy-start.4 = (f32[1,2,3072]{2,1,0:T(2,128)S(1)}, f32[1,2,3072]{2,1,0:T(2,128)}, u32[]{:S(2)}) copy-start(f32[1,2,3072]{2,1,0:T(2,128)} %param.12) | copy-start | bytes 73732
  122.2 13.5 %all-to-all-start.2 = ((bf16[16,64,128]{2,1,0:T(8,128)(2,1)}), bf16[16,64,128]{2,1,0:T(8,128)(2,1)S(1)}, u32[]{:S(2)}, u32[]{:S(2)}) async-start(bf16[16,64,128]{2,1,0:T(8,128)(2,1)} %shard_map.99), calls=%async_computation.2 | async-start | bytes 524288 | tf_op jit(solution)/shard_map/all_to_all | solution.py:126
  135.8 6.3 %collective-permute-start = (bf16[16,224,128]{2,1,0:T(8,128)(2,1)S(1)}, bf16[16,224,128]{2,1,0:T(8,128)(2,1)S(1)}, u32[]{:S(2)}, u32[]{:S(2)}) collective-permute-start(bf16[16,224,128]{2,1,0:T(8,128)(2,1)S(1)} %constant_dynamic-update-slice_fusion), channel_id=1, source_target_pairs={{0,16},{16,0},{1,17},{17,1},{2,18},{18,2},{3,19},{19,3},{4,20},{20... | collective-permute-start | bytes 2752520 | tf_op jit(solution)/shard_map/ppermute | solution.py:23
  148.8 1.3 collective-permute-start.1
  150.1 4.7 %copy-start.3 = (f32[1,224,32]{1,2,0:T(8,128)S(1)}, f32[1,224,32]{1,2,0:T(8,128)}, u32[]{:S(2)}) copy-start(f32[1,224,32]{1,2,0:T(8,128)} %param.14) | copy-start | bytes 86020
  150.9 3.9 %collective-permute-start.2 = (f32[2,224,32]{1,2,0:T(8,128)S(1)}, f32[2,224,32]{1,2,0:T(8,128)S(1)}, u32[]{:S(2)}, u32[]{:S(2)}) collective-permute-start(f32[2,224,32]{1,2,0:T(8,128)S(1)} %select_bitcast_fusion.2), channel_id=1, source_target_pairs={{0,16},{16,0},{1,17},{17,1},{2,18},{18,2},{3,19},{19,3},{4,20},{20... | collective-permute-start | bytes 172040 | tf_op jit(solution)/shard_map/ppermute | solution.py:23
Sparse Core Ops, SparseCore 0:
  54.5 74.0 all-gather.1

commit v10 on v6

--- a/solution.py
+++ b/solution.py
@@ -49,12 +49,11 @@
     return (alpha_now, alpha_prev)
 
 
-def attention_kernel(x_ref, bias_ref, o_ref):
-    block = o_ref.shape[0]
-    start = pl.multiple_of(pl.program_id(0) * block, block)
-    query = x_ref[pl.ds(start, block), 0:128]
-    keyset = x_ref[:, 128:256]
-    values = x_ref[:, 256:384]
+def attention_kernel(q_ref, k_ref, v_ref, bias_ref, o_ref):
+    query = q_ref[0, 0]
+    slot_count = k_ref.shape[0] * k_ref.shape[2]
+    keyset = k_ref[...].reshape(slot_count, k_ref.shape[3])
+    values = v_ref[...].reshape(slot_count, v_ref.shape[3])
     bias = bias_ref[...]
     lane = lax.broadcasted_iota(jnp.int32, query.shape, 1)
     results = []
@@ -73,19 +72,22 @@
     o_ref[...] = jnp.where(lane < HEAD, results[0], results[1]).astype(o_ref.dtype)
 
 
-def attention(grouped, bias, block_rows=256):
-    slot_count, width = grouped.shape
+def attention(blocks, bias):
+    piece_count, unused, capacity, width = blocks.shape
+    whole = (piece_count, 1, capacity, width)
     return pl.pallas_call(
         attention_kernel,
-        grid=(slot_count // block_rows,),
+        grid=(piece_count,),
         in_specs=[
-            pl.BlockSpec((slot_count, width), lambda i: (0, 0)),
-            pl.BlockSpec((1, slot_count), lambda i: (0, 0)),
+            pl.BlockSpec((1, 1, capacity, width), lambda i: (i, 0, 0, 0)),
+            pl.BlockSpec(whole, lambda i: (0, 1, 0, 0)),
+            pl.BlockSpec(whole, lambda i: (0, 2, 0, 0)),
+            pl.BlockSpec((1, piece_count * capacity), lambda i: (0, 0)),
         ],
-        out_specs=pl.BlockSpec((block_rows, width // 3), lambda i: (i, 0)),
-        out_shape=jax.ShapeDtypeStruct((slot_count, width // 3), jnp.bfloat16),
+        out_specs=pl.BlockSpec((capacity, width), lambda i: (i, 0)),
+        out_shape=jax.ShapeDtypeStruct((piece_count * capacity, width), jnp.bfloat16),
         compiler_params=pltpu.CompilerParams(vmem_limit_bytes=48 * 1024 * 1024),
-    )(grouped, bias)
+    )(blocks, blocks, blocks, bias)
 
 
 def modulate(hidden, row_mean, spread, shift_part, gain_part):
@@ -101,15 +103,14 @@
     group_width = attn_width // seq_count
     slot_count = capacity * seq_count
     outgoing = projected[0, 0].reshape(capacity, 3, seq_count, group_width)
-    outgoing = outgoing.transpose(2, 0, 1, 3)
+    outgoing = outgoing.transpose(2, 1, 0, 3)
     arrived = lax.all_to_all(outgoing, "seq", split_axis=0, concat_axis=0, tiled=True)
-    grouped = arrived.reshape(slot_count, 3 * group_width)
     out_weight = out_weight + arrived[0, 0, 0, 0] * jnp.zeros((), out_weight.dtype)
     key_slots, unused_video = slot_masks(
         lengths, text_len, jnp.arange(slot_count, dtype=jnp.int32), capacity
     )
     bias = jnp.where(key_slots, 0.0, -jnp.inf).astype(jnp.float32)
-    attended = attention(grouped, bias)
+    attended = attention(arrived, bias)
     returned = lax.all_to_all(
         attended.reshape(seq_count, capacity, group_width),
         "seq",

time: 157 us -> 157 us (level)
  starting transfers between devices: 6.82 us -> 8.48 us
    reshape x1 -> x0, local copies, waits for them, and re-layouts: 1.89 us -> none  [body(): grouped = arrived.reshape(slot_count, 3 * group_width)]
    ppermute x3, starting transfers between devices: 3.15 us -> 4.81 us  [partner_2(): lax.ppermute(array, axis, [(i, i ^ 1 << bit) for i in range(lax.axis_size...]
    unnamed x12 -> x13, local copies, waits for them, and re-layouts: 2.9 us -> 3.35 us
  transfers between devices with their start and end apart: 5 -> 5, of which waited for: 3 -> 3; matrix products, arithmetic and copies ran while one was open for 3% -> 2% of each run, Pallas kernels for 34% -> 33%
where the time goes in v10:
time: 157 us
  Pallas kernels  51.6 us (33%)
  blocking collectives  42 us (27%)
  waiting for transfers between devices  21.3 us (14%)
  between operations  17.8 us (11%)
  starting transfers between devices  8.48 us (5%)
  matrix products  6.37 us (4%)
  local copies, waits for them, and re-layouts  4.62 us (3%)
  other arithmetic  4.38 us (3%)
    pallas_call x1, Pallas kernels, attention(): pl.pallas_call(attention_kernel, grid=(piece_count,), in_specs=[pl.BlockS...  51.6 us
    all_to_all x1, blocking collectives, body(): lax.all_to_all(outgoing, 'seq', split_axis=0, concat_axis=0, tiled=True)  42 us
    all_to_all x1, waiting for transfers between devices, body(): lax.all_to_all(attended.reshape(seq_count, capacity, group_width), 'seq',...  18.5 us
    dot_general x1, matrix products, body(): jnp.einsum('agsj,gjc->asc', both, weight_half.reshape(seq_count, group_wi...  5.61 us
    ppermute x3, starting transfers between devices, partner_2(): lax.ppermute(array, axis, [(i, i ^ 1 << bit) for i in range(lax.axis_size...  4.81 us
    all_to_all x1, starting transfers between devices, body(): lax.all_to_all(attended.reshape(seq_count, capacity, group_width), 'seq',...  3.63 us
    unnamed x13, local copies, waits for them, and re-layouts  3.35 us
  transfers between devices with their start and end apart: 5, of which 3 were waited for; matrix products, arithmetic and copies ran while one was open for 2% of the time, Pallas kernels for 33%

profile of v10, /device:TPU:1, one launch (start us, length us, event | category | flops | bytes accessed | tf_op | source)
XLA Modules:
  0.0 156.5 jit_solution(11835431907243129285)
XLA Ops:
  7.2 0.0 copy-start
  7.2 0.0 all-gather.2.cloned.1.call-start
  7.2 2.4 %copy.27 = bf16[28,8,48,128]{3,2,1,0:T(8,128)(2,1)S(1)} copy(bf16[28,8,48,128]{3,1,2,0:T(8,128)(2,1)} %bitcast.75) | data formatting | bytes 5505024
  9.6 0.7 copy.29
  10.3 0.0 copy-start.2
  10.4 0.0 copy-start.5
  10.4 42.0 %all_to_all.10.q_ref.k_ref.v_ref = bf16[16,3,224,128]{3,2,1,0:T(8,128)(2,1)S(1)} all-to-all(bf16[16,3,224,128]{3,2,1,0:T(8,128)(2,1)S(1)} %bitcast.73), channel_id=1, replica_groups=mesh['req'=8,'cfg'=2,'seq'=16] {'seq'}, dimensions={0} | all-to-all | bytes 5505024 | tf_op jit(solution)/shard_map/all_to_all | solution.py:107
  52.4 0.5 slice.38
  53.6 0.8 broadcast_add_fusion
  54.3 0.0 all-gather.2.cloned.1.call-update
  55.0 0.2 reduce_window_sum.12
  55.2 0.2 select_reduce_fusion.1
  55.4 0.1 and_select_fusion.bias_ref
  55.5 0.0 copy-start.4
  55.5 51.6 %shard_map.98 = bf16[3584,128]{1,0:T(8,128)(2,1)S(1)} custom-call(bf16[16,3,224,128]{3,2,1,0:T(8,128)(2,1)S(1)} %all_to_all.10.q_ref.k_ref.v_ref, bf16[16,3,224,128]{3,2,1,0:T(8,128)(2,1)S(1)} %all_to_all.10.q_ref.k_ref.v_ref, bf16[16,3,224,128]{3,2,1,0:T(8,128)(2,1)S(1)} %all_to_all.10.q_ref.k_ref.v_ref, f32[1,3584]{1,0:T(1,128)S(1)} %and_select_fusion.bias_ref), custom_call_target="tpu_custom_call" | custom-call | tf_op jit(solution)/shard_map/pallas_call | solution.py:78
  107.1 0.9 copy-done.1
  108.1 3.6 %all-to-all-start.1 = ((bf16[16,224,128]{2,1,0:T(8,128)(2,1)}), bf16[16,224,128]{2,1,0:T(8,128)(2,1)S(1)}, u32[]{:S(2)}, u32[]{:S(2)}) async-start(bf16[16,224,128]{2,1,0:T(8,128)(2,1)} %bitcast.72), calls=%async_computation.1 | async-start | bytes 1835008 | tf_op jit(solution)/shard_map/all_to_all | solution.py:114
  111.7 18.5 %all-to-all-done.1 = bf16[16,224,128]{2,1,0:T(8,128)(2,1)S(1)} async-done(((bf16[16,224,128]{2,1,0:T(8,128)(2,1)}), bf16[16,224,128]{2,1,0:T(8,128)(2,1)S(1)}, u32[]{:S(2)}, u32[]{:S(2)}) %all-to-all-start.1) | async-done | bytes 917536 | tf_op jit(solution)/shard_map/all_to_all | solution.py:114
  130.3 3.9 %collective-permute-start = (bf16[16,224,128]{2,1,0:T(8,128)(2,1)S(1)}, bf16[16,224,128]{2,1,0:T(8,128)(2,1)S(1)}, u32[]{:S(2)}, u32[]{:S(2)}) collective-permute-start(bf16[16,224,128]{2,1,0:T(8,128)(2,1)S(1)} %all-to-all-done.1), channel_id=1, source_target_pairs={{0,16},{16,0},{1,17},{17,1},{2,18},{18,2},{3,19},{19,3},{4,20},{20... | collective-permute-start | bytes 2752520 | tf_op jit(solution)/shard_map/ppermute | solution.py:22
  134.3 2.0 %collective-permute-done = bf16[16,224,128]{2,1,0:T(8,128)(2,1)S(1)} collective-permute-done((bf16[16,224,128]{2,1,0:T(8,128)(2,1)S(1)}, bf16[16,224,128]{2,1,0:T(8,128)(2,1)S(1)}, u32[]{:S(2)}, u32[]{:S(2)}) %collective-permute-start) | collective-permute-done | bytes 917536 | tf_op jit(solution)/shard_map/ppermute | solution.py:22
  136.3 1.1 select_bitcast_fusion.1
  137.3 5.6 %fusion.22 = (f32[2,224]{1,0:T(2,128)S(1)}, f32[2,224]{1,0:T(2,128)S(1)}, f32[2,224,1536]{2,1,0:T(8,128)S(1)}) fusion(bf16[16,128,1536,1]{2,1,0,3:T(8,128)(2,1)} %bitcast.83, bf16[1,16,224,128]{3,2,1,0:T(8,128)(2,1)} %get-tuple-element.11, bf16[1,16,224,128]{3,2,1,0:T(8,128)(2,1)S(1)} %get-tuple-element.10), kind=kOutput, calls=%fused_computation.61 | convolution fusion | flops 2821553152 | bytes 10882560 | tf_op jit(solution)/shard_map/agsj,gjc->asc/dot_general | solution.py:128
  143.0 0.5 collective-permute-start.1
  143.4 0.1 select_reduce_fusion.2
  143.6 0.7 collective-permute-done.1
  144.3 0.0 copy-start.3
  144.3 0.8 fusion.3
  145.1 0.4 collective-permute-start.2
  146.2 0.6 select_reduce_fusion.5
  147.5 0.6 select_reduce_fusion.4
  149.0 0.0 collective-permute-done.2
  149.0 0.6 add_select_fusion
  (20 shorter events, 0.2 us)
Async XLA Ops:
  7.2 127.0 %copy-start = (bf16[3072,64]{0,1:T(8,128)(2,1)S(1)}, bf16[3072,64]{0,1:T(8,128)(2,1)}, u32[]{:S(2)}) copy-start(bf16[3072,64]{0,1:T(8,128)(2,1)} %param.13) | copy-start | bytes 1179652
  7.2 130.2 %all-gather.2.cloned.1.call-start = ((), (), s32[]{:S(2)}) async-start(), calls=%async_computation.2 | async-start | bytes 6684672 | tf_op jit(solution)/shard_map/all_gather | solution.py:122
  10.3 43.2 %copy-start.2 = (bf16[128,1536]{1,0:T(8,128)(2,1)S(1)}, bf16[128,1536]{1,0:T(8,128)(2,1)}, u32[]{:S(2)}) copy-start(bf16[128,1536]{1,0:T(8,128)(2,1)} %param.11) | copy-start | bytes 1179652
  10.4 44.7 %copy-start.5 = (s32[1,16]{1,0:T(1,128)S(1)}, s32[1,16]{1,0:T(1,128)}, u32[]{:S(2)}) copy-start(s32[1,16]{1,0:T(1,128)} %param.9) | copy-start | bytes 196
  55.5 78.7 %copy-start.4 = (f32[1,2,3072]{2,1,0:T(2,128)S(1)}, f32[1,2,3072]{2,1,0:T(2,128)}, u32[]{:S(2)}) copy-start(f32[1,2,3072]{2,1,0:T(2,128)} %param.12) | copy-start | bytes 73732
  107.1 0.9 copy-start.1
  108.1 22.2 %all-to-all-start.1 = ((bf16[16,224,128]{2,1,0:T(8,128)(2,1)}), bf16[16,224,128]{2,1,0:T(8,128)(2,1)S(1)}, u32[]{:S(2)}, u32[]{:S(2)}) async-start(bf16[16,224,128]{2,1,0:T(8,128)(2,1)} %bitcast.72), calls=%async_computation.1 | async-start | bytes 1835008 | tf_op jit(solution)/shard_map/all_to_all | solution.py:114
  130.3 6.0 %collective-permute-start = (bf16[16,224,128]{2,1,0:T(8,128)(2,1)S(1)}, bf16[16,224,128]{2,1,0:T(8,128)(2,1)S(1)}, u32[]{:S(2)}, u32[]{:S(2)}) collective-permute-start(bf16[16,224,128]{2,1,0:T(8,128)(2,1)S(1)} %all-to-all-done.1), channel_id=1, source_target_pairs={{0,16},{16,0},{1,17},{17,1},{2,18},{18,2},{3,19},{19,3},{4,20},{20... | collective-permute-start | bytes 2752520 | tf_op jit(solution)/shard_map/ppermute | solution.py:22
  143.0 1.3 collective-permute-start.1
  144.3 4.7 %copy-start.3 = (f32[1,224,32]{1,2,0:T(8,128)S(1)}, f32[1,224,32]{1,2,0:T(8,128)}, u32[]{:S(2)}) copy-start(f32[1,224,32]{1,2,0:T(8,128)} %param.14) | copy-start | bytes 86020
  145.1 3.9 %collective-permute-start.2 = (f32[2,224,32]{1,2,0:T(8,128)S(1)}, f32[2,224,32]{1,2,0:T(8,128)S(1)}, u32[]{:S(2)}, u32[]{:S(2)}) collective-permute-start(f32[2,224,32]{1,2,0:T(8,128)S(1)} %select_bitcast_fusion.2), channel_id=1, source_target_pairs={{0,16},{16,0},{1,17},{17,1},{2,18},{18,2},{3,19},{19,3},{4,20},{20... | collective-permute-start | bytes 172040 | tf_op jit(solution)/shard_map/ppermute | solution.py:22
Sparse Core Ops, SparseCore 0:
  54.5 73.7 all-gather.1

commit v11 on v10

--- a/solution.py
+++ b/solution.py
@@ -122,19 +122,17 @@
     weight_half = lax.all_gather(out_weight, "seq", axis=0, tiled=True)
     partner_rows = partner_2(returned, "cfg", 0)
     own_first = cfg_index == 0
-    both = jnp.stack(
-        [jnp.where(own_first, returned, partner_rows), jnp.where(own_first, partner_rows, returned)]
-    )
-    hidden = jnp.einsum(
-        "agsj,gjc->asc",
-        both,
-        weight_half.reshape(seq_count, group_width, out_weight.shape[1]),
-        preferred_element_type=jnp.float32,
+    weight_rows = weight_half.reshape(seq_count, group_width, out_weight.shape[1])
+    hidden = jnp.stack(
+        [
+            jnp.einsum("gsj,gjc->sc", rows, weight_rows, preferred_element_type=jnp.float32)
+            for rows in (returned, partner_rows)
+        ]
     )
     half_width = out_weight.shape[1]
     column_start = cfg_index * half_width
     sums = jnp.stack([jnp.sum(hidden, axis=2), jnp.sum(hidden * hidden, axis=2)])
-    sums = sums + partner_2(sums, "cfg", 0)
+    sums = sums + partner_2(sums, "cfg", 0)[:, ::-1]
     row_mean = (sums[0] / D)[:, :, None]
     spread = (sums[1] / D)[:, :, None] - row_mean * row_mean
     shift_part = lax.dynamic_slice_in_dim(modulation[0, 0], column_start, half_width, 0)
@@ -146,9 +144,9 @@
     ).reshape(2, capacity, 2, OUT_CH // 2)
     own_half = jnp.where(own_first, velocity[:, :, 0], velocity[:, :, 1])
     other_half = jnp.where(own_first, velocity[:, :, 1], velocity[:, :, 0])
-    velocity = own_half + partner_2(other_half, "cfg", 0)
-    conditional = velocity[0][None]
-    unconditional = velocity[1][None]
+    velocity = own_half + partner_2(other_half, "cfg", 0)[::-1]
+    conditional = jnp.where(own_first, velocity[0], velocity[1])[None]
+    unconditional = jnp.where(own_first, velocity[1], velocity[0])[None]
     own_slots = lax.axis_index("seq") * capacity + jnp.arange(capacity, dtype=jnp.int32)
     unused_keys, video_slots = slot_masks(lengths, text_len, own_slots, capacity)
     video_mask = video_slots[:, :, None]

time: 157 us -> 155 us (0.987)
  blocking collectives: 42 us -> 66.7 us
  waiting for transfers between devices: 21.3 us -> 1.05 us
  starting transfers between devices: 8.48 us -> 2.11 us
    all_to_all x0 -> x1, blocking collectives: none -> 24.7 us  [body(): lax.all_to_all(attended.reshape(seq_count, capacity, group_width), 'seq',...]
    all_to_all x1 -> x0, waiting for transfers between devices: 18.5 us -> none  [body(): lax.all_to_all(attended.reshape(seq_count, capacity, group_width), 'seq',...]
    all_to_all x1 -> x0, starting transfers between devices: 3.63 us -> none  [body(): lax.all_to_all(attended.reshape(seq_count, capacity, group_width), 'seq',...]
    ppermute x3, starting transfers between devices: 4.81 us -> 2.07 us  [partner_2(): lax.ppermute(array, axis, [(i, i ^ 1 << bit) for i in range(lax.axis_size...]
    ppermute x3, waiting for transfers between devices: 2.69 us -> 1.02 us  [partner_2(): lax.ppermute(array, axis, [(i, i ^ 1 << bit) for i in range(lax.axis_size...]
    dot_general x1 -> x2, matrix products: 5.61 us -> 6.64 us  [body(): jnp.einsum('gsj,gjc->sc', rows, weight_rows, preferred_element_type=jnp.f...]
  transfers between devices with their start and end apart: 5 -> 4, of which waited for: 3 -> 1; matrix products, arithmetic and copies ran while one was open for 2% -> 4% of each run, Pallas kernels for 33% -> 33%
where the time goes in v11:
time: 155 us
  blocking collectives  66.7 us (43%)
  Pallas kernels  51.7 us (33%)
  between operations  17.8 us (11%)
  matrix products  7.35 us (5%)
  local copies, waits for them, and re-layouts  4.47 us (3%)
  other arithmetic  3.77 us (2%)
  starting transfers between devices  2.11 us (1%)
    pallas_call x1, Pallas kernels, attention(): pl.pallas_call(attention_kernel, grid=(piece_count,), in_specs=[pl.BlockS...  51.7 us
    all_to_all x1, blocking collectives, body(): lax.all_to_all(outgoing, 'seq', split_axis=0, concat_axis=0, tiled=True)  42 us
    all_to_all x1, blocking collectives, body(): lax.all_to_all(attended.reshape(seq_count, capacity, group_width), 'seq',...  24.7 us
    dot_general x2, matrix products, body(): jnp.einsum('gsj,gjc->sc', rows, weight_rows, preferred_element_type=jnp.f...  6.64 us
    unnamed x13, local copies, waits for them, and re-layouts  3.15 us
  transfers between devices with their start and end apart: 4, of which 1 were waited for; matrix products, arithmetic and copies ran while one was open for 4% of the time, Pallas kernels for 33%

profile of v11, /device:TPU:1, one launch (start us, length us, event | category | flops | bytes accessed | tf_op | source)
XLA Modules:
  0.0 155.0 jit_solution(7377082009180691873)
XLA Ops:
  7.2 0.0 copy-start
  7.2 0.0 all-gather.2.cloned.1.call-start
  7.2 2.4 %copy.26 = bf16[28,8,48,128]{3,2,1,0:T(8,128)(2,1)S(1)} copy(bf16[28,8,48,128]{3,1,2,0:T(8,128)(2,1)} %bitcast.75) | data formatting | bytes 5505024
  9.6 0.7 copy.28
  10.3 0.0 copy-start.1
  10.4 0.0 copy-start.4
  10.4 42.0 %all_to_all.10.q_ref.k_ref.v_ref = bf16[16,3,224,128]{3,2,1,0:T(8,128)(2,1)S(1)} all-to-all(bf16[16,3,224,128]{3,2,1,0:T(8,128)(2,1)S(1)} %bitcast.73), channel_id=1, replica_groups=mesh['req'=8,'cfg'=2,'seq'=16] {'seq'}, dimensions={0} | all-to-all | bytes 5505024 | tf_op jit(solution)/shard_map/all_to_all | solution.py:107
  52.4 0.5 slice.40
  53.6 0.8 broadcast_add_fusion
  54.3 0.0 all-gather.2.cloned.1.call-update
  55.0 0.2 reduce_window_sum.12
  55.2 0.2 select_reduce_fusion.1
  55.4 0.1 and_select_fusion.bias_ref
  55.5 0.0 copy-start.3
  55.5 51.7 %shard_map.98 = bf16[3584,128]{1,0:T(8,128)(2,1)S(1)} custom-call(bf16[16,3,224,128]{3,2,1,0:T(8,128)(2,1)S(1)} %all_to_all.10.q_ref.k_ref.v_ref, bf16[16,3,224,128]{3,2,1,0:T(8,128)(2,1)S(1)} %all_to_all.10.q_ref.k_ref.v_ref, bf16[16,3,224,128]{3,2,1,0:T(8,128)(2,1)S(1)} %all_to_all.10.q_ref.k_ref.v_ref, f32[1,3584]{1,0:T(1,128)S(1)} %and_select_fusion.bias_ref), custom_call_target="tpu_custom_call" | custom-call | tf_op jit(solution)/shard_map/pallas_call | solution.py:78
  107.2 24.7 %all_to_all.11 = bf16[16,224,128]{2,1,0:T(8,128)(2,1)S(1)} all-to-all(bf16[16,224,128]{2,1,0:T(8,128)(2,1)S(1)} %bitcast.72), channel_id=1, replica_groups=mesh['req'=8,'cfg'=2,'seq'=16] {'seq'}, dimensions={0} | all-to-all | bytes 1835008 | tf_op jit(solution)/shard_map/all_to_all | solution.py:114
  131.9 1.7 %collective-permute-start = (bf16[16,224,128]{2,1,0:T(8,128)(2,1)S(1)}, bf16[16,224,128]{2,1,0:T(8,128)(2,1)}, u32[]{:S(2)}, u32[]{:S(2)}) collective-permute-start(bf16[16,224,128]{2,1,0:T(8,128)(2,1)S(1)} %all_to_all.11), channel_id=1, source_target_pairs={{0,16},{16,0},{1,17},{17,1},{2,18},{18,2},{3,19},{19,3},{4,20},{20... | collective-permute-start | bytes 2752520 | tf_op jit(solution)/shard_map/ppermute | solution.py:22
  133.8 0.0 all-gather.2.cloned.1.call-done
  133.8 3.9 %convolution_bitcast_fusion.1 = f32[1,224,1536]{2,1,0:T(8,128)S(1)} fusion(bf16[16,224,128]{2,1,0:T(8,128)(2,1)S(1)} %all_to_all.11, bf16[16,128,1536]{2,1,0:T(8,128)(2,1)} %bitcast.83), kind=kOutput, calls=%fused_computation.5 | convolution fusion | flops 1409286144 | bytes 8585216 | tf_op jit(solution)/shard_map/gsj,gjc->sc/dot_general | solution.py:128
  137.7 0.7 copy-done.5
  138.4 2.8 %convolution_bitcast_fusion = f32[1,224,1536]{2,1,0:T(8,128)S(1)} fusion(bf16[16,224,128]{2,1,0:T(8,128)(2,1)} %collective-permute-done, bf16[16,128,1536]{2,1,0:T(8,128)(2,1)S(1)} %bitcast.84), kind=kOutput, calls=%fused_computation.4 | convolution fusion | flops 1409286144 | bytes 8585216 | tf_op jit(solution)/shard_map/gsj,gjc->sc/dot_general | solution.py:128
  141.2 0.4 fusion
  141.6 0.1 collective-permute-start.1
  141.7 0.1 select_reduce_fusion.2
  141.9 1.0 collective-permute-done.1
  142.9 0.1 rev.6
  143.0 0.0 copy-start.2
  143.0 0.7 fusion.1
  143.7 0.3 collective-permute-start.2
  144.7 0.6 select_reduce_fusion.5
  146.0 0.6 select_reduce_fusion.4
  147.5 0.6 add_select_fusion
  (21 shorter events, 0.2 us)
Async XLA Ops:
  7.2 126.5 %copy-start = (bf16[3072,64]{0,1:T(8,128)(2,1)S(1)}, bf16[3072,64]{0,1:T(8,128)(2,1)}, u32[]{:S(2)}) copy-start(bf16[3072,64]{0,1:T(8,128)(2,1)} %param.13) | copy-start | bytes 1179652
  7.2 126.6 %all-gather.2.cloned.1.call-start = ((), (), s32[]{:S(2)}) async-start(), calls=%async_computation.2 | async-start | bytes 6684672 | tf_op jit(solution)/shard_map/all_gather | solution.py:122
  10.3 43.2 %copy-start.1 = (bf16[128,1536]{1,0:T(8,128)(2,1)S(1)}, bf16[128,1536]{1,0:T(8,128)(2,1)}, u32[]{:S(2)}) copy-start(bf16[128,1536]{1,0:T(8,128)(2,1)} %param.11) | copy-start | bytes 1179652
  10.4 44.7 %copy-start.4 = (s32[1,16]{1,0:T(1,128)S(1)}, s32[1,16]{1,0:T(1,128)}, u32[]{:S(2)}) copy-start(s32[1,16]{1,0:T(1,128)} %param.9) | copy-start | bytes 196
  55.5 78.2 %copy-start.3 = (f32[1,2,3072]{2,1,0:T(2,128)S(1)}, f32[1,2,3072]{2,1,0:T(2,128)}, u32[]{:S(2)}) copy-start(f32[1,2,3072]{2,1,0:T(2,128)} %param.12) | copy-start | bytes 73732
  131.9 5.8 %collective-permute-start = (bf16[16,224,128]{2,1,0:T(8,128)(2,1)S(1)}, bf16[16,224,128]{2,1,0:T(8,128)(2,1)}, u32[]{:S(2)}, u32[]{:S(2)}) collective-permute-start(bf16[16,224,128]{2,1,0:T(8,128)(2,1)S(1)} %all_to_all.11), channel_id=1, source_target_pairs={{0,16},{16,0},{1,17},{17,1},{2,18},{18,2},{3,19},{19,3},{4,20},{20... | collective-permute-start | bytes 2752520 | tf_op jit(solution)/shard_map/ppermute | solution.py:22
  133.8 4.6 %copy-start.5 = (bf16[2048,1536]{1,0:T(8,128)(2,1)S(1)}, bf16[2048,1536]{1,0:T(8,128)(2,1)}, u32[]{:S(2)}) copy-start(bf16[2048,1536]{1,0:T(8,128)(2,1)} %all-gather.2.cloned.1.call-done) | copy-start | bytes 18874372
  141.6 1.3 collective-permute-start.1
  143.0 4.5 %copy-start.2 = (f32[1,224,32]{1,2,0:T(8,128)S(1)}, f32[1,224,32]{1,2,0:T(8,128)}, u32[]{:S(2)}) copy-start(f32[1,224,32]{1,2,0:T(8,128)} %param.14) | copy-start | bytes 86020
  143.7 3.7 %collective-permute-start.2 = (f32[2,224,32]{1,2,0:T(8,128)S(1)}, f32[2,224,32]{1,2,0:T(8,128)S(1)}, u32[]{:S(2)}, u32[]{:S(2)}) collective-permute-start(f32[2,224,32]{1,2,0:T(8,128)S(1)} %select_bitcast_fusion), channel_id=1, source_target_pairs={{0,16},{16,0},{1,17},{17,1},{2,18},{18,2},{3,19},{19,3},{4,20},{20... | collective-permute-start | bytes 172040 | tf_op jit(solution)/shard_map/ppermute | solution.py:22
Sparse Core Ops, SparseCore 0:
  54.5 75.2 all-gather.1

commit v12 on v11

--- a/solution.py
+++ b/solution.py
@@ -44,9 +44,9 @@
     log_keep = jnp.log1p(-root_beta * root_beta)
     current = timestep[0]
     earlier = jnp.maximum(current - step_gap, 0)
-    alpha_now = jnp.exp(jnp.sum(jnp.where(indices <= current, log_keep, 0.0)))
-    alpha_prev = jnp.exp(jnp.sum(jnp.where(indices <= earlier, log_keep, 0.0)))
-    return (alpha_now, alpha_prev)
+    limits = jnp.stack([current, earlier])[:, None]
+    alphas = jnp.exp(jnp.sum(jnp.where(indices[None, :] <= limits, log_keep[None, :], 0.0), axis=1))
+    return (alphas[0], alphas[1])
 
 
 def attention_kernel(q_ref, k_ref, v_ref, bias_ref, o_ref):

time: 155 us -> 156 us (level)
  blocking collectives: 66.7 us -> 42 us
  waiting for transfers between devices: 1.05 us -> 19.6 us
  starting transfers between devices: 2.11 us -> 7.33 us
    all_to_all x1 -> x0, blocking collectives: 24.7 us -> none  [body(): lax.all_to_all(attended.reshape(seq_count, capacity, group_width), 'seq',...]
    all_to_all x0 -> x1, waiting for transfers between devices: none -> 18.6 us  [body(): lax.all_to_all(attended.reshape(seq_count, capacity, group_width), 'seq',...]
    all_to_all x0 -> x1, starting transfers between devices: none -> 3.63 us  [body(): lax.all_to_all(attended.reshape(seq_count, capacity, group_width), 'seq',...]
    ppermute x3, starting transfers between devices: 2.07 us -> 3.66 us  [partner_2(): lax.ppermute(array, axis, [(i, i ^ 1 << bit) for i in range(lax.axis_size...]
    unnamed x13 -> x15, local copies, waits for them, and re-layouts: 3.15 us -> 4.05 us
  transfers between devices with their start and end apart: 4 -> 5, of which waited for: 1 -> 2; matrix products, arithmetic and copies ran while one was open for 4% -> 3% of each run, Pallas kernels for 33% -> 33%
where the time goes in v12:
time: 156 us
  Pallas kernels  51.5 us (33%)
  blocking collectives  42 us (27%)
  waiting for transfers between devices  19.6 us (13%)
  between operations  19 us (12%)
  matrix products  7.43 us (5%)
  starting transfers between devices  7.33 us (5%)
  local copies, waits for them, and re-layouts  5.96 us (4%)
  other arithmetic  2.83 us (2%)
    pallas_call x1, Pallas kernels, attention(): pl.pallas_call(attention_kernel, grid=(piece_count,), in_specs=[pl.BlockS...  51.5 us
    all_to_all x1, blocking collectives, body(): lax.all_to_all(outgoing, 'seq', split_axis=0, concat_axis=0, tiled=True)  42 us
    all_to_all x1, waiting for transfers between devices, body(): lax.all_to_all(attended.reshape(seq_count, capacity, group_width), 'seq',...  18.6 us
    dot_general x2, matrix products, body(): jnp.einsum('gsj,gjc->sc', rows, weight_rows, preferred_element_type=jnp.f...  6.67 us
    unnamed x15, local copies, waits for them, and re-layouts  4.05 us
    ppermute x3, starting transfers between devices, partner_2(): lax.ppermute(array, axis, [(i, i ^ 1 << bit) for i in range(lax.axis_size...  3.66 us
    all_to_all x1, starting transfers between devices, body(): lax.all_to_all(attended.reshape(seq_count, capacity, group_width), 'seq',...  3.63 us
  transfers between devices with their start and end apart: 5, of which 2 were waited for; matrix products, arithmetic and copies ran while one was open for 3% of the time, Pallas kernels for 33%

profile of v12, /device:TPU:1, one launch (start us, length us, event | category | flops | bytes accessed | tf_op | source)
XLA Modules:
  0.0 155.7 jit_solution(5677758139690251273)
XLA Ops:
  7.2 0.0 copy-start
  7.2 0.0 all-gather.2.cloned.1.call-start
  7.2 2.4 %copy.26 = bf16[28,8,48,128]{3,2,1,0:T(8,128)(2,1)S(1)} copy(bf16[28,8,48,128]{3,1,2,0:T(8,128)(2,1)} %bitcast.76) | data formatting | bytes 5505024
  9.6 0.7 copy.28
  10.4 42.0 %all_to_all.10.q_ref.k_ref.v_ref = bf16[16,3,224,128]{3,2,1,0:T(8,128)(2,1)S(1)} all-to-all(bf16[16,3,224,128]{3,2,1,0:T(8,128)(2,1)S(1)} %bitcast.74), channel_id=1, replica_groups=mesh['req'=8,'cfg'=2,'seq'=16] {'seq'}, dimensions={0} | all-to-all | bytes 5505024 | tf_op jit(solution)/shard_map/all_to_all | solution.py:107
  52.4 0.5 slice.48
  53.6 0.8 broadcast_add_fusion
  54.3 0.0 all-gather.2.cloned.1.call-update
  55.7 0.2 reduce_window_sum.12
  55.9 0.1 select_reduce_fusion.2
  56.0 0.1 select_reduce_fusion.1
  56.2 0.1 and_select_fusion.bias_ref
  56.3 51.5 %shard_map.98 = bf16[3584,128]{1,0:T(8,128)(2,1)S(1)} custom-call(bf16[16,3,224,128]{3,2,1,0:T(8,128)(2,1)S(1)} %all_to_all.10.q_ref.k_ref.v_ref, bf16[16,3,224,128]{3,2,1,0:T(8,128)(2,1)S(1)} %all_to_all.10.q_ref.k_ref.v_ref, bf16[16,3,224,128]{3,2,1,0:T(8,128)(2,1)S(1)} %all_to_all.10.q_ref.k_ref.v_ref, f32[1,3584]{1,0:T(1,128)S(1)} %and_select_fusion.bias_ref), custom_call_target="tpu_custom_call" | custom-call | tf_op jit(solution)/shard_map/pallas_call | solution.py:78
  107.8 0.9 copy-done.1
  108.8 3.6 %all-to-all-start.1 = ((bf16[16,224,128]{2,1,0:T(8,128)(2,1)}), bf16[16,224,128]{2,1,0:T(8,128)(2,1)S(1)}, u32[]{:S(2)}, u32[]{:S(2)}) async-start(bf16[16,224,128]{2,1,0:T(8,128)(2,1)} %bitcast.73), calls=%async_computation.1 | async-start | bytes 1835008 | tf_op jit(solution)/shard_map/all_to_all | solution.py:114
  112.5 18.6 %all-to-all-done.1 = bf16[16,224,128]{2,1,0:T(8,128)(2,1)S(1)} async-done(((bf16[16,224,128]{2,1,0:T(8,128)(2,1)}), bf16[16,224,128]{2,1,0:T(8,128)(2,1)S(1)}, u32[]{:S(2)}, u32[]{:S(2)}) %all-to-all-start.1) | async-done | bytes 917536 | tf_op jit(solution)/shard_map/all_to_all | solution.py:114
  131.1 3.3 %collective-permute-start = (bf16[16,224,128]{2,1,0:T(8,128)(2,1)S(1)}, bf16[16,224,128]{2,1,0:T(8,128)(2,1)}, u32[]{:S(2)}, u32[]{:S(2)}) collective-permute-start(bf16[16,224,128]{2,1,0:T(8,128)(2,1)S(1)} %all-to-all-done.1), channel_id=1, source_target_pairs={{0,16},{16,0},{1,17},{17,1},{2,18},{18,2},{3,19},{19,3},{4,20},{20... | collective-permute-start | bytes 2752520 | tf_op jit(solution)/shard_map/ppermute | solution.py:22
  134.4 0.1 pad_add_fusion
  134.5 0.0 all-gather.2.cloned.1.call-done
  134.5 3.9 %convolution_bitcast_fusion.1 = f32[1,224,1536]{2,1,0:T(8,128)S(1)} fusion(bf16[16,224,128]{2,1,0:T(8,128)(2,1)S(1)} %all-to-all-done.1, bf16[16,128,1536]{2,1,0:T(8,128)(2,1)} %bitcast.84), kind=kOutput, calls=%fused_computation.5 | convolution fusion | flops 1409286144 | bytes 8585216 | tf_op jit(solution)/shard_map/gsj,gjc->sc/dot_general | solution.py:128
  138.5 0.7 copy-done.6
  139.2 2.8 %convolution_bitcast_fusion = f32[1,224,1536]{2,1,0:T(8,128)S(1)} fusion(bf16[16,224,128]{2,1,0:T(8,128)(2,1)} %collective-permute-done, bf16[16,128,1536]{2,1,0:T(8,128)(2,1)S(1)} %bitcast.85), kind=kOutput, calls=%fused_computation.4 | convolution fusion | flops 1409286144 | bytes 8585216 | tf_op jit(solution)/shard_map/gsj,gjc->sc/dot_general | solution.py:128
  141.9 0.5 fusion
  142.4 0.1 collective-permute-start.1
  142.5 0.2 fusion.7
  142.8 0.9 collective-permute-done.1
  143.7 0.1 rev.6
  143.8 0.0 copy-start.3
  143.8 0.8 fusion.1
  144.6 0.3 collective-permute-start.2
  144.8 0.6 fusion.19
  148.2 0.6 add_select_fusion
  (27 shorter events, 0.3 us)
Async XLA Ops:
  7.2 127.3 %copy-start = (bf16[3072,64]{0,1:T(8,128)(2,1)S(1)}, bf16[3072,64]{0,1:T(8,128)(2,1)}, u32[]{:S(2)}) copy-start(bf16[3072,64]{0,1:T(8,128)(2,1)} %param.13) | copy-start | bytes 1179652
  7.2 127.3 %all-gather.2.cloned.1.call-start = ((), (), s32[]{:S(2)}) async-start(), calls=%async_computation.2 | async-start | bytes 6684672 | tf_op jit(solution)/shard_map/all_gather | solution.py:122
  10.3 43.2 %copy-start.2 = (bf16[128,1536]{1,0:T(8,128)(2,1)S(1)}, bf16[128,1536]{1,0:T(8,128)(2,1)}, u32[]{:S(2)}) copy-start(bf16[128,1536]{1,0:T(8,128)(2,1)} %param.11) | copy-start | bytes 1179652
  10.4 45.3 %copy-start.5 = (s32[1,16]{1,0:T(1,128)S(1)}, s32[1,16]{1,0:T(1,128)}, u32[]{:S(2)}) copy-start(s32[1,16]{1,0:T(1,128)} %param.9) | copy-start | bytes 196
  56.3 56.2 %copy-start.4 = (f32[1,2,3072]{2,1,0:T(2,128)S(1)}, f32[1,2,3072]{2,1,0:T(2,128)}, u32[]{:S(2)}) copy-start(f32[1,2,3072]{2,1,0:T(2,128)} %param.12) | copy-start | bytes 73732
  107.8 0.9 copy-start.1
  108.8 22.3 %all-to-all-start.1 = ((bf16[16,224,128]{2,1,0:T(8,128)(2,1)}), bf16[16,224,128]{2,1,0:T(8,128)(2,1)S(1)}, u32[]{:S(2)}, u32[]{:S(2)}) async-start(bf16[16,224,128]{2,1,0:T(8,128)(2,1)} %bitcast.73), calls=%async_computation.1 | async-start | bytes 1835008 | tf_op jit(solution)/shard_map/all_to_all | solution.py:114
  131.1 7.4 %collective-permute-start = (bf16[16,224,128]{2,1,0:T(8,128)(2,1)S(1)}, bf16[16,224,128]{2,1,0:T(8,128)(2,1)}, u32[]{:S(2)}, u32[]{:S(2)}) collective-permute-start(bf16[16,224,128]{2,1,0:T(8,128)(2,1)S(1)} %all-to-all-done.1), channel_id=1, source_target_pairs={{0,16},{16,0},{1,17},{17,1},{2,18},{18,2},{3,19},{19,3},{4,20},{20... | collective-permute-start | bytes 2752520 | tf_op jit(solution)/shard_map/ppermute | solution.py:22
  134.5 4.6 %copy-start.6 = (bf16[2048,1536]{1,0:T(8,128)(2,1)S(1)}, bf16[2048,1536]{1,0:T(8,128)(2,1)}, u32[]{:S(2)}) copy-start(bf16[2048,1536]{1,0:T(8,128)(2,1)} %all-gather.2.cloned.1.call-done) | copy-start | bytes 18874372
  142.4 1.3 collective-permute-start.1
  143.8 4.4 %copy-start.3 = (f32[1,224,32]{1,2,0:T(8,128)S(1)}, f32[1,224,32]{1,2,0:T(8,128)}, u32[]{:S(2)}) copy-start(f32[1,224,32]{1,2,0:T(8,128)} %param.14) | copy-start | bytes 86020
  144.6 3.6 %collective-permute-start.2 = (f32[2,224,32]{1,2,0:T(8,128)S(1)}, f32[2,224,32]{1,2,0:T(8,128)S(1)}, u32[]{:S(2)}, u32[]{:S(2)}) collective-permute-start(f32[2,224,32]{1,2,0:T(8,128)S(1)} %select_bitcast_fusion), channel_id=1, source_target_pairs={{0,16},{16,0},{1,17},{17,1},{2,18},{18,2},{3,19},{19,3},{4,20},{20... | collective-permute-start | bytes 172040 | tf_op jit(solution)/shard_map/ppermute | solution.py:22
Sparse Core Ops, SparseCore 0:
  54.5 73.2 all-gather.1
